TPU v7x, 768 devices: a whole 4x8x12 slice. The times are simulated.
768 devices in a mesh: sub: 192 (over y, z, core), col: 4 (over x).
Axes of the slice: x: 4, y: 8, z: 12, core: 2. Of those that a mesh axis runs over, the one named last changes fastest.
Arguments:
- right_sides: float32 [64, 196608], P(None, ('sub', 'col')), may hold values from -6 to 6
- operator: float32 [192, 1536, 1024], P('sub', None, 'col'), may hold values from -0.15625 to 0.15625
- local_inverse: float32 [192, 1536, 1024], P('sub', None, 'col'), may hold values from -0.15625 to 0.15625
- coarse_basis: float32 [192, 1536, 64], P('sub'), may hold values from -0.15625 to 0.15625
- coarse_inverse: float32 [12288, 12288], P('sub', 'col'), may hold values from -0.15625 to 0.15625
- send_index: int32 [192, 4, 4, 32], P('sub', 'col'), may hold values from 0 to 255
- halo_count: int32 [192, 4, 4], P('sub', 'col'), may hold values from 1 to 32, as said below
Outputs:
- solution: float32 [64, 196608], P(None, ('sub', 'col'))
- residual: float32 [64, 196608], P(None, ('sub', 'col'))
Inputs may be any that keep to these rules, and one draw needn't show every extreme that they name: `halo_count`: on every device of every draw at least one of its 4 counts equals 32.
All inputs are finite; a program needn't handle non-finite values.
Results may differ from a plain program's by a relative error of at most 0.000078.
Values sent between devices are 32-bit elements; how exact they have to be, the bound alone decides.
No kernel may reach another device: no remote copies, remote signals or barrier semaphores. Data moves between devices by JAX's collectives and lax.ppermute only.
A program may use at most 32 MiB of HBM per device.

v0:
```python
import jax
import jax.numpy as jnp
from jax import lax
from jax.sharding import PartitionSpec as P

HIGH = lax.Precision.HIGHEST


def passed_along(block, axis, distance):
    devices = range(lax.axis_size(axis))
    route = [(i - distance, i) for i in devices if i - distance in devices]
    return lax.ppermute(block, axis, route)


def body(
    right_sides, operator, local_inverse, coarse_basis, coarse_inverse, send_index, halo_count
):
    own_width = right_sides.shape[1]
    rhs_width = right_sides.shape[0]
    halo_slots = send_index.shape[3]
    stride = lax.axis_size("sub") // 4
    offsets = (1, -1, stride, -stride)
    send_rows = send_index[0, 0]
    counts = halo_count[0, 0]
    live_slots = (jnp.arange(halo_slots, dtype=jnp.int32)[None, :] < counts[:, None]).astype(
        jnp.float32
    )
    operator_rows = operator[0]
    inverse_rows = local_inverse[0]
    basis_rows = coarse_basis[0]
    mode_count = basis_rows.shape[1]
    block_len = basis_rows.shape[0] // lax.axis_size("col")
    column_index = lax.axis_index("col")
    quarter = coarse_inverse.shape[1] // lax.axis_size("sub")

    def extend_apply(field, matrices):
        pieces = [field]
        for number in range(len(offsets)):
            packed = jnp.take(field, send_rows[number], axis=1) * live_slots[number][None, :]
            pieces.append(passed_along(packed, "sub", offsets[number]))
        own_and_halo = jnp.concatenate(pieces, axis=1)
        segment = lax.all_gather(own_and_halo, "col", axis=1, tiled=True)
        return tuple([jnp.dot(segment, matrix, precision=HIGH) for matrix in matrices])

    def precondition(field):
        local_part, coeff_rows = extend_apply(field, (inverse_rows, basis_rows))
        mode_coeffs = coeff_rows.T
        segment = lax.all_gather(
            mode_coeffs.reshape(1, mode_count * rhs_width), "sub", axis=0, tiled=True
        )
        held = segment.shape[0]
        blocks = segment.reshape(held, mode_count, rhs_width)
        kept_rows = lax.dynamic_slice_in_dim(blocks, column_index * quarter, quarter, 1).reshape(
            held * quarter, rhs_width
        )
        partial_sum = jnp.dot(coarse_inverse, kept_rows, precision=HIGH)
        coarse_vals = lax.psum(partial_sum, "col")
        own_basis = lax.dynamic_slice_in_dim(basis_rows, column_index * block_len, own_width, 0)
        coarse_part = lax.dot_general(
            coarse_vals, own_basis, (((0,), (1,)), ((), ())), precision=HIGH
        )
        return local_part + coarse_part

    first_pass = precondition(right_sides)
    applied_parts = extend_apply(first_pass, (operator_rows,))
    residual = right_sides - applied_parts[0]
    solution = first_pass + precondition(residual)
    return (solution, residual)


def solution(mesh):
    placed = (
        P(None, ("sub", "col")),
        P("sub", None, "col"),
        P("sub", None, "col"),
        P("sub", None, None),
        P("sub", "col"),
        P("sub", "col", None, None),
        P("sub", "col", None),
    )
    return jax.shard_map(
        body,
        mesh=mesh,
        in_specs=placed,
        out_specs=(P(None, ("sub", "col")), P(None, ("sub", "col"))),
        check_vma=False,
    )
```

profile of v0, /device:TPU:1, one launch (start us, length us, event | category | flops | bytes accessed | tf_op | source)
XLA Modules:
  0.0 438.8 jit_solution(14193039663653351945)
XLA Ops:
  10.6 12.4 %collective-permute-start.1 = (f32[64,32]{1,0:T(8,128)S(1)}, f32[64,32]{1,0:T(8,128)S(1)}, u32[]{:S(2)}, u32[]{:S(2)}) collective-permute-start(f32[64,32]{1,0:T(8,128)S(1)} %bitcast_multiply_fusion.10), channel_id=1, source_target_pairs={{4,0},{8,4},{12,8},{16,12},{20,16},{24,20},{28,24},{32,28},{36,32}... | collective-permute-start | bytes 24584 | tf_op jit(solution)/shard_map/ppermute | solution.py:12
  23.7 1.9 collective-permute-start
  26.9 1.3 collective-permute-start.2
  28.9 1.3 collective-permute-start.3
  30.3 4.2 collective-permute-done.3
  34.6 9.6 %all_gather.15 = f32[64,1536]{1,0:T(8,128)S(1)} all-gather(f32[64,384]{1,0:T(8,128)S(1)} %concatenate.9), channel_id=1, replica_groups=mesh['sub'=192,'col'=4] {'col'}, dimensions={1}, use_global_device_ids=true | all-gather | bytes 491520 | tf_op jit(solution)/shard_map/all_gather | solution.py:42
  45.6 128.1 %all-gather.5.cloned.1.call-done = f32[192,1,4096]{2,1,0:T(1,128)} async-done(((f32[1,1,4096]{2,1,0:T(1,128)}), f32[192,1,4096]{2,1,0:T(1,128)}) %all-gather.5.cloned.1.call-update) | async-done | bytes 3145744 | tf_op jit(solution)/shard_map/all_gather | solution.py:48
  173.6 8.4 %copy.100 = f32[192,1,4096]{0,2,1:T(8,128)} copy(f32[192,1,4096]{2,1,0:T(1,128)} %all-gather.5.cloned.1.call-done) | data formatting | bytes 6291456 | tf_op jit(solution)/shard_map/all_gather | solution.py:48
  182.0 2.4 constant_dynamic-slice_fusion.1
  184.4 2.1 copy.101
  186.5 4.4 convolution_bitcast_fusion.3
  190.9 13.9 %psum.14 = f32[64,64]{0,1:T(8,128)S(1)} all-reduce(f32[64,64]{0,1:T(8,128)} %convolution_bitcast_fusion.3), channel_id=1, replica_groups=mesh['sub'=192,'col'=4] {'col'}, use_global_device_ids=true, to_apply=%region_0.0 | all-reduce | flops 4096 | bytes 32768 | tf_op jit(solution)/shard_map/psum | solution.py:57
  205.8 1.5 fusion.6
  207.4 1.1 copy.102
  213.5 6.4 %collective-permute-start.5 = (f32[64,32]{1,0:T(8,128)S(1)}, f32[64,32]{1,0:T(8,128)S(1)}, u32[]{:S(2)}, u32[]{:S(2)}) collective-permute-start(f32[64,32]{1,0:T(8,128)S(1)} %bitcast_multiply_fusion.6), channel_id=1, source_target_pairs={{4,0},{8,4},{12,8},{16,12},{20,16},{24,20},{28,24},{32,28},{36,32}... | collective-permute-start | bytes 24584 | tf_op jit(solution)/shard_map/ppermute | solution.py:12
  220.0 2.9 collective-permute-start.4
  222.9 2.8 collective-permute-start.6
  225.6 1.3 collective-permute-start.7
  227.0 5.2 %collective-permute-done.7 = f32[64,32]{1,0:T(8,128)S(1)} collective-permute-done((f32[64,32]{1,0:T(8,128)S(1)}, f32[64,32]{1,0:T(8,128)S(1)}, u32[]{:S(2)}, u32[]{:S(2)}) %collective-permute-start.7) | collective-permute-done | bytes 8224 | tf_op jit(solution)/shard_map/ppermute | solution.py:12
  232.2 9.8 %all_gather.17 = f32[64,1536]{1,0:T(8,128)S(1)} all-gather(f32[64,384]{1,0:T(8,128)S(1)} %concatenate.10), channel_id=1, replica_groups=mesh['sub'=192,'col'=4] {'col'}, dimensions={1}, use_global_device_ids=true | all-gather | bytes 491520 | tf_op jit(solution)/shard_map/all_gather | solution.py:42
  246.4 1.3 collective-permute-start.11
  247.7 6.3 %collective-permute-start.10 = (f32[64,32]{1,0:T(8,128)S(1)}, f32[64,32]{1,0:T(8,128)S(1)}, u32[]{:S(2)}, u32[]{:S(2)}) collective-permute-start(f32[64,32]{1,0:T(8,128)S(1)} %bitcast_multiply_fusion.1), channel_id=1, source_target_pairs={{0,192},{4,196},{8,200},{12,204},{16,208},{20,212},{24,216},{28,22... | collective-permute-start | bytes 24584 | tf_op jit(solution)/shard_map/ppermute | solution.py:12
  254.0 7.0 %collective-permute-start.9 = (f32[64,32]{1,0:T(8,128)S(1)}, f32[64,32]{1,0:T(8,128)S(1)}, u32[]{:S(2)}, u32[]{:S(2)}) collective-permute-start(f32[64,32]{1,0:T(8,128)S(1)} %bitcast_multiply_fusion.2), channel_id=1, source_target_pairs={{4,0},{8,4},{12,8},{16,12},{20,16},{24,20},{28,24},{32,28},{36,32}... | collective-permute-start | bytes 24584 | tf_op jit(solution)/shard_map/ppermute | solution.py:12
  261.0 2.6 collective-permute-start.8
  264.7 10.7 %all_gather.18 = f32[64,1536]{1,0:T(8,128)S(1)} all-gather(f32[64,384]{1,0:T(8,128)S(1)} %concatenate.11), channel_id=1, replica_groups=mesh['sub'=192,'col'=4] {'col'}, dimensions={1}, use_global_device_ids=true | all-gather | bytes 491520 | tf_op jit(solution)/shard_map/all_gather | solution.py:42
  276.6 120.8 %all-gather.7.cloned.1.call-done = f32[192,1,4096]{2,1,0:T(1,128)} async-done(((f32[1,1,4096]{2,1,0:T(1,128)}), f32[192,1,4096]{2,1,0:T(1,128)}) %all-gather.7.cloned.1.call-update) | async-done | bytes 3145744 | tf_op jit(solution)/shard_map/all_gather | solution.py:48
  397.4 8.4 %copy.119 = f32[192,1,4096]{0,2,1:T(8,128)} copy(f32[192,1,4096]{2,1,0:T(1,128)} %all-gather.7.cloned.1.call-done) | data formatting | bytes 6291456 | tf_op jit(solution)/shard_map/all_gather | solution.py:48
  405.8 2.4 constant_dynamic-slice_fusion
  408.2 2.1 copy.120
  410.3 4.4 convolution_bitcast_fusion.2
  414.7 13.9 %psum.15 = f32[64,64]{0,1:T(8,128)S(1)} all-reduce(f32[64,64]{0,1:T(8,128)} %convolution_bitcast_fusion.2), channel_id=1, replica_groups=mesh['sub'=192,'col'=4] {'col'}, use_global_device_ids=true, to_apply=%region_1.3 | all-reduce | flops 4096 | bytes 32768 | tf_op jit(solution)/shard_map/psum | solution.py:57
  429.6 2.4 fusion.12
  (113 shorter events, 21.3 us)
Async XLA Ops:
  7.2 198.6 %copy-start = (f32[1,1536,256]{2,1,0:T(8,128)S(1)}, f32[1,1536,256]{2,1,0:T(8,128)}, u32[]{:S(2)}) copy-start(f32[1,1536,256]{2,1,0:T(8,128)} %param.11) | copy-start | bytes 4718596
  7.2 27.3 %copy-start.5 = (f32[64,256]{1,0:T(8,128)S(1)}, f32[64,256]{1,0:T(8,128)}, u32[]{:S(2)}) copy-start(f32[64,256]{1,0:T(8,128)} %param.9) | copy-start | bytes 196612
  7.2 37.0 %copy-start.1 = (f32[1,1536,64]{1,2,0:T(8,128)S(1)}, f32[1,1536,64]{1,2,0:T(8,128)}, u32[]{:S(2)}) copy-start(f32[1,1536,64]{1,2,0:T(8,128)} %param.12) | copy-start | bytes 1179652
  7.2 166.4 %all-gather.5.cloned.1.call-start = ((), (), s32[]{:S(2)}) async-start(), calls=%async_computation | async-start | bytes 3162112 | tf_op jit(solution)/shard_map/all_gather | solution.py:48
  8.1 2.5 copy-start.12
  8.1 15.6 %copy-start.15 = (f32[32]{0:T(128)}, f32[32]{0:T(128)S(1)}, u32[]{:S(2)}) copy-start(f32[32]{0:T(128)S(1)} %get-tuple-element.14) | copy-start | bytes 388
  8.1 36.6 %copy-start.8 = (f32[32]{0:T(128)}, f32[32]{0:T(128)S(1)}, u32[]{:S(2)}) copy-start(f32[32]{0:T(128)S(1)} %get-tuple-element.11) | copy-start | bytes 388
  8.1 36.6 %copy-start.10 = (f32[32]{0:T(128)}, f32[32]{0:T(128)S(1)}, u32[]{:S(2)}) copy-start(f32[32]{0:T(128)S(1)} %get-tuple-element.12) | copy-start | bytes 388
  10.6 19.6 %collective-permute-start.1 = (f32[64,32]{1,0:T(8,128)S(1)}, f32[64,32]{1,0:T(8,128)S(1)}, u32[]{:S(2)}, u32[]{:S(2)}) collective-permute-start(f32[64,32]{1,0:T(8,128)S(1)} %bitcast_multiply_fusion.10), channel_id=1, source_target_pairs={{4,0},{8,4},{12,8},{16,12},{20,16},{24,20},{28,24},{32,28},{36,32}... | collective-permute-start | bytes 24584 | tf_op jit(solution)/shard_map/ppermute | solution.py:12
  23.7 6.5 %collective-permute-start = (f32[64,32]{1,0:T(8,128)S(1)}, f32[64,32]{1,0:T(8,128)S(1)}, u32[]{:S(2)}, u32[]{:S(2)}) collective-permute-start(f32[64,32]{1,0:T(8,128)S(1)} %bitcast_multiply_fusion.11), channel_id=1, source_target_pairs={{0,4},{4,8},{8,12},{12,16},{16,20},{20,24},{24,28},{28,32},{32,36}... | collective-permute-start | bytes 24584 | tf_op jit(solution)/shard_map/ppermute | solution.py:12
  26.9 3.3 collective-permute-start.2
  28.3 153.8 %copy-start.20 = (s32[1024]{0:T(1024)}, s32[1024]{0:T(1024)S(1)}, u32[]{:S(2)}) copy-start(s32[1024]{0:T(1024)S(1)} %pad_clamp_fusion) | copy-start | bytes 12292
  28.9 5.6 %collective-permute-start.3 = (f32[64,32]{1,0:T(8,128)S(1)}, f32[64,32]{1,0:T(8,128)S(1)}, u32[]{:S(2)}, u32[]{:S(2)}) collective-permute-start(f32[64,32]{1,0:T(8,128)S(1)} %bitcast_multiply_fusion.8), channel_id=1, source_target_pairs={{192,0},{196,4},{200,8},{204,12},{208,16},{212,20},{216,24},{220,2... | collective-permute-start | bytes 24584 | tf_op jit(solution)/shard_map/ppermute | solution.py:12
  45.5 351.9 %all-gather.7.cloned.1.call-start = ((), (), s32[]{:S(2)}) async-start(), calls=%async_computation.1 | async-start | bytes 3162112 | tf_op jit(solution)/shard_map/all_gather | solution.py:48
  207.4 6.2 %copy-start.13 = (f32[32]{0:T(128)S(1)}, f32[32]{0:T(128)}, u32[]{:S(2)}) copy-start(f32[32]{0:T(128)} %copy-done.12) | copy-start | bytes 388
  207.4 24.8 %copy-start.4 = (f32[64,256]{1,0:T(8,128)S(1)}, f32[64,256]{1,0:T(8,128)}, u32[]{:S(2)}) copy-start(f32[64,256]{1,0:T(8,128)} %fusion.6) | copy-start | bytes 196612
  207.4 34.7 %copy-start.3 = (f32[1,1536,256]{2,1,0:T(8,128)S(1)}, f32[1,1536,256]{2,1,0:T(8,128)}, u32[]{:S(2)}) copy-start(f32[1,1536,256]{2,1,0:T(8,128)} %param.10) | copy-start | bytes 4718596
  207.4 34.7 %copy-start.6 = (f32[64,256]{1,0:T(8,128)S(1)}, f32[64,256]{1,0:T(8,128)}, u32[]{:S(2)}) copy-start(f32[64,256]{1,0:T(8,128)} %param.9) | copy-start | bytes 196612
  213.5 13.4 %collective-permute-start.5 = (f32[64,32]{1,0:T(8,128)S(1)}, f32[64,32]{1,0:T(8,128)S(1)}, u32[]{:S(2)}, u32[]{:S(2)}) collective-permute-start(f32[64,32]{1,0:T(8,128)S(1)} %bitcast_multiply_fusion.6), channel_id=1, source_target_pairs={{4,0},{8,4},{12,8},{16,12},{20,16},{24,20},{28,24},{32,28},{36,32}... | collective-permute-start | bytes 24584 | tf_op jit(solution)/shard_map/ppermute | solution.py:12
  220.0 7.0 %collective-permute-start.4 = (f32[64,32]{1,0:T(8,128)S(1)}, f32[64,32]{1,0:T(8,128)S(1)}, u32[]{:S(2)}, u32[]{:S(2)}) collective-permute-start(f32[64,32]{1,0:T(8,128)S(1)} %bitcast_multiply_fusion.7), channel_id=1, source_target_pairs={{0,4},{4,8},{8,12},{12,16},{16,20},{20,24},{24,28},{28,32},{32,36}... | collective-permute-start | bytes 24584 | tf_op jit(solution)/shard_map/ppermute | solution.py:12
  222.9 4.1 collective-permute-start.6
  225.6 6.5 %collective-permute-start.7 = (f32[64,32]{1,0:T(8,128)S(1)}, f32[64,32]{1,0:T(8,128)S(1)}, u32[]{:S(2)}, u32[]{:S(2)}) collective-permute-start(f32[64,32]{1,0:T(8,128)S(1)} %bitcast_multiply_fusion.4), channel_id=1, source_target_pairs={{192,0},{196,4},{200,8},{204,12},{208,16},{212,20},{216,24},{220,2... | collective-permute-start | bytes 24584 | tf_op jit(solution)/shard_map/ppermute | solution.py:12
  242.1 4.1 copy-start.16
  242.1 4.2 copy-start.14
  242.1 4.3 copy-start.11
  242.1 4.3 copy-start.9
  243.0 21.6 %copy-start.7 = (f32[64,256]{1,0:T(8,128)}, f32[64,256]{1,0:T(8,128)S(1)}, u32[]{:S(2)}) copy-start(f32[64,256]{1,0:T(8,128)S(1)} %fusion.15) | copy-start | bytes 196612
  243.0 32.4 %copy-start.2 = (f32[1,1536,64]{1,2,0:T(8,128)S(1)}, f32[1,1536,64]{1,2,0:T(8,128)}, u32[]{:S(2)}) copy-start(f32[1,1536,64]{1,2,0:T(8,128)} %param.12) | copy-start | bytes 1179652
  246.4 17.2 %collective-permute-start.11 = (f32[64,32]{1,0:T(8,128)S(1)}, f32[64,32]{1,0:T(8,128)S(1)}, u32[]{:S(2)}, u32[]{:S(2)}) collective-permute-start(f32[64,32]{1,0:T(8,128)S(1)} %bitcast_multiply_fusion), channel_id=1, source_target_pairs={{192,0},{196,4},{200,8},{204,12},{208,16},{212,20},{216,24},{220,2... | collective-permute-start | bytes 24584 | tf_op jit(solution)/shard_map/ppermute | solution.py:12
  247.7 15.9 %collective-permute-start.10 = (f32[64,32]{1,0:T(8,128)S(1)}, f32[64,32]{1,0:T(8,128)S(1)}, u32[]{:S(2)}, u32[]{:S(2)}) collective-permute-start(f32[64,32]{1,0:T(8,128)S(1)} %bitcast_multiply_fusion.1), channel_id=1, source_target_pairs={{0,192},{4,196},{8,200},{12,204},{16,208},{20,212},{24,216},{28,22... | collective-permute-start | bytes 24584 | tf_op jit(solution)/shard_map/ppermute | solution.py:12
  254.0 9.6 %collective-permute-start.9 = (f32[64,32]{1,0:T(8,128)S(1)}, f32[64,32]{1,0:T(8,128)S(1)}, u32[]{:S(2)}, u32[]{:S(2)}) collective-permute-start(f32[64,32]{1,0:T(8,128)S(1)} %bitcast_multiply_fusion.2), channel_id=1, source_target_pairs={{4,0},{8,4},{12,8},{16,12},{20,16},{24,20},{28,24},{32,28},{36,32}... | collective-permute-start | bytes 24584 | tf_op jit(solution)/shard_map/ppermute | solution.py:12
  261.0 3.6 collective-permute-start.8
  (3 other events, 2.9 us)
Sparse Core Ops, SparseCore 0:
  45.6 127.9 all-gather.4
  276.8 120.6 all-gather.6
where the time goes:
time: 443 us; the launch traced here: 439 us
  waiting for transfers between devices  259 us (58%)
  blocking collectives  57.9 us (13%)
  starting transfers between devices  47.5 us (11%)
  local copies, waits for them, and re-layouts  39.3 us (9%)
  matrix products  16.6 us (4%)
  between operations  14.6 us (3%)
    all_gather x2, waiting for transfers between devices, precondition(): lax.all_gather(mode_coeffs.reshape(1, mode_count * rhs_width), 'sub', axi...  249 us
    ppermute x12, starting transfers between devices, passed_along(): return lax.ppermute(block, axis, route)  47.4 us
    all_gather x3, blocking collectives, extend_apply(): segment = lax.all_gather(own_and_halo, 'col', axis=1, tiled=True)  30.1 us
    psum x2, blocking collectives, precondition(): coarse_vals = lax.psum(partial_sum, 'col')  27.7 us
    all_gather x2, local copies, waits for them, and re-layouts, precondition(): lax.all_gather(mode_coeffs.reshape(1, mode_count * rhs_width), 'sub', axi...  16.8 us
    ppermute x12, waiting for transfers between devices, passed_along(): return lax.ppermute(block, axis, route)  10.4 us
    gather x24, local copies, waits for them, and re-layouts, extend_apply(): jnp.take(field, send_rows[number], axis=1) * live_slots[number][None, :]  8.96 us
    dynamic_slice x4, local copies, waits for them, and re-layouts, precondition(): lax.dynamic_slice_in_dim(blocks, column_index * quarter, quarter, 1)  8.9 us
  transfers between devices with their start and end apart: 14, of which 5 were waited for; matrix products, arithmetic and copies ran while one was open for 0% of the time, Pallas kernels for 0%

commit v1 on v0

v1 whole, which is shorter than its diff:
```python
import jax
import jax.numpy as jnp
from jax import lax
from jax.sharding import Mesh, PartitionSpec as P

HIGH = lax.Precision.HIGHEST
CORES = 2
ZLEN = 12
SUB = ("y", "z", "core")


def passed_along(block, distance, subs):
    route = [(i - distance, i) for i in range(subs) if 0 <= i - distance < subs]
    return lax.ppermute(block, SUB, route)


def body(
    right_sides, operator, local_inverse, coarse_basis, coarse_inverse, send_index, halo_count
):
    own_width = right_sides.shape[1]
    rhs_width = right_sides.shape[0]
    halo_slots = send_index.shape[3]
    n_col = lax.axis_size("col")
    subs = lax.axis_size("y") * ZLEN * CORES
    stride = subs // 4
    offsets = (1, -1, stride, -stride)
    send_rows = send_index[0, 0]
    counts = halo_count[0, 0]
    live_slots = (jnp.arange(halo_slots, dtype=jnp.int32)[None, :] < counts[:, None]).astype(
        jnp.float32
    )
    operator_rows = operator[0]
    inverse_rows = local_inverse[0]
    basis_rows = coarse_basis[0]
    mode_count = basis_rows.shape[1]
    block_len = basis_rows.shape[0] // n_col
    column_index = lax.axis_index("col")
    quarter = mode_count // n_col

    def extend_apply(field, matrices):
        pieces = [field]
        for number in range(len(offsets)):
            packed = jnp.take(field, send_rows[number], axis=1) * live_slots[number][None, :]
            pieces.append(passed_along(packed, offsets[number], subs))
        own_and_halo = jnp.concatenate(pieces, axis=1)
        segment = lax.all_gather(own_and_halo, "col", axis=1, tiled=True)
        return tuple([jnp.dot(segment, matrix, precision=HIGH) for matrix in matrices])

    def precondition(field):
        local_part, coeff_rows = extend_apply(field, (inverse_rows, basis_rows))
        mode_coeffs = coeff_rows.T
        mine = lax.dynamic_slice_in_dim(mode_coeffs, column_index * quarter, quarter, 0)
        row = lax.all_gather(mine[None], ("z", "core"), axis=0, tiled=True)
        kept_rows = lax.all_gather(row, "y", axis=0, tiled=True).reshape(
            subs * quarter, rhs_width
        )
        partial_sum = jnp.dot(coarse_inverse, kept_rows, precision=HIGH)
        every = lax.all_gather(partial_sum[None], "col", axis=0, tiled=True)
        coarse_vals = jnp.sum(every, axis=0)
        own_basis = lax.dynamic_slice_in_dim(basis_rows, column_index * block_len, own_width, 0)
        coarse_part = lax.dot_general(
            coarse_vals, own_basis, (((0,), (1,)), ((), ())), precision=HIGH
        )
        return local_part + coarse_part

    first_pass = precondition(right_sides)
    applied_parts = extend_apply(first_pass, (operator_rows,))
    residual = right_sides - applied_parts[0]
    solution = first_pass + precondition(residual)
    return (solution, residual)


def solution(mesh):
    subs, n_col = mesh.devices.shape
    fine = Mesh(
        mesh.devices.reshape(subs // (ZLEN * CORES), ZLEN, CORES, n_col), SUB + ("col",)
    )
    placed = (
        P(None, SUB + ("col",)),
        P(SUB, None, "col"),
        P(SUB, None, "col"),
        P(SUB, None, None),
        P(SUB, "col"),
        P(SUB, "col", None, None),
        P(SUB, "col", None),
    )
    return jax.shard_map(
        body,
        mesh=fine,
        in_specs=placed,
        out_specs=(P(None, SUB + ("col",)), P(None, SUB + ("col",))),
        check_vma=False,
    )
```

time: 443 us -> 250 us (0.56)
  the two profiles are of different devices: /device:TPU:1 before, /device:TPU:2 now
where the time goes in v1:
time: 250 us; the launch traced here: 249 us
  blocking collectives  170 us (68%)
  starting transfers between devices  43.1 us (17%)
  waiting for transfers between devices  12.5 us (5%)
  matrix products  11.5 us (5%)
  local copies, waits for them, and re-layouts  9.46 us (4%)
    all_gather x2, blocking collectives, precondition(): lax.all_gather(row, 'y', axis=0, tiled=True)  62 us
    all_gather x2, blocking collectives, precondition(): row = lax.all_gather(mine[None], ('z', 'core'), axis=0, tiled=True)  46.2 us
    ppermute x12, starting transfers between devices, passed_along(): return lax.ppermute(block, SUB, route)  43.1 us
    all_gather x3, blocking collectives, extend_apply(): segment = lax.all_gather(own_and_halo, 'col', axis=1, tiled=True)  37.7 us
    all_gather x2, blocking collectives, precondition(): every = lax.all_gather(partial_sum[None], 'col', axis=0, tiled=True)  24 us
    ppermute x12, waiting for transfers between devices, passed_along(): return lax.ppermute(block, SUB, route)  12.5 us
    gather x24, local copies, waits for them, and re-layouts, extend_apply(): jnp.take(field, send_rows[number], axis=1) * live_slots[number][None, :]  7.86 us
    dot_general x5, matrix products, extend_apply(): jnp.dot(segment, matrix, precision=HIGH)  5.69 us
  transfers between devices with their start and end apart: 12, of which 4 were waited for; matrix products, arithmetic and copies ran while one was open for 1% of the time, Pallas kernels for 0%

profile of v1, /device:TPU:2, one launch (start us, length us, event | category | flops | bytes accessed | tf_op | source)
XLA Modules:
  0.0 249.3 jit_solution(11406883313806987691)
XLA Ops:
  0.7 0.9 fusion.28
  1.5 0.8 compare_and_fusion
  2.4 0.9 copy.33
  4.0 1.3 collective-permute-start.1
  6.0 3.0 %collective-permute-start = (f32[64,32]{1,0:T(8,128)S(1)}, f32[64,32]{1,0:T(8,128)S(1)}, u32[]{:S(2)}, u32[]{:S(2)}) collective-permute-start(f32[64,32]{1,0:T(8,128)S(1)} %bitcast_multiply_fusion.11), channel_id=1, source_target_pairs={{0,4},{4,8},{8,12},{12,16},{16,20},{20,24},{24,28},{28,32},{32,36}... | collective-permute-start | bytes 24584 | tf_op jit(solution)/shard_map/ppermute | solution.py:14
  9.7 16.0 %collective-permute-start.2 = (f32[64,32]{1,0:T(8,128)S(1)}, f32[64,32]{1,0:T(8,128)S(1)}, u32[]{:S(2)}, u32[]{:S(2)}) collective-permute-start(f32[64,32]{1,0:T(8,128)S(1)} %bitcast_multiply_fusion.9), channel_id=1, source_target_pairs={{0,192},{4,196},{8,200},{12,204},{16,208},{20,212},{24,216},{28,22... | collective-permute-start | bytes 24584 | tf_op jit(solution)/shard_map/ppermute | solution.py:14
  26.4 1.3 collective-permute-start.3
  27.7 6.3 %collective-permute-done.3 = f32[64,32]{1,0:T(8,128)S(1)} collective-permute-done((f32[64,32]{1,0:T(8,128)S(1)}, f32[64,32]{1,0:T(8,128)S(1)}, u32[]{:S(2)}, u32[]{:S(2)}) %collective-permute-start.3) | collective-permute-done | bytes 8224 | tf_op jit(solution)/shard_map/ppermute | solution.py:14
  34.1 12.7 %all_gather.27 = f32[64,1536]{1,0:T(8,128)S(1)} all-gather(f32[64,384]{1,0:T(8,128)S(1)} %concatenate.9), channel_id=1, replica_groups=mesh['y'=8,'z'=12,'core'=2,'col'=4] {'col'}, dimensions={1}, use_global_device_ids=true | all-gather | bytes 491520 | tf_op jit(solution)/shard_map/all_gather | solution.py:46
  47.3 22.9 %all-gather = f32[384,64]{1,0:T(8,128)S(1)} all-gather(f32[16,64]{1,0:T(8,128)S(1)} %dynamic-slice_bitcast_fusion.1), channel_id=2, replica_groups=mesh['y'=8,'z'=12,'core'=2,'col'=4] {'z','core'}, dimensions={0}, use_global_device_ids=true | all-gather | bytes 102400 | tf_op jit(solution)/shard_map/all_gather | solution.py:53
  70.2 29.9 %all_gather.29 = f32[192,16,64]{2,1,0:T(8,128)S(1)} all-gather(f32[24,16,64]{2,1,0:T(8,128)S(1)} %bitcast.98), channel_id=1, replica_groups=mesh['y'=8,'z'=12,'core'=2,'col'=4] {'y'}, dimensions={0}, use_global_device_ids=true | all-gather | bytes 884736 | tf_op jit(solution)/shard_map/all_gather | solution.py:54
  100.1 2.6 %convolution_bitcast_fusion.1 = f32[64,64]{0,1:T(8,128)S(1)} fusion(f32[3072,64]{1,0:T(8,128)S(1)} %bitcast.96, f32[64,3072]{1,0:T(8,128)S(1)} %copy-done.1), kind=kOutput, calls=%fused_computation.23 | convolution fusion | flops 150994944 | bytes 1589248 | tf_op jit(solution)/shard_map/dot_general | solution.py:57
  102.8 12.0 %all-gather.1 = f32[256,64]{1,0:T(8,128)S(1)} all-gather(f32[64,64]{1,0:T(8,128)S(1)} %copy.41), channel_id=3, replica_groups=mesh['y'=8,'z'=12,'core'=2,'col'=4] {'col'}, dimensions={0}, use_global_device_ids=true | all-gather | bytes 81920 | tf_op jit(solution)/shard_map/all_gather | solution.py:58
  115.1 0.9 fusion.6
  118.7 1.3 collective-permute-start.5
  120.0 3.0 %collective-permute-start.4 = (f32[64,32]{1,0:T(8,128)S(1)}, f32[64,32]{1,0:T(8,128)S(1)}, u32[]{:S(2)}, u32[]{:S(2)}) collective-permute-start(f32[64,32]{1,0:T(8,128)S(1)} %bitcast_multiply_fusion.7), channel_id=1, source_target_pairs={{0,4},{4,8},{8,12},{12,16},{16,20},{20,24},{24,28},{28,32},{32,36}... | collective-permute-start | bytes 24584 | tf_op jit(solution)/shard_map/ppermute | solution.py:14
  123.1 3.4 %collective-permute-start.6 = (f32[64,32]{1,0:T(8,128)S(1)}, f32[64,32]{1,0:T(8,128)S(1)}, u32[]{:S(2)}, u32[]{:S(2)}) collective-permute-start(f32[64,32]{1,0:T(8,128)S(1)} %bitcast_multiply_fusion.5), channel_id=1, source_target_pairs={{0,192},{4,196},{8,200},{12,204},{16,208},{20,212},{24,216},{28,22... | collective-permute-start | bytes 24584 | tf_op jit(solution)/shard_map/ppermute | solution.py:14
  126.5 1.3 collective-permute-start.7
  128.1 5.1 %collective-permute-done.7 = f32[64,32]{1,0:T(8,128)S(1)} collective-permute-done((f32[64,32]{1,0:T(8,128)S(1)}, f32[64,32]{1,0:T(8,128)S(1)}, u32[]{:S(2)}, u32[]{:S(2)}) %collective-permute-start.7) | collective-permute-done | bytes 8224 | tf_op jit(solution)/shard_map/ppermute | solution.py:14
  133.3 12.5 %all_gather.31 = f32[64,1536]{1,0:T(8,128)S(1)} all-gather(f32[64,384]{1,0:T(8,128)S(1)} %concatenate.10), channel_id=1, replica_groups=mesh['y'=8,'z'=12,'core'=2,'col'=4] {'col'}, dimensions={1}, use_global_device_ids=true | all-gather | bytes 491520 | tf_op jit(solution)/shard_map/all_gather | solution.py:46
  145.9 2.3 fusion.15
  150.9 1.3 collective-permute-start.11
  152.2 6.8 %collective-permute-start.10 = (f32[64,32]{1,0:T(8,128)S(1)}, f32[64,32]{1,0:T(8,128)S(1)}, u32[]{:S(2)}, u32[]{:S(2)}) collective-permute-start(f32[64,32]{1,0:T(8,128)S(1)} %bitcast_multiply_fusion.1), channel_id=1, source_target_pairs={{0,192},{4,196},{8,200},{12,204},{16,208},{20,212},{24,216},{28,22... | collective-permute-start | bytes 24584 | tf_op jit(solution)/shard_map/ppermute | solution.py:14
  159.0 1.3 collective-permute-start.9
  160.3 3.0 %collective-permute-start.8 = (f32[64,32]{1,0:T(8,128)S(1)}, f32[64,32]{1,0:T(8,128)S(1)}, u32[]{:S(2)}, u32[]{:S(2)}) collective-permute-start(f32[64,32]{1,0:T(8,128)S(1)} %bitcast_multiply_fusion.3), channel_id=1, source_target_pairs={{0,4},{4,8},{8,12},{12,16},{16,20},{20,24},{24,28},{28,32},{32,36}... | collective-permute-start | bytes 24584 | tf_op jit(solution)/shard_map/ppermute | solution.py:14
  163.4 0.8 collective-permute-done.8
  164.3 12.5 %all_gather.32 = f32[64,1536]{1,0:T(8,128)S(1)} all-gather(f32[64,384]{1,0:T(8,128)S(1)} %concatenate.11), channel_id=1, replica_groups=mesh['y'=8,'z'=12,'core'=2,'col'=4] {'col'}, dimensions={1}, use_global_device_ids=true | all-gather | bytes 491520 | tf_op jit(solution)/shard_map/all_gather | solution.py:46
  177.3 23.4 %all-gather.2 = f32[384,64]{1,0:T(8,128)S(1)} all-gather(f32[16,64]{1,0:T(8,128)S(1)} %dynamic-slice_bitcast_fusion), channel_id=4, replica_groups=mesh['y'=8,'z'=12,'core'=2,'col'=4] {'z','core'}, dimensions={0}, use_global_device_ids=true | all-gather | bytes 102400 | tf_op jit(solution)/shard_map/all_gather | solution.py:53
  200.7 32.1 %all_gather.34 = f32[192,16,64]{2,1,0:T(8,128)S(1)} all-gather(f32[24,16,64]{2,1,0:T(8,128)S(1)} %bitcast.99), channel_id=1, replica_groups=mesh['y'=8,'z'=12,'core'=2,'col'=4] {'y'}, dimensions={0}, use_global_device_ids=true | all-gather | bytes 884736 | tf_op jit(solution)/shard_map/all_gather | solution.py:54
  232.8 2.6 %convolution_bitcast_fusion = f32[64,64]{0,1:T(8,128)S(1)} fusion(f32[3072,64]{1,0:T(8,128)S(1)} %bitcast.97, f32[64,3072]{1,0:T(8,128)S(1)} %copy-done.1), kind=kOutput, calls=%fused_computation.22 | convolution fusion | flops 150994944 | bytes 1589248 | tf_op jit(solution)/shard_map/dot_general | solution.py:57
  235.5 12.0 %all-gather.3 = f32[256,64]{1,0:T(8,128)S(1)} all-gather(f32[64,64]{1,0:T(8,128)S(1)} %copy.59), channel_id=5, replica_groups=mesh['y'=8,'z'=12,'core'=2,'col'=4] {'col'}, dimensions={0}, use_global_device_ids=true | all-gather | bytes 81920 | tf_op jit(solution)/shard_map/all_gather | solution.py:58
  247.7 1.5 fusion.12
  (75 shorter events, 10.4 us)
Async XLA Ops:
  0.6 114.4 %copy-start = (f32[1,1536,256]{2,1,0:T(8,128)S(1)}, f32[1,1536,256]{2,1,0:T(8,128)}, u32[]{:S(2)}) copy-start(f32[1,1536,256]{2,1,0:T(8,128)} %param.11) | copy-start | bytes 4718596
  0.6 33.4 %copy-start.3 = (f32[64,256]{1,0:T(8,128)S(1)}, f32[64,256]{1,0:T(8,128)}, u32[]{:S(2)}) copy-start(f32[64,256]{1,0:T(8,128)} %param.9) | copy-start | bytes 196612
  0.7 46.2 %copy-start.2 = (f32[1,1536,64]{1,2,0:T(8,128)S(1)}, f32[1,1536,64]{1,2,0:T(8,128)}, u32[]{:S(2)}) copy-start(f32[1,1536,64]{1,2,0:T(8,128)} %param.12) | copy-start | bytes 1179652
  4.0 23.7 %collective-permute-start.1 = (f32[64,32]{1,0:T(8,128)S(1)}, f32[64,32]{1,0:T(8,128)S(1)}, u32[]{:S(2)}, u32[]{:S(2)}) collective-permute-start(f32[64,32]{1,0:T(8,128)S(1)} %bitcast_multiply_fusion.10), channel_id=1, source_target_pairs={{4,0},{8,4},{12,8},{16,12},{20,16},{24,20},{28,24},{32,28},{36,32}... | collective-permute-start | bytes 24584 | tf_op jit(solution)/shard_map/ppermute | solution.py:14
  6.0 21.7 %collective-permute-start = (f32[64,32]{1,0:T(8,128)S(1)}, f32[64,32]{1,0:T(8,128)S(1)}, u32[]{:S(2)}, u32[]{:S(2)}) collective-permute-start(f32[64,32]{1,0:T(8,128)S(1)} %bitcast_multiply_fusion.11), channel_id=1, source_target_pairs={{0,4},{4,8},{8,12},{12,16},{16,20},{20,24},{24,28},{28,32},{32,36}... | collective-permute-start | bytes 24584 | tf_op jit(solution)/shard_map/ppermute | solution.py:14
  9.7 18.0 %collective-permute-start.2 = (f32[64,32]{1,0:T(8,128)S(1)}, f32[64,32]{1,0:T(8,128)S(1)}, u32[]{:S(2)}, u32[]{:S(2)}) collective-permute-start(f32[64,32]{1,0:T(8,128)S(1)} %bitcast_multiply_fusion.9), channel_id=1, source_target_pairs={{0,192},{4,196},{8,200},{12,204},{16,208},{20,212},{24,216},{28,22... | collective-permute-start | bytes 24584 | tf_op jit(solution)/shard_map/ppermute | solution.py:14
  26.4 7.6 %collective-permute-start.3 = (f32[64,32]{1,0:T(8,128)S(1)}, f32[64,32]{1,0:T(8,128)S(1)}, u32[]{:S(2)}, u32[]{:S(2)}) collective-permute-start(f32[64,32]{1,0:T(8,128)S(1)} %bitcast_multiply_fusion.8), channel_id=1, source_target_pairs={{192,0},{196,4},{200,8},{204,12},{208,16},{212,20},{216,24},{220,2... | collective-permute-start | bytes 24584 | tf_op jit(solution)/shard_map/ppermute | solution.py:14
  34.1 66.0 %copy-start.1 = (f32[64,3072]{1,0:T(8,128)S(1)}, f32[64,3072]{1,0:T(8,128)}, u32[]{:S(2)}) copy-start(f32[64,3072]{1,0:T(8,128)} %param.13) | copy-start | bytes 2359300
  118.7 9.1 %collective-permute-start.5 = (f32[64,32]{1,0:T(8,128)S(1)}, f32[64,32]{1,0:T(8,128)S(1)}, u32[]{:S(2)}, u32[]{:S(2)}) collective-permute-start(f32[64,32]{1,0:T(8,128)S(1)} %bitcast_multiply_fusion.6), channel_id=1, source_target_pairs={{4,0},{8,4},{12,8},{16,12},{20,16},{24,20},{28,24},{32,28},{36,32}... | collective-permute-start | bytes 24584 | tf_op jit(solution)/shard_map/ppermute | solution.py:14
  120.0 7.8 %collective-permute-start.4 = (f32[64,32]{1,0:T(8,128)S(1)}, f32[64,32]{1,0:T(8,128)S(1)}, u32[]{:S(2)}, u32[]{:S(2)}) collective-permute-start(f32[64,32]{1,0:T(8,128)S(1)} %bitcast_multiply_fusion.7), channel_id=1, source_target_pairs={{0,4},{4,8},{8,12},{12,16},{16,20},{20,24},{24,28},{28,32},{32,36}... | collective-permute-start | bytes 24584 | tf_op jit(solution)/shard_map/ppermute | solution.py:14
  123.1 5.0 %collective-permute-start.6 = (f32[64,32]{1,0:T(8,128)S(1)}, f32[64,32]{1,0:T(8,128)S(1)}, u32[]{:S(2)}, u32[]{:S(2)}) collective-permute-start(f32[64,32]{1,0:T(8,128)S(1)} %bitcast_multiply_fusion.5), channel_id=1, source_target_pairs={{0,192},{4,196},{8,200},{12,204},{16,208},{20,212},{24,216},{28,22... | collective-permute-start | bytes 24584 | tf_op jit(solution)/shard_map/ppermute | solution.py:14
  126.5 6.7 %collective-permute-start.7 = (f32[64,32]{1,0:T(8,128)S(1)}, f32[64,32]{1,0:T(8,128)S(1)}, u32[]{:S(2)}, u32[]{:S(2)}) collective-permute-start(f32[64,32]{1,0:T(8,128)S(1)} %bitcast_multiply_fusion.4), channel_id=1, source_target_pairs={{192,0},{196,4},{200,8},{204,12},{208,16},{212,20},{216,24},{220,2... | collective-permute-start | bytes 24584 | tf_op jit(solution)/shard_map/ppermute | solution.py:14
  148.2 29.1 %copy-start.4 = (f32[64,256]{1,0:T(8,128)}, f32[64,256]{1,0:T(8,128)S(1)}, u32[]{:S(2)}) copy-start(f32[64,256]{1,0:T(8,128)S(1)} %fusion.15) | copy-start | bytes 196612
  150.9 12.4 %collective-permute-start.11 = (f32[64,32]{1,0:T(8,128)S(1)}, f32[64,32]{1,0:T(8,128)S(1)}, u32[]{:S(2)}, u32[]{:S(2)}) collective-permute-start(f32[64,32]{1,0:T(8,128)S(1)} %bitcast_multiply_fusion), channel_id=1, source_target_pairs={{192,0},{196,4},{200,8},{204,12},{208,16},{212,20},{216,24},{220,2... | collective-permute-start | bytes 24584 | tf_op jit(solution)/shard_map/ppermute | solution.py:14
  152.2 11.1 %collective-permute-start.10 = (f32[64,32]{1,0:T(8,128)S(1)}, f32[64,32]{1,0:T(8,128)S(1)}, u32[]{:S(2)}, u32[]{:S(2)}) collective-permute-start(f32[64,32]{1,0:T(8,128)S(1)} %bitcast_multiply_fusion.1), channel_id=1, source_target_pairs={{0,192},{4,196},{8,200},{12,204},{16,208},{20,212},{24,216},{28,22... | collective-permute-start | bytes 24584 | tf_op jit(solution)/shard_map/ppermute | solution.py:14
  159.0 4.4 %collective-permute-start.9 = (f32[64,32]{1,0:T(8,128)S(1)}, f32[64,32]{1,0:T(8,128)S(1)}, u32[]{:S(2)}, u32[]{:S(2)}) collective-permute-start(f32[64,32]{1,0:T(8,128)S(1)} %bitcast_multiply_fusion.2), channel_id=1, source_target_pairs={{4,0},{8,4},{12,8},{16,12},{20,16},{24,20},{28,24},{32,28},{36,32}... | collective-permute-start | bytes 24584 | tf_op jit(solution)/shard_map/ppermute | solution.py:14
  160.3 3.9 %collective-permute-start.8 = (f32[64,32]{1,0:T(8,128)S(1)}, f32[64,32]{1,0:T(8,128)S(1)}, u32[]{:S(2)}, u32[]{:S(2)}) collective-permute-start(f32[64,32]{1,0:T(8,128)S(1)} %bitcast_multiply_fusion.3), channel_id=1, source_target_pairs={{0,4},{4,8},{8,12},{12,16},{16,20},{20,24},{24,28},{28,32},{32,36}... | collective-permute-start | bytes 24584 | tf_op jit(solution)/shard_map/ppermute | solution.py:14

commit v2 on v1

v2 whole, which is shorter than its diff:
```python
import jax
import jax.numpy as jnp
from jax import lax
from jax.sharding import Mesh, PartitionSpec as P

HIGH = lax.Precision.HIGHEST
CORES = 2
ZLEN = 12
SUB = ("y", "z", "core")


def passed_along(block, distance, subs):
    route = [(i - distance, i) for i in range(subs) if 0 <= i - distance < subs]
    return lax.ppermute(block, SUB, route)


def body(
    right_sides, operator, local_inverse, coarse_basis, coarse_inverse, send_index, halo_count
):
    own_width = right_sides.shape[1]
    rhs_width = right_sides.shape[0]
    halo_slots = send_index.shape[3]
    n_nb = send_index.shape[2]
    n_col = lax.axis_size("col")
    ylen = lax.axis_size("y")
    subs = ylen * ZLEN * CORES
    stride = subs // 4
    offsets = (1, -1, stride, -stride)
    send_rows = send_index[0, 0]
    counts = halo_count[0, 0]
    slots = jnp.arange(halo_slots, dtype=jnp.int32)
    live_slots = (slots[None, :] < counts[:, None]).astype(jnp.float32)
    basis_rows = coarse_basis[0]
    mode_count = basis_rows.shape[1]
    block_len = basis_rows.shape[0] // n_col
    blocks_of = lambda m: m.reshape(n_col, block_len, m.shape[-1])
    operator_rows = blocks_of(operator[0])
    inverse_rows = blocks_of(local_inverse[0])
    basis_blocks = blocks_of(basis_rows)
    own_basis_all = basis_blocks[:, :own_width]
    column_index = lax.axis_index("col")
    quarter = mode_count // n_col
    own_basis = lax.dynamic_index_in_dim(own_basis_all, column_index, 0, keepdims=False)

    def pack_own(field):
        packed = [
            jnp.take(field, send_rows[n], axis=1) * live_slots[n][None, :] for n in range(n_nb)
        ]
        return jnp.concatenate(packed, axis=1)

    def halos(packs):
        got = [passed_along(packs[:, :, n], offsets[n], subs) for n in range(n_nb)]
        return got

    def ext_of(own_all, got):
        return jnp.concatenate([own_all] + got, axis=2)

    def apply(ext, blocks):
        return lax.dot_general(ext, blocks, (((0, 2), (0, 1)), ((), ())), precision=HIGH)

    def gathered_ext(field, extra=None):
        payload = jnp.concatenate([field, pack_own(field)], axis=1)
        if extra is not None:
            payload = jnp.concatenate([payload, extra], axis=0)
        g = lax.all_gather(payload[None], "col", axis=0, tiled=True)
        own_all = g[:, :rhs_width, :own_width]
        packs = g[:, :rhs_width, own_width:].reshape(n_col, rhs_width, n_nb, halo_slots)
        return ext_of(own_all, halos(packs)), g[:, rhs_width:]

    def coarse_partial(ext):
        coeff = apply(ext, basis_blocks)
        mine = lax.dynamic_slice_in_dim(coeff, column_index * quarter, quarter, 1).T
        g = lax.all_gather(mine[None], "z", axis=0, tiled=True)
        g = lax.all_gather(g[None], ("y", "core"), axis=0, tiled=True)
        g = g.reshape(ylen, CORES, ZLEN, quarter, rhs_width).transpose(0, 2, 1, 3, 4)
        kept_rows = g.reshape(subs * quarter, rhs_width)
        return jnp.dot(coarse_inverse, kept_rows, precision=HIGH)

    index_row = jnp.concatenate(
        [
            send_rows.reshape(-1).astype(jnp.float32),
            counts.astype(jnp.float32),
            jnp.zeros((own_width + n_nb * halo_slots - n_nb * halo_slots - n_nb,), jnp.float32),
        ]
    )[None]
    ext_b, idx = gathered_ext(right_sides, index_row)
    send_all = idx[:, 0, : n_nb * halo_slots].astype(jnp.int32).reshape(n_col, n_nb, halo_slots)
    counts_all = idx[:, 0, n_nb * halo_slots : n_nb * halo_slots + n_nb].astype(jnp.int32)
    live_all = (slots[None, None, :] < counts_all[:, :, None]).astype(jnp.float32)

    local_1 = apply(ext_b, inverse_rows)
    partial_1 = coarse_partial(ext_b)
    g = lax.all_gather(
        jnp.concatenate([local_1, partial_1.T], axis=1)[None], "col", axis=0, tiled=True
    )
    local_all = g[:, :, :own_width]
    coarse_1 = jnp.sum(g[:, :, own_width:], axis=0)
    coarse_part_all = jnp.einsum("rm,com->cro", coarse_1, own_basis_all, precision=HIGH)
    first_all = local_all + coarse_part_all
    packs_first = jnp.stack(
        [
            jnp.take_along_axis(first_all, send_all[:, n][:, None, :], axis=2)
            * live_all[:, n][:, None, :]
            for n in range(n_nb)
        ],
        axis=2,
    )
    ext_f = ext_of(first_all, halos(packs_first))
    applied = apply(ext_f, operator_rows)
    residual = right_sides - applied
    first_pass = lax.dynamic_index_in_dim(first_all, column_index, 0, keepdims=False)

    ext_r, _ = gathered_ext(residual)
    local_2 = apply(ext_r, inverse_rows)
    partial_2 = coarse_partial(ext_r)
    g2 = lax.all_gather(partial_2.T[None], "col", axis=0, tiled=True)
    coarse_2 = jnp.sum(g2, axis=0)
    coarse_part_2 = lax.dot_general(
        coarse_2, own_basis, (((1,), (1,)), ((), ())), precision=HIGH
    )
    solution = first_pass + (local_2 + coarse_part_2)
    return (solution, residual)


def solution(mesh):
    subs, n_col = mesh.devices.shape
    fine = Mesh(
        mesh.devices.reshape(subs // (ZLEN * CORES), ZLEN, CORES, n_col), SUB + ("col",)
    )
    placed = (
        P(None, SUB + ("col",)),
        P(SUB, None, "col"),
        P(SUB, None, "col"),
        P(SUB, None, None),
        P(SUB, "col"),
        P(SUB, "col", None, None),
        P(SUB, "col", None),
    )
    return jax.shard_map(
        body,
        mesh=fine,
        in_specs=placed,
        out_specs=(P(None, SUB + ("col",)), P(None, SUB + ("col",))),
        check_vma=False,
    )
```

time: 250 us -> 263 us (1.052)
  the two profiles are of different devices: /device:TPU:2 before, /device:TPU:1 now
where the time goes in v2:
time: 263 us; the launch traced here: 260 us
  blocking collectives  142 us (54%)
  starting transfers between devices  44.6 us (17%)
  local copies, waits for them, and re-layouts  41.5 us (16%)
  matrix products  11.5 us (4%)
  waiting for transfers between devices  10.5 us (4%)
  other arithmetic  7.78 us (3%)
    all_gather x2, blocking collectives, coarse_partial(): g = lax.all_gather(g[None], ('y', 'core'), axis=0, tiled=True)  54.7 us
    all_gather x2, blocking collectives, coarse_partial(): g = lax.all_gather(mine[None], 'z', axis=0, tiled=True)  45.9 us
    ppermute x12, starting transfers between devices, passed_along(): return lax.ppermute(block, SUB, route)  44.6 us
    all_gather x2, blocking collectives, gathered_ext(): g = lax.all_gather(payload[None], 'col', axis=0, tiled=True)  21.7 us
    unnamed x78, local copies, waits for them, and re-layouts  12.5 us
    gather x12, local copies, waits for them, and re-layouts, body(): jnp.take_along_axis(first_all, send_all[:, n][:, None, :], axis=2)  12.1 us
    all_gather x1, blocking collectives, body(): lax.all_gather(jnp.concatenate([local_1, partial_1.T], axis=1)[None], 'co...  10.9 us
    ppermute x12, waiting for transfers between devices, passed_along(): return lax.ppermute(block, SUB, route)  10.5 us
  transfers between devices with their start and end apart: 12, of which 3 were waited for; matrix products, arithmetic and copies ran while one was open for 3% of the time, Pallas kernels for 0%

profile of v2, /device:TPU:1, one launch (start us, length us, event | category | flops | bytes accessed | tf_op | source)
XLA Modules:
  0.0 259.7 jit_solution(5912756422985759774)
XLA Ops:
  7.9 11.0 %all-gather.8 = f32[4,65,384]{2,1,0:T(8,128)S(1)} all-gather(f32[1,65,384]{2,1,0:T(8,128)S(1)} %maximum_bitcast_fusion), channel_id=2, replica_groups=mesh['y'=8,'z'=12,'core'=2,'col'=4] {'col'}, dimensions={0}, use_global_device_ids=true | all-gather | bytes 499200 | tf_op jit(solution)/shard_map/all_gather | solution.py:65
  19.9 7.4 %collective-permute-start = (f32[4,64,32]{2,1,0:T(8,128)}, f32[4,64,32]{2,1,0:T(8,128)S(1)}, u32[]{:S(2)}, u32[]{:S(2)}) collective-permute-start(f32[4,64,32]{2,1,0:T(8,128)} %bitcast.15), channel_id=1, source_target_pairs={{0,4},{4,8},{8,12},{12,16},{16,20},{20,24},{24,28},{28,32},{32,36}... | collective-permute-start | bytes 98312 | tf_op jit(solution)/shard_map/ppermute | solution.py:14
  28.1 7.9 %collective-permute-start.1 = (f32[4,64,32]{2,1,0:T(8,128)}, f32[4,64,32]{2,1,0:T(8,128)S(1)}, u32[]{:S(2)}, u32[]{:S(2)}) collective-permute-start(f32[4,64,32]{2,1,0:T(8,128)} %bitcast.16), channel_id=1, source_target_pairs={{4,0},{8,4},{12,8},{16,12},{20,16},{24,20},{28,24},{32,28},{36,32}... | collective-permute-start | bytes 98312 | tf_op jit(solution)/shard_map/ppermute | solution.py:14
  48.4 27.1 %all-gather.1 = f32[192,64]{1,0:T(8,128)S(1)} all-gather(f32[16,64]{1,0:T(8,128)S(1)} %dynamic-slice_bitcast_fusion.1), channel_id=3, replica_groups=mesh['y'=8,'z'=12,'core'=2,'col'=4] {'z'}, dimensions={0}, use_global_device_ids=true | all-gather | bytes 53248 | tf_op jit(solution)/shard_map/all_gather | solution.py:73
  75.5 27.0 %all-gather.2 = f32[192,16,64]{2,1,0:T(8,128)S(1)} all-gather(f32[12,16,64]{2,1,0:T(8,128)S(1)} %bitcast.179), channel_id=4, replica_groups=mesh['y'=8,'z'=12,'core'=2,'col'=4] {'y','core'}, dimensions={0}, use_global_device_ids=true | all-gather | bytes 835584 | tf_op jit(solution)/shard_map/all_gather | solution.py:74
  103.6 2.6 %fusion.18 = f32[64,64]{1,0:T(8,128)S(1)} fusion(f32[3072,64]{1,0:T(8,128)S(1)} %bitcast.164, f32[64,3072]{1,0:T(8,128)S(1)} %copy-done.1), kind=kOutput, calls=%fused_computation.92 | convolution fusion | flops 150994944 | bytes 1589248 | tf_op jit(solution)/shard_map/dot_general | solution.py:77
  106.2 10.9 %all-gather.3 = f32[256,320]{1,0:T(8,128)S(1)} all-gather(f32[64,320]{1,0:T(8,128)S(1)} %pad_maximum_fusion), channel_id=5, replica_groups=mesh['y'=8,'z'=12,'core'=2,'col'=4] {'col'}, dimensions={0}, use_global_device_ids=true | all-gather | bytes 409600 | tf_op jit(solution)/shard_map/all_gather | solution.py:93
  117.7 1.8 gather_fusion.7
  119.5 1.8 gather_fusion.6
  121.4 1.8 gather_fusion.5
  123.2 1.8 gather_fusion.4
  127.9 1.6 copy.148
  132.5 4.9 %collective-permute-start.6 = (f32[4,64,32]{2,1,0:T(8,128)S(1)}, f32[4,64,32]{2,1,0:T(8,128)S(1)}, u32[]{:S(2)}, u32[]{:S(2)}) collective-permute-start(f32[4,64,32]{2,1,0:T(8,128)S(1)} %bitcast_multiply_fusion.1), channel_id=1, source_target_pairs={{0,192},{4,196},{8,200},{12,204},{16,208},{20,212},{24,216},{28,22... | collective-permute-start | bytes 98312 | tf_op jit(solution)/shard_map/ppermute | solution.py:14
  138.0 4.3 %collective-permute-start.4 = (f32[4,64,32]{2,1,0:T(8,128)S(1)}, f32[4,64,32]{2,1,0:T(8,128)S(1)}, u32[]{:S(2)}, u32[]{:S(2)}) collective-permute-start(f32[4,64,32]{2,1,0:T(8,128)S(1)} %bitcast_multiply_fusion.3), channel_id=1, source_target_pairs={{0,4},{4,8},{8,12},{12,16},{16,20},{20,24},{24,28},{28,32},{32,36}... | collective-permute-start | bytes 98312 | tf_op jit(solution)/shard_map/ppermute | solution.py:14
  142.4 1.9 collective-permute-start.5
  145.7 3.1 %collective-permute-done.5 = f32[4,64,32]{2,1,0:T(8,128)} collective-permute-done((f32[4,64,32]{2,1,0:T(8,128)S(1)}, f32[4,64,32]{2,1,0:T(8,128)}, u32[]{:S(2)}, u32[]{:S(2)}) %collective-permute-start.5) | collective-permute-done | bytes 32800 | tf_op jit(solution)/shard_map/ppermute | solution.py:14
  150.1 2.3 fusion.3
  156.6 10.7 %all-gather.4 = f32[256,384]{1,0:T(8,128)S(1)} all-gather(f32[64,384]{1,0:T(8,128)} %concatenate.30), channel_id=6, replica_groups=mesh['y'=8,'z'=12,'core'=2,'col'=4] {'col'}, dimensions={0}, use_global_device_ids=true | all-gather | bytes 491520 | tf_op jit(solution)/shard_map/all_gather | solution.py:65
  167.9 1.7 copy.157
  169.6 1.6 fusion.15
  171.2 1.6 copy.176
  172.8 1.6 copy.175
  175.9 4.3 %collective-permute-start.8 = (f32[4,64,32]{2,1,0:T(8,128)}, f32[4,64,32]{2,1,0:T(8,128)S(1)}, u32[]{:S(2)}, u32[]{:S(2)}) collective-permute-start(f32[4,64,32]{2,1,0:T(8,128)} %bitcast.184), channel_id=1, source_target_pairs={{0,4},{4,8},{8,12},{12,16},{16,20},{20,24},{24,28},{28,32},{32,36}... | collective-permute-start | bytes 98312 | tf_op jit(solution)/shard_map/ppermute | solution.py:14
  180.2 1.9 collective-permute-start.9
  182.1 6.6 %collective-permute-start.10 = (f32[4,64,32]{2,1,0:T(8,128)}, f32[4,64,32]{2,1,0:T(8,128)}, u32[]{:S(2)}, u32[]{:S(2)}) collective-permute-start(f32[4,64,32]{2,1,0:T(8,128)} %bitcast.182), channel_id=1, source_target_pairs={{0,192},{4,196},{8,200},{12,204},{16,208},{20,212},{24,216},{28,22... | collective-permute-start | bytes 98312 | tf_op jit(solution)/shard_map/ppermute | solution.py:14
  188.8 1.5 collective-permute-start.11
  191.0 6.7 %collective-permute-done.11 = f32[4,64,32]{2,1,0:T(8,128)} collective-permute-done((f32[4,64,32]{2,1,0:T(8,128)}, f32[4,64,32]{2,1,0:T(8,128)}, u32[]{:S(2)}, u32[]{:S(2)}) %collective-permute-start.11) | collective-permute-done | bytes 32800 | tf_op jit(solution)/shard_map/ppermute | solution.py:14
  199.5 18.8 %all-gather.5 = f32[192,64]{1,0:T(8,128)S(1)} all-gather(f32[16,64]{1,0:T(8,128)S(1)} %dynamic-slice_bitcast_fusion), channel_id=7, replica_groups=mesh['y'=8,'z'=12,'core'=2,'col'=4] {'z'}, dimensions={0}, use_global_device_ids=true | all-gather | bytes 53248 | tf_op jit(solution)/shard_map/all_gather | solution.py:73
  218.3 27.7 %all-gather.6 = f32[192,16,64]{2,1,0:T(8,128)S(1)} all-gather(f32[12,16,64]{2,1,0:T(8,128)S(1)} %bitcast.180), channel_id=8, replica_groups=mesh['y'=8,'z'=12,'core'=2,'col'=4] {'y','core'}, dimensions={0}, use_global_device_ids=true | all-gather | bytes 835584 | tf_op jit(solution)/shard_map/all_gather | solution.py:74
  246.2 2.6 %fusion.19 = f32[64,64]{1,0:T(8,128)S(1)} fusion(f32[3072,64]{1,0:T(8,128)S(1)} %bitcast.166, f32[64,3072]{1,0:T(8,128)S(1)} %copy-done.1), kind=kOutput, calls=%fused_computation.93 | convolution fusion | flops 150994944 | bytes 1589248 | tf_op jit(solution)/shard_map/dot_general | solution.py:77
  248.8 9.1 %all-gather.7 = f32[256,64]{1,0:T(8,128)S(1)} all-gather(f32[64,64]{1,0:T(8,128)S(1)} %fusion.19), channel_id=9, replica_groups=mesh['y'=8,'z'=12,'core'=2,'col'=4] {'col'}, dimensions={0}, use_global_device_ids=true | all-gather | bytes 81920 | tf_op jit(solution)/shard_map/all_gather | solution.py:116
  258.2 1.5 fusion.2
  (179 shorter events, 40.7 us)
Async XLA Ops:
  0.6 46.8 %copy-start = (f32[1,1536,256]{2,1,0:T(8,128)S(1)}, f32[1,1536,256]{2,1,0:T(8,128)}, u32[]{:S(2)}) copy-start(f32[1,1536,256]{2,1,0:T(8,128)} %param.13) | copy-start | bytes 4718596
  0.6 7.0 %copy-start.3 = (f32[64,256]{1,0:T(8,128)S(1)}, f32[64,256]{1,0:T(8,128)}, u32[]{:S(2)}) copy-start(f32[64,256]{1,0:T(8,128)} %param.11) | copy-start | bytes 196612
  2.3 5.5 %copy-start.17 = (pred[32]{0:T(512)(128)(4,1)}, pred[32]{0:T(512)(128)(4,1)S(1)}, u32[]{:S(2)}) copy-start(pred[32]{0:T(512)(128)(4,1)S(1)} %get-tuple-element.4) | copy-start | bytes 100
  2.3 5.5 %copy-start.19 = (pred[32]{0:T(512)(128)(4,1)}, pred[32]{0:T(512)(128)(4,1)S(1)}, u32[]{:S(2)}) copy-start(pred[32]{0:T(512)(128)(4,1)S(1)} %get-tuple-element.32) | copy-start | bytes 100
  2.3 5.5 %copy-start.21 = (pred[32]{0:T(512)(128)(4,1)}, pred[32]{0:T(512)(128)(4,1)S(1)}, u32[]{:S(2)}) copy-start(pred[32]{0:T(512)(128)(4,1)S(1)} %get-tuple-element.34) | copy-start | bytes 100
  2.4 5.5 %copy-start.23 = (pred[32]{0:T(512)(128)(4,1)}, pred[32]{0:T(512)(128)(4,1)S(1)}, u32[]{:S(2)}) copy-start(pred[32]{0:T(512)(128)(4,1)S(1)} %get-tuple-element.36) | copy-start | bytes 100
  3.8 4.1 %copy-start.27 = (f32[32]{0:T(128)}, f32[32]{0:T(128)S(1)}, u32[]{:S(2)}) copy-start(f32[32]{0:T(128)S(1)} %get-tuple-element.29) | copy-start | bytes 388
  3.8 4.1 %copy-start.29 = (f32[32]{0:T(128)}, f32[32]{0:T(128)S(1)}, u32[]{:S(2)}) copy-start(f32[32]{0:T(128)S(1)} %get-tuple-element.30) | copy-start | bytes 388
  3.8 4.1 %copy-start.31 = (f32[32]{0:T(128)}, f32[32]{0:T(128)S(1)}, u32[]{:S(2)}) copy-start(f32[32]{0:T(128)S(1)} %get-tuple-element.31) | copy-start | bytes 388
  7.9 35.6 %copy-start.6 = (f32[1,1536,64]{1,2,0:T(8,128)S(1)}, f32[1,1536,64]{1,2,0:T(8,128)}, u32[]{:S(2)}) copy-start(f32[1,1536,64]{1,2,0:T(8,128)} %param.14) | copy-start | bytes 1179652
  19.9 23.8 %collective-permute-start = (f32[4,64,32]{2,1,0:T(8,128)}, f32[4,64,32]{2,1,0:T(8,128)S(1)}, u32[]{:S(2)}, u32[]{:S(2)}) collective-permute-start(f32[4,64,32]{2,1,0:T(8,128)} %bitcast.15), channel_id=1, source_target_pairs={{0,4},{4,8},{8,12},{12,16},{16,20},{20,24},{24,28},{28,32},{32,36}... | collective-permute-start | bytes 98312 | tf_op jit(solution)/shard_map/ppermute | solution.py:14
  28.1 15.6 %collective-permute-start.1 = (f32[4,64,32]{2,1,0:T(8,128)}, f32[4,64,32]{2,1,0:T(8,128)S(1)}, u32[]{:S(2)}, u32[]{:S(2)}) collective-permute-start(f32[4,64,32]{2,1,0:T(8,128)} %bitcast.16), channel_id=1, source_target_pairs={{4,0},{8,4},{12,8},{16,12},{20,16},{24,20},{28,24},{32,28},{36,32}... | collective-permute-start | bytes 98312 | tf_op jit(solution)/shard_map/ppermute | solution.py:14
  36.8 7.0 %collective-permute-start.2 = (f32[4,64,32]{2,1,0:T(8,128)}, f32[4,64,32]{2,1,0:T(8,128)S(1)}, u32[]{:S(2)}, u32[]{:S(2)}) collective-permute-start(f32[4,64,32]{2,1,0:T(8,128)} %bitcast.17), channel_id=1, source_target_pairs={{0,192},{4,196},{8,200},{12,204},{16,208},{20,212},{24,216},{28,22... | collective-permute-start | bytes 98312 | tf_op jit(solution)/shard_map/ppermute | solution.py:14
  38.8 6.9 %collective-permute-start.3 = (f32[4,64,32]{2,1,0:T(8,128)}, f32[4,64,32]{2,1,0:T(8,128)}, u32[]{:S(2)}, u32[]{:S(2)}) collective-permute-start(f32[4,64,32]{2,1,0:T(8,128)} %bitcast.18), channel_id=1, source_target_pairs={{192,0},{196,4},{200,8},{204,12},{208,16},{212,20},{216,24},{220,2... | collective-permute-start | bytes 98312 | tf_op jit(solution)/shard_map/ppermute | solution.py:14
  43.7 73.4 %copy-start.2 = (f32[4,384,64]{1,2,0:T(8,128)}, f32[4,384,64]{1,2,0:T(8,128)S(1)}, u32[]{:S(2)}) copy-start(f32[4,384,64]{1,2,0:T(8,128)S(1)} %copy.133) | copy-start | bytes 1179652
  125.1 17.3 %copy-start.12 = (f32[4,32]{1,0:T(4,128)S(1)}, f32[4,32]{1,0:T(4,128)}, u32[]{:S(2)}) copy-start(f32[4,32]{1,0:T(4,128)} %get-tuple-element.22) | copy-start | bytes 1540
  125.1 17.3 %copy-start.33 = (pred[4,32]{1,0:T(4,128)(4,1)S(1)}, pred[4,32]{1,0:T(4,128)(4,1)}, u32[]{:S(2)}) copy-start(pred[4,32]{1,0:T(4,128)(4,1)} %and_bitcast_fusion.2) | copy-start | bytes 388
  125.1 25.0 %copy-start.4 = (f32[64,256]{1,0:T(8,128)S(1)}, f32[64,256]{1,0:T(8,128)}, u32[]{:S(2)}) copy-start(f32[64,256]{1,0:T(8,128)} %param.11) | copy-start | bytes 196612
  130.5 13.9 %collective-permute-start.7 = (f32[4,64,32]{2,1,0:T(8,128)S(1)}, f32[4,64,32]{2,1,0:T(8,128)S(1)}, u32[]{:S(2)}, u32[]{:S(2)}) collective-permute-start(f32[4,64,32]{2,1,0:T(8,128)S(1)} %bitcast_multiply_fusion), channel_id=1, source_target_pairs={{192,0},{196,4},{200,8},{204,12},{208,16},{212,20},{216,24},{220,2... | collective-permute-start | bytes 98312 | tf_op jit(solution)/shard_map/ppermute | solution.py:14
  132.5 11.9 %collective-permute-start.6 = (f32[4,64,32]{2,1,0:T(8,128)S(1)}, f32[4,64,32]{2,1,0:T(8,128)S(1)}, u32[]{:S(2)}, u32[]{:S(2)}) collective-permute-start(f32[4,64,32]{2,1,0:T(8,128)S(1)} %bitcast_multiply_fusion.1), channel_id=1, source_target_pairs={{0,192},{4,196},{8,200},{12,204},{16,208},{20,212},{24,216},{28,22... | collective-permute-start | bytes 98312 | tf_op jit(solution)/shard_map/ppermute | solution.py:14
  138.0 6.3 %collective-permute-start.4 = (f32[4,64,32]{2,1,0:T(8,128)S(1)}, f32[4,64,32]{2,1,0:T(8,128)S(1)}, u32[]{:S(2)}, u32[]{:S(2)}) collective-permute-start(f32[4,64,32]{2,1,0:T(8,128)S(1)} %bitcast_multiply_fusion.3), channel_id=1, source_target_pairs={{0,4},{4,8},{8,12},{12,16},{16,20},{20,24},{24,28},{28,32},{32,36}... | collective-permute-start | bytes 98312 | tf_op jit(solution)/shard_map/ppermute | solution.py:14
  142.4 6.4 %collective-permute-start.5 = (f32[4,64,32]{2,1,0:T(8,128)S(1)}, f32[4,64,32]{2,1,0:T(8,128)}, u32[]{:S(2)}, u32[]{:S(2)}) collective-permute-start(f32[4,64,32]{2,1,0:T(8,128)S(1)} %bitcast_multiply_fusion.2), channel_id=1, source_target_pairs={{4,0},{8,4},{12,8},{16,12},{20,16},{24,20},{28,24},{32,28},{36,32}... | collective-permute-start | bytes 98312 | tf_op jit(solution)/shard_map/ppermute | solution.py:14
  150.1 5.6 %copy-start.22 = (pred[32]{0:T(512)(128)(4,1)S(1)}, pred[32]{0:T(512)(128)(4,1)}, u32[]{:S(2)}) copy-start(pred[32]{0:T(512)(128)(4,1)} %copy-done.21) | copy-start | bytes 100
  150.1 5.6 %copy-start.24 = (pred[32]{0:T(512)(128)(4,1)S(1)}, pred[32]{0:T(512)(128)(4,1)}, u32[]{:S(2)}) copy-start(pred[32]{0:T(512)(128)(4,1)} %copy-done.23) | copy-start | bytes 100
  150.1 5.7 %copy-start.18 = (pred[32]{0:T(512)(128)(4,1)S(1)}, pred[32]{0:T(512)(128)(4,1)}, u32[]{:S(2)}) copy-start(pred[32]{0:T(512)(128)(4,1)} %copy-done.17) | copy-start | bytes 100
  150.1 5.7 %copy-start.20 = (pred[32]{0:T(512)(128)(4,1)S(1)}, pred[32]{0:T(512)(128)(4,1)}, u32[]{:S(2)}) copy-start(pred[32]{0:T(512)(128)(4,1)} %copy-done.19) | copy-start | bytes 100
  152.4 17.2 %copy-start.5 = (f32[64,256]{1,0:T(8,128)}, f32[64,256]{1,0:T(8,128)S(1)}, u32[]{:S(2)}) copy-start(f32[64,256]{1,0:T(8,128)S(1)} %fusion.3) | copy-start | bytes 196612
  175.9 15.0 %collective-permute-start.8 = (f32[4,64,32]{2,1,0:T(8,128)}, f32[4,64,32]{2,1,0:T(8,128)S(1)}, u32[]{:S(2)}, u32[]{:S(2)}) collective-permute-start(f32[4,64,32]{2,1,0:T(8,128)} %bitcast.184), channel_id=1, source_target_pairs={{0,4},{4,8},{8,12},{12,16},{16,20},{20,24},{24,28},{28,32},{32,36}... | collective-permute-start | bytes 98312 | tf_op jit(solution)/shard_map/ppermute | solution.py:14
  180.2 10.7 %collective-permute-start.9 = (f32[4,64,32]{2,1,0:T(8,128)}, f32[4,64,32]{2,1,0:T(8,128)}, u32[]{:S(2)}, u32[]{:S(2)}) collective-permute-start(f32[4,64,32]{2,1,0:T(8,128)} %bitcast.183), channel_id=1, source_target_pairs={{4,0},{8,4},{12,8},{16,12},{20,16},{24,20},{28,24},{32,28},{36,32}... | collective-permute-start | bytes 98312 | tf_op jit(solution)/shard_map/ppermute | solution.py:14
  182.1 8.8 %collective-permute-start.10 = (f32[4,64,32]{2,1,0:T(8,128)}, f32[4,64,32]{2,1,0:T(8,128)}, u32[]{:S(2)}, u32[]{:S(2)}) collective-permute-start(f32[4,64,32]{2,1,0:T(8,128)} %bitcast.182), channel_id=1, source_target_pairs={{0,192},{4,196},{8,200},{12,204},{16,208},{20,212},{24,216},{28,22... | collective-permute-start | bytes 98312 | tf_op jit(solution)/shard_map/ppermute | solution.py:14
  188.8 8.9 %collective-permute-start.11 = (f32[4,64,32]{2,1,0:T(8,128)}, f32[4,64,32]{2,1,0:T(8,128)}, u32[]{:S(2)}, u32[]{:S(2)}) collective-permute-start(f32[4,64,32]{2,1,0:T(8,128)} %bitcast.181), channel_id=1, source_target_pairs={{192,0},{196,4},{200,8},{204,12},{208,16},{212,20},{216,24},{220,2... | collective-permute-start | bytes 98312 | tf_op jit(solution)/shard_map/ppermute | solution.py:14
  246.2 11.8 %slice-start = ((f32[4,384,64]{1,2,0:T(8,128)}), f32[4,256,64]{1,2,0:T(8,128)S(1)}, s32[]{:S(2)}) async-start(f32[4,384,64]{1,2,0:T(8,128)} %copy-done.2), calls=%async_computation | async-start | bytes 524288 | tf_op jit(solution)/shard_map/slice | solution.py:40
  (15 other events, 32.5 us)

commit v3 on v2

--- a/solution.py
+++ b/solution.py
@@ -41,12 +41,13 @@
     column_index = lax.axis_index("col")
     quarter = mode_count // n_col
     own_basis = lax.dynamic_index_in_dim(own_basis_all, column_index, 0, keepdims=False)
+    rows = jnp.arange(own_width, dtype=jnp.int32)
+    select_own = (
+        (rows[:, None, None] == send_rows[None]).astype(jnp.float32) * live_slots[None]
+    ).reshape(own_width, n_nb * halo_slots)
 
     def pack_own(field):
-        packed = [
-            jnp.take(field, send_rows[n], axis=1) * live_slots[n][None, :] for n in range(n_nb)
-        ]
-        return jnp.concatenate(packed, axis=1)
+        return jnp.dot(field, select_own, precision=HIGH)
 
     def halos(packs):
         got = [passed_along(packs[:, :, n], offsets[n], subs) for n in range(n_nb)]
@@ -97,15 +98,20 @@
     coarse_1 = jnp.sum(g[:, :, own_width:], axis=0)
     coarse_part_all = jnp.einsum("rm,com->cro", coarse_1, own_basis_all, precision=HIGH)
     first_all = local_all + coarse_part_all
-    packs_first = jnp.stack(
-        [
-            jnp.take_along_axis(first_all, send_all[:, n][:, None, :], axis=2)
-            * live_all[:, n][:, None, :]
-            for n in range(n_nb)
-        ],
-        axis=2,
-    )
-    ext_f = ext_of(first_all, halos(packs_first))
+    select_all = (rows[None, :, None, None] == send_all[:, None]).astype(jnp.float32) * live_all[
+        :, None
+    ]
+    got_first = [
+        passed_along(
+            lax.dot_general(
+                first_all, select_all[:, :, n], (((2,), (1,)), ((0,), (0,))), precision=HIGH
+            ),
+            offsets[n],
+            subs,
+        )
+        for n in range(n_nb)
+    ]
+    ext_f = ext_of(first_all, got_first)
     applied = apply(ext_f, operator_rows)
     residual = right_sides - applied
     first_pass = lax.dynamic_index_in_dim(first_all, column_index, 0, keepdims=False)

time: 263 us -> 239 us (0.909)
  local copies, waits for them, and re-layouts: 41.5 us -> 20.9 us
  other arithmetic: 7.78 us -> 2.75 us
  waiting for transfers between devices: 10.5 us -> 5.64 us
  blocking collectives: 142 us -> 145 us
  matrix products: 11.5 us -> 14.4 us
    gather x28 -> x0, local copies, waits for them, and re-layouts: 17.9 us -> none  [the longest x12 12.1 us: body(): jnp.take_along_axis(first_all, send_all[:, n][:, None, :], axis=2)]
    ppermute x12, waiting for transfers between devices: 10.5 us -> 5.64 us  [passed_along(): return lax.ppermute(block, SUB, route)]
    unnamed x78 -> x27, local copies, waits for them, and re-layouts: 12.5 us -> 8.88 us
    all_gather x2, blocking collectives: 45.9 us -> 49 us  [coarse_partial(): g = lax.all_gather(mine[None], 'z', axis=0, tiled=True)]
    and x5 -> x0, other arithmetic: 2.92 us -> none  [the longest x4 2.09 us: body(): jnp.take_along_axis(first_all, send_all[:, n][:, None, :], axis=2)]
    dot_general x0 -> x6, matrix products: none -> 2.7 us  [the longest x4 1.4 us: body(): lax.dot_general(first_all, select_all[:, :, n], (((2,), (1,)), ((0,), (0,...]
  transfers between devices with their start and end apart: 12 -> 12, of which waited for: 3 -> 4; matrix products, arithmetic and copies ran while one was open for 3% -> 4% of each run, Pallas kernels for 0% -> 0%
where the time goes in v3:
time: 239 us; the launch traced here: 236 us
  blocking collectives  145 us (61%)
  starting transfers between devices  46.9 us (20%)
  local copies, waits for them, and re-layouts  20.9 us (9%)
  matrix products  14.4 us (6%)
  waiting for transfers between devices  5.64 us (2%)
  other arithmetic  2.75 us (1%)
    all_gather x2, blocking collectives, coarse_partial(): g = lax.all_gather(g[None], ('y', 'core'), axis=0, tiled=True)  53.3 us
    all_gather x2, blocking collectives, coarse_partial(): g = lax.all_gather(mine[None], 'z', axis=0, tiled=True)  49 us
    ppermute x12, starting transfers between devices, passed_along(): return lax.ppermute(block, SUB, route)  46.9 us
    all_gather x2, blocking collectives, gathered_ext(): g = lax.all_gather(payload[None], 'col', axis=0, tiled=True)  22.5 us
    all_gather x1, blocking collectives, body(): lax.all_gather(jnp.concatenate([local_1, partial_1.T], axis=1)[None], 'co...  10.6 us
    all_gather x1, blocking collectives, body(): g2 = lax.all_gather(partial_2.T[None], 'col', axis=0, tiled=True)  9.43 us
    unnamed x27, local copies, waits for them, and re-layouts  8.88 us
    dot_general x5, matrix products, apply(): lax.dot_general(ext, blocks, (((0, 2), (0, 1)), ((), ())), precision=HIGH)  5.82 us
  transfers between devices with their start and end apart: 12, of which 4 were waited for; matrix products, arithmetic and copies ran while one was open for 4% of the time, Pallas kernels for 0%

profile of v3, /device:TPU:1, one launch (start us, length us, event | category | flops | bytes accessed | tf_op | source)
XLA Modules:
  0.0 236.4 jit_solution(14947691715766698563)
XLA Ops:
  5.1 10.9 %all-gather.8 = f32[4,65,384]{2,1,0:T(8,128)S(1)} all-gather(f32[1,65,384]{2,1,0:T(8,128)S(1)} %maximum_bitcast_fusion), channel_id=2, replica_groups=mesh['y'=8,'z'=12,'core'=2,'col'=4] {'col'}, dimensions={0}, use_global_device_ids=true | all-gather | bytes 499200 | tf_op jit(solution)/shard_map/all_gather | solution.py:66
  16.9 7.4 %collective-permute-start = (f32[4,64,32]{2,1,0:T(8,128)}, f32[4,64,32]{2,1,0:T(8,128)S(1)}, u32[]{:S(2)}, u32[]{:S(2)}) collective-permute-start(f32[4,64,32]{2,1,0:T(8,128)} %bitcast.4), channel_id=1, source_target_pairs={{0,4},{4,8},{8,12},{12,16},{16,20},{20,24},{24,28},{28,32},{32,36}... | collective-permute-start | bytes 98312 | tf_op jit(solution)/shard_map/ppermute | solution.py:14
  24.5 8.0 %collective-permute-start.1 = (f32[4,64,32]{2,1,0:T(8,128)S(1)}, f32[4,64,32]{2,1,0:T(8,128)S(1)}, u32[]{:S(2)}, u32[]{:S(2)}) collective-permute-start(f32[4,64,32]{2,1,0:T(8,128)S(1)} %bitcast.115), channel_id=1, source_target_pairs={{4,0},{8,4},{12,8},{16,12},{20,16},{24,20},{28,24},{32,28},{36,32}... | collective-permute-start | bytes 98312 | tf_op jit(solution)/shard_map/ppermute | solution.py:14
  33.2 1.3 collective-permute-start.2
  35.3 1.3 collective-permute-start.3
  39.5 2.7 %collective-permute-done.3 = f32[4,64,32]{2,1,0:T(8,128)} collective-permute-done((f32[4,64,32]{2,1,0:T(8,128)}, f32[4,64,32]{2,1,0:T(8,128)}, u32[]{:S(2)}, u32[]{:S(2)}) %collective-permute-start.3) | collective-permute-done | bytes 32800 | tf_op jit(solution)/shard_map/ppermute | solution.py:14
  42.2 1.2 concatenate.27
  43.9 27.1 %all-gather.1 = f32[192,64]{1,0:T(8,128)S(1)} all-gather(f32[16,64]{1,0:T(8,128)S(1)} %dynamic-slice_bitcast_fusion.1), channel_id=3, replica_groups=mesh['y'=8,'z'=12,'core'=2,'col'=4] {'z'}, dimensions={0}, use_global_device_ids=true | all-gather | bytes 53248 | tf_op jit(solution)/shard_map/all_gather | solution.py:74
  70.9 27.0 %all-gather.2 = f32[192,16,64]{2,1,0:T(8,128)S(1)} all-gather(f32[12,16,64]{2,1,0:T(8,128)S(1)} %bitcast.113), channel_id=4, replica_groups=mesh['y'=8,'z'=12,'core'=2,'col'=4] {'y','core'}, dimensions={0}, use_global_device_ids=true | all-gather | bytes 835584 | tf_op jit(solution)/shard_map/all_gather | solution.py:75
  99.3 2.6 %fusion.32 = f32[64,64]{1,0:T(8,128)S(1)} fusion(f32[3072,64]{1,0:T(8,128)S(1)} %bitcast.101, f32[64,3072]{1,0:T(8,128)S(1)} %copy-done.1), kind=kOutput, calls=%fused_computation.57 | convolution fusion | flops 150994944 | bytes 1589248 | tf_op jit(solution)/shard_map/dot_general | solution.py:78
  101.9 10.6 %all-gather.3 = f32[256,320]{1,0:T(8,128)S(1)} all-gather(f32[64,320]{1,0:T(8,128)S(1)} %pad_maximum_fusion), channel_id=5, replica_groups=mesh['y'=8,'z'=12,'core'=2,'col'=4] {'col'}, dimensions={0}, use_global_device_ids=true | all-gather | bytes 409600 | tf_op jit(solution)/shard_map/all_gather | solution.py:94
  114.3 1.3 collective-permute-start.7
  115.6 5.6 %collective-permute-start.6 = (f32[4,64,32]{2,1,0:T(8,128)S(1)}, f32[4,64,32]{2,1,0:T(8,128)}, u32[]{:S(2)}, u32[]{:S(2)}) collective-permute-start(f32[4,64,32]{2,1,0:T(8,128)S(1)} %fusion.9), channel_id=1, source_target_pairs={{0,192},{4,196},{8,200},{12,204},{16,208},{20,212},{24,216},{28,22... | collective-permute-start | bytes 98312 | tf_op jit(solution)/shard_map/ppermute | solution.py:14
  121.2 4.6 %collective-permute-start.5 = (f32[4,64,32]{2,1,0:T(8,128)S(1)}, f32[4,64,32]{2,1,0:T(8,128)}, u32[]{:S(2)}, u32[]{:S(2)}) collective-permute-start(f32[4,64,32]{2,1,0:T(8,128)S(1)} %fusion.10), channel_id=1, source_target_pairs={{4,0},{8,4},{12,8},{16,12},{20,16},{24,20},{28,24},{32,28},{36,32}... | collective-permute-start | bytes 98312 | tf_op jit(solution)/shard_map/ppermute | solution.py:14
  125.8 2.0 collective-permute-start.4
  129.7 2.0 concatenate.29
  131.7 2.4 %fusion.3 = f32[64,256]{1,0:T(8,128)S(1)} fusion(f32[64,256]{1,0:T(8,128)S(1)} %copy-done.6, f32[4,64,384]{2,1,0:T(8,128)} %concatenate.29, f32[4,384,256]{2,1,0:T(8,128)} %bitcast.107), kind=kOutput, calls=%fused_computation.6 | convolution fusion | flops 302006272 | bytes 2097152 | tf_op jit(solution)/shard_map/dot_general | solution.py:60
  134.4 11.6 %all-gather.4 = f32[256,384]{1,0:T(8,128)S(1)} all-gather(f32[64,384]{1,0:T(8,128)S(1)} %pad_maximum_fusion.1), channel_id=6, replica_groups=mesh['y'=8,'z'=12,'core'=2,'col'=4] {'col'}, dimensions={0}, use_global_device_ids=true | all-gather | bytes 491520 | tf_op jit(solution)/shard_map/all_gather | solution.py:66
  147.7 1.6 fusion.30
  149.2 1.6 copy.75
  150.8 3.2 %collective-permute-start.10 = (f32[4,64,32]{2,1,0:T(8,128)}, f32[4,64,32]{2,1,0:T(8,128)}, u32[]{:S(2)}, u32[]{:S(2)}) collective-permute-start(f32[4,64,32]{2,1,0:T(8,128)} %bitcast.116), channel_id=1, source_target_pairs={{0,192},{4,196},{8,200},{12,204},{16,208},{20,212},{24,216},{28,22... | collective-permute-start | bytes 98312 | tf_op jit(solution)/shard_map/ppermute | solution.py:14
  154.0 1.6 copy.76
  155.6 1.3 collective-permute-start.11
  157.7 6.9 %collective-permute-start.8 = (f32[4,64,32]{2,1,0:T(8,128)}, f32[4,64,32]{2,1,0:T(8,128)}, u32[]{:S(2)}, u32[]{:S(2)}) collective-permute-start(f32[4,64,32]{2,1,0:T(8,128)} %bitcast.118), channel_id=1, source_target_pairs={{0,4},{4,8},{8,12},{12,16},{16,20},{20,24},{24,28},{28,32},{32,36}... | collective-permute-start | bytes 98312 | tf_op jit(solution)/shard_map/ppermute | solution.py:14
  165.3 4.2 %collective-permute-start.9 = (f32[4,64,32]{2,1,0:T(8,128)}, f32[4,64,32]{2,1,0:T(8,128)S(1)}, u32[]{:S(2)}, u32[]{:S(2)}) collective-permute-start(f32[4,64,32]{2,1,0:T(8,128)} %bitcast.119), channel_id=1, source_target_pairs={{4,0},{8,4},{12,8},{16,12},{20,16},{24,20},{28,24},{32,28},{36,32}... | collective-permute-start | bytes 98312 | tf_op jit(solution)/shard_map/ppermute | solution.py:14
  169.5 1.7 slice.102
  172.2 1.3 concatenate.31
  174.0 22.0 %all-gather.5 = f32[192,64]{1,0:T(8,128)S(1)} all-gather(f32[16,64]{1,0:T(8,128)S(1)} %dynamic-slice_bitcast_fusion), channel_id=7, replica_groups=mesh['y'=8,'z'=12,'core'=2,'col'=4] {'z'}, dimensions={0}, use_global_device_ids=true | all-gather | bytes 53248 | tf_op jit(solution)/shard_map/all_gather | solution.py:74
  196.0 26.3 %all-gather.6 = f32[192,16,64]{2,1,0:T(8,128)S(1)} all-gather(f32[12,16,64]{2,1,0:T(8,128)S(1)} %bitcast.114), channel_id=8, replica_groups=mesh['y'=8,'z'=12,'core'=2,'col'=4] {'y','core'}, dimensions={0}, use_global_device_ids=true | all-gather | bytes 835584 | tf_op jit(solution)/shard_map/all_gather | solution.py:75
  222.5 2.6 %fusion.33 = f32[64,64]{1,0:T(8,128)S(1)} fusion(f32[3072,64]{1,0:T(8,128)S(1)} %bitcast.104, f32[64,3072]{1,0:T(8,128)S(1)} %copy-done.1), kind=kOutput, calls=%fused_computation.58 | convolution fusion | flops 150994944 | bytes 1589248 | tf_op jit(solution)/shard_map/dot_general | solution.py:78
  225.2 9.4 %all-gather.7 = f32[256,64]{1,0:T(8,128)S(1)} all-gather(f32[64,64]{1,0:T(8,128)S(1)} %fusion.33), channel_id=9, replica_groups=mesh['y'=8,'z'=12,'core'=2,'col'=4] {'col'}, dimensions={0}, use_global_device_ids=true | all-gather | bytes 81920 | tf_op jit(solution)/shard_map/all_gather | solution.py:122
  234.8 1.5 fusion.2
  (83 shorter events, 20.7 us)
Async XLA Ops:
  0.6 97.5 %copy-start = (f32[1,1536,256]{2,1,0:T(8,128)S(1)}, f32[1,1536,256]{2,1,0:T(8,128)}, u32[]{:S(2)}) copy-start(f32[1,1536,256]{2,1,0:T(8,128)} %param.9) | copy-start | bytes 4718596
  16.0 21.9 %copy-start.5 = (f32[1,1536,64]{1,2,0:T(8,128)S(1)}, f32[1,1536,64]{1,2,0:T(8,128)}, u32[]{:S(2)}) copy-start(f32[1,1536,64]{1,2,0:T(8,128)} %param.10) | copy-start | bytes 1179652
  16.9 21.9 %collective-permute-start = (f32[4,64,32]{2,1,0:T(8,128)}, f32[4,64,32]{2,1,0:T(8,128)S(1)}, u32[]{:S(2)}, u32[]{:S(2)}) collective-permute-start(f32[4,64,32]{2,1,0:T(8,128)} %bitcast.4), channel_id=1, source_target_pairs={{0,4},{4,8},{8,12},{12,16},{16,20},{20,24},{24,28},{28,32},{32,36}... | collective-permute-start | bytes 98312 | tf_op jit(solution)/shard_map/ppermute | solution.py:14
  24.5 14.3 %collective-permute-start.1 = (f32[4,64,32]{2,1,0:T(8,128)S(1)}, f32[4,64,32]{2,1,0:T(8,128)S(1)}, u32[]{:S(2)}, u32[]{:S(2)}) collective-permute-start(f32[4,64,32]{2,1,0:T(8,128)S(1)} %bitcast.115), channel_id=1, source_target_pairs={{4,0},{8,4},{12,8},{16,12},{20,16},{24,20},{28,24},{32,28},{36,32}... | collective-permute-start | bytes 98312 | tf_op jit(solution)/shard_map/ppermute | solution.py:14
  33.2 5.6 %collective-permute-start.2 = (f32[4,64,32]{2,1,0:T(8,128)}, f32[4,64,32]{2,1,0:T(8,128)S(1)}, u32[]{:S(2)}, u32[]{:S(2)}) collective-permute-start(f32[4,64,32]{2,1,0:T(8,128)} %bitcast.6), channel_id=1, source_target_pairs={{0,192},{4,196},{8,200},{12,204},{16,208},{20,212},{24,216},{28,22... | collective-permute-start | bytes 98312 | tf_op jit(solution)/shard_map/ppermute | solution.py:14
  35.3 6.9 %collective-permute-start.3 = (f32[4,64,32]{2,1,0:T(8,128)}, f32[4,64,32]{2,1,0:T(8,128)}, u32[]{:S(2)}, u32[]{:S(2)}) collective-permute-start(f32[4,64,32]{2,1,0:T(8,128)} %bitcast.7), channel_id=1, source_target_pairs={{192,0},{196,4},{200,8},{204,12},{208,16},{212,20},{216,24},{220,2... | collective-permute-start | bytes 98312 | tf_op jit(solution)/shard_map/ppermute | solution.py:14
  38.8 0.7 copy-start.8
  98.1 1.1 copy-start.1
  99.3 13.2 %copy-start.2 = (f32[4,384,64]{1,2,0:T(8,128)S(1)}, f32[4,384,64]{1,2,0:T(8,128)}, u32[]{:S(2)}) copy-start(f32[4,384,64]{1,2,0:T(8,128)} %copy.48) | copy-start | bytes 1179652
  99.3 13.6 %copy-start.3 = (f32[4,256,4,32]{1,3,0,2:T(8,128)S(1)}, f32[4,256,4,32]{1,3,0,2:T(8,128)}, u32[]{:S(2)}) copy-start(f32[4,256,4,32]{1,3,0,2:T(8,128)} %fusion.4) | copy-start | bytes 1572868
  112.9 18.8 %copy-start.6 = (f32[64,256]{1,0:T(8,128)S(1)}, f32[64,256]{1,0:T(8,128)}, u32[]{:S(2)}) copy-start(f32[64,256]{1,0:T(8,128)} %param.7) | copy-start | bytes 196612
  114.3 13.4 %collective-permute-start.7 = (f32[4,64,32]{2,1,0:T(8,128)S(1)}, f32[4,64,32]{2,1,0:T(8,128)}, u32[]{:S(2)}, u32[]{:S(2)}) collective-permute-start(f32[4,64,32]{2,1,0:T(8,128)S(1)} %fusion.8), channel_id=1, source_target_pairs={{192,0},{196,4},{200,8},{204,12},{208,16},{212,20},{216,24},{220,2... | collective-permute-start | bytes 98312 | tf_op jit(solution)/shard_map/ppermute | solution.py:14
  115.6 12.1 %collective-permute-start.6 = (f32[4,64,32]{2,1,0:T(8,128)S(1)}, f32[4,64,32]{2,1,0:T(8,128)}, u32[]{:S(2)}, u32[]{:S(2)}) collective-permute-start(f32[4,64,32]{2,1,0:T(8,128)S(1)} %fusion.9), channel_id=1, source_target_pairs={{0,192},{4,196},{8,200},{12,204},{16,208},{20,212},{24,216},{28,22... | collective-permute-start | bytes 98312 | tf_op jit(solution)/shard_map/ppermute | solution.py:14
  121.2 7.4 %collective-permute-start.5 = (f32[4,64,32]{2,1,0:T(8,128)S(1)}, f32[4,64,32]{2,1,0:T(8,128)}, u32[]{:S(2)}, u32[]{:S(2)}) collective-permute-start(f32[4,64,32]{2,1,0:T(8,128)S(1)} %fusion.10), channel_id=1, source_target_pairs={{4,0},{8,4},{12,8},{16,12},{20,16},{24,20},{28,24},{32,28},{36,32}... | collective-permute-start | bytes 98312 | tf_op jit(solution)/shard_map/ppermute | solution.py:14
  125.8 3.9 %collective-permute-start.4 = (f32[4,64,32]{2,1,0:T(8,128)S(1)}, f32[4,64,32]{2,1,0:T(8,128)}, u32[]{:S(2)}, u32[]{:S(2)}) collective-permute-start(f32[4,64,32]{2,1,0:T(8,128)S(1)} %fusion.11), channel_id=1, source_target_pairs={{0,4},{4,8},{8,12},{12,16},{16,20},{20,24},{24,28},{28,32},{32,36}... | collective-permute-start | bytes 98312 | tf_op jit(solution)/shard_map/ppermute | solution.py:14
  134.1 11.9 %copy-start.7 = (f32[64,256]{1,0:T(8,128)}, f32[64,256]{1,0:T(8,128)S(1)}, u32[]{:S(2)}) copy-start(f32[64,256]{1,0:T(8,128)S(1)} %fusion.3) | copy-start | bytes 196612
  146.0 0.8 copy-start.4
  150.8 20.4 %collective-permute-start.10 = (f32[4,64,32]{2,1,0:T(8,128)}, f32[4,64,32]{2,1,0:T(8,128)}, u32[]{:S(2)}, u32[]{:S(2)}) collective-permute-start(f32[4,64,32]{2,1,0:T(8,128)} %bitcast.116), channel_id=1, source_target_pairs={{0,192},{4,196},{8,200},{12,204},{16,208},{20,212},{24,216},{28,22... | collective-permute-start | bytes 98312 | tf_op jit(solution)/shard_map/ppermute | solution.py:14
  155.6 15.6 %collective-permute-start.11 = (f32[4,64,32]{2,1,0:T(8,128)}, f32[4,64,32]{2,1,0:T(8,128)}, u32[]{:S(2)}, u32[]{:S(2)}) collective-permute-start(f32[4,64,32]{2,1,0:T(8,128)} %bitcast.117), channel_id=1, source_target_pairs={{192,0},{196,4},{200,8},{204,12},{208,16},{212,20},{216,24},{220,2... | collective-permute-start | bytes 98312 | tf_op jit(solution)/shard_map/ppermute | solution.py:14
  157.7 13.6 %collective-permute-start.8 = (f32[4,64,32]{2,1,0:T(8,128)}, f32[4,64,32]{2,1,0:T(8,128)}, u32[]{:S(2)}, u32[]{:S(2)}) collective-permute-start(f32[4,64,32]{2,1,0:T(8,128)} %bitcast.118), channel_id=1, source_target_pairs={{0,4},{4,8},{8,12},{12,16},{16,20},{20,24},{24,28},{28,32},{32,36}... | collective-permute-start | bytes 98312 | tf_op jit(solution)/shard_map/ppermute | solution.py:14
  165.3 6.9 %collective-permute-start.9 = (f32[4,64,32]{2,1,0:T(8,128)}, f32[4,64,32]{2,1,0:T(8,128)S(1)}, u32[]{:S(2)}, u32[]{:S(2)}) collective-permute-start(f32[4,64,32]{2,1,0:T(8,128)} %bitcast.119), channel_id=1, source_target_pairs={{4,0},{8,4},{12,8},{16,12},{20,16},{24,20},{28,24},{32,28},{36,32}... | collective-permute-start | bytes 98312 | tf_op jit(solution)/shard_map/ppermute | solution.py:14
  222.5 12.1 %slice-start = ((f32[4,384,64]{1,2,0:T(8,128)}), f32[4,256,64]{1,2,0:T(8,128)S(1)}, s32[]{:S(2)}) async-start(f32[4,384,64]{1,2,0:T(8,128)} %copy.48), calls=%async_computation | async-start | bytes 524288 | tf_op jit(solution)/shard_map/slice | solution.py:40

commit v4 on v3

--- a/solution.py
+++ b/solution.py
@@ -71,7 +71,8 @@
     def coarse_partial(ext):
         coeff = apply(ext, basis_blocks)
         mine = lax.dynamic_slice_in_dim(coeff, column_index * quarter, quarter, 1).T
-        g = lax.all_gather(mine[None], "z", axis=0, tiled=True)
+        spread = jnp.broadcast_to(mine[None], (ZLEN,) + mine.shape)
+        g = lax.all_to_all(spread, "z", 0, 0, tiled=True)
         g = lax.all_gather(g[None], ("y", "core"), axis=0, tiled=True)
         g = g.reshape(ylen, CORES, ZLEN, quarter, rhs_width).transpose(0, 2, 1, 3, 4)
         kept_rows = g.reshape(subs * quarter, rhs_width)

time: 239 us -> 229 us (0.958)
  blocking collectives: 145 us -> 88 us
  starting transfers between devices: 46.9 us -> 71.9 us
  waiting for transfers between devices: 5.64 us -> 24.3 us
    all_gather x2 -> x0, blocking collectives: 49 us -> none  [coarse_partial(): g = lax.all_gather(mine[None], 'z', axis=0, tiled=True)]
    all_to_all x0 -> x2, starting transfers between devices: none -> 24.8 us  [coarse_partial(): g = lax.all_to_all(spread, 'z', 0, 0, tiled=True)]
    all_to_all x0 -> x2, waiting for transfers between devices: none -> 18.5 us  [coarse_partial(): g = lax.all_to_all(spread, 'z', 0, 0, tiled=True)]
    all_gather x2, blocking collectives: 53.3 us -> 45.9 us  [coarse_partial(): g = lax.all_gather(g[None], ('y', 'core'), axis=0, tiled=True)]
    unnamed x27 -> x37, local copies, waits for them, and re-layouts: 8.88 us -> 12.4 us
  transfers between devices with their start and end apart: 12 -> 14, of which waited for: 4 -> 6; matrix products, arithmetic and copies ran while one was open for 4% -> 4% of each run, Pallas kernels for 0% -> 0%
where the time goes in v4:
time: 229 us; the launch traced here: 227 us
  blocking collectives  88 us (38%)
  starting transfers between devices  71.9 us (31%)
  waiting for transfers between devices  24.3 us (11%)
  local copies, waits for them, and re-layouts  22.6 us (10%)
  matrix products  14.2 us (6%)
  other arithmetic  4.34 us (2%)
    ppermute x12, starting transfers between devices, passed_along(): return lax.ppermute(block, SUB, route)  47 us
    all_gather x2, blocking collectives, coarse_partial(): g = lax.all_gather(g[None], ('y', 'core'), axis=0, tiled=True)  45.9 us
    all_to_all x2, starting transfers between devices, coarse_partial(): g = lax.all_to_all(spread, 'z', 0, 0, tiled=True)  24.8 us
    all_gather x2, blocking collectives, gathered_ext(): g = lax.all_gather(payload[None], 'col', axis=0, tiled=True)  22.2 us
    all_to_all x2, waiting for transfers between devices, coarse_partial(): g = lax.all_to_all(spread, 'z', 0, 0, tiled=True)  18.5 us
    unnamed x37, local copies, waits for them, and re-layouts  12.4 us
    all_gather x1, blocking collectives, body(): lax.all_gather(jnp.concatenate([local_1, partial_1.T], axis=1)[None], 'co...  10.6 us
    all_gather x1, blocking collectives, body(): g2 = lax.all_gather(partial_2.T[None], 'col', axis=0, tiled=True)  9.42 us
  transfers between devices with their start and end apart: 14, of which 6 were waited for; matrix products, arithmetic and copies ran while one was open for 4% of the time, Pallas kernels for 0%

profile of v4, /device:TPU:1, one launch (start us, length us, event | category | flops | bytes accessed | tf_op | source)
XLA Modules:
  0.0 226.5 jit_solution(15976882838855029114)
XLA Ops:
  5.1 10.9 %all-gather.6 = f32[4,65,384]{2,1,0:T(8,128)S(1)} all-gather(f32[1,65,384]{2,1,0:T(8,128)S(1)} %maximum_bitcast_fusion), channel_id=2, replica_groups=mesh['y'=8,'z'=12,'core'=2,'col'=4] {'col'}, dimensions={0}, use_global_device_ids=true | all-gather | bytes 499200 | tf_op jit(solution)/shard_map/all_gather | solution.py:66
  16.9 7.4 %collective-permute-start = (f32[4,64,32]{2,1,0:T(8,128)}, f32[4,64,32]{2,1,0:T(8,128)S(1)}, u32[]{:S(2)}, u32[]{:S(2)}) collective-permute-start(f32[4,64,32]{2,1,0:T(8,128)} %bitcast.4), channel_id=1, source_target_pairs={{0,4},{4,8},{8,12},{12,16},{16,20},{20,24},{24,28},{28,32},{32,36}... | collective-permute-start | bytes 98312 | tf_op jit(solution)/shard_map/ppermute | solution.py:14
  25.1 7.9 %collective-permute-start.1 = (f32[4,64,32]{2,1,0:T(8,128)}, f32[4,64,32]{2,1,0:T(8,128)S(1)}, u32[]{:S(2)}, u32[]{:S(2)}) collective-permute-start(f32[4,64,32]{2,1,0:T(8,128)} %bitcast.5), channel_id=1, source_target_pairs={{4,0},{8,4},{12,8},{16,12},{20,16},{24,20},{28,24},{32,28},{36,32}... | collective-permute-start | bytes 98312 | tf_op jit(solution)/shard_map/ppermute | solution.py:14
  33.8 1.3 collective-permute-start.2
  35.9 1.3 collective-permute-start.3
  40.1 2.7 %collective-permute-done.3 = f32[4,64,32]{2,1,0:T(8,128)} collective-permute-done((f32[4,64,32]{2,1,0:T(8,128)}, f32[4,64,32]{2,1,0:T(8,128)}, u32[]{:S(2)}, u32[]{:S(2)}) %collective-permute-start.3) | collective-permute-done | bytes 32800 | tf_op jit(solution)/shard_map/ppermute | solution.py:14
  45.3 16.3 %all-to-all-start = ((f32[12,1,1024]{2,1,0:T(1,128)}), f32[12,1,1024]{2,1,0:T(1,128)S(1)}, u32[]{:S(2)}, u32[]{:S(2)}) async-start(f32[12,1,1024]{2,1,0:T(1,128)} %reshape.99), calls=%async_computation | async-start | bytes 98304 | tf_op jit(solution)/shard_map/all_to_all | solution.py:75
  62.5 8.8 %all-to-all-done = f32[12,1,1024]{2,1,0:T(1,128)S(1)} async-done(((f32[12,1,1024]{2,1,0:T(1,128)}), f32[12,1,1024]{2,1,0:T(1,128)S(1)}, u32[]{:S(2)}, u32[]{:S(2)}) %all-to-all-start) | async-done | bytes 49184 | tf_op jit(solution)/shard_map/all_to_all | solution.py:75
  72.8 22.3 %all-gather.1 = f32[192,16,64]{2,1,0:T(8,128)S(1)} all-gather(f32[12,16,64]{2,1,0:T(8,128)S(1)} %reshape.100), channel_id=3, replica_groups=mesh['y'=8,'z'=12,'core'=2,'col'=4] {'y','core'}, dimensions={0}, use_global_device_ids=true | all-gather | bytes 835584 | tf_op jit(solution)/shard_map/all_gather | solution.py:76
  96.2 2.6 %fusion.32 = f32[64,64]{1,0:T(8,128)S(1)} fusion(f32[3072,64]{1,0:T(8,128)S(1)} %bitcast.100, f32[64,3072]{1,0:T(8,128)S(1)} %copy-done.1), kind=kOutput, calls=%fused_computation.57 | convolution fusion | flops 150994944 | bytes 1589248 | tf_op jit(solution)/shard_map/dot_general | solution.py:79
  98.9 10.6 %all-gather.2 = f32[256,320]{1,0:T(8,128)S(1)} all-gather(f32[64,320]{1,0:T(8,128)S(1)} %pad_maximum_fusion), channel_id=4, replica_groups=mesh['y'=8,'z'=12,'core'=2,'col'=4] {'col'}, dimensions={0}, use_global_device_ids=true | all-gather | bytes 409600 | tf_op jit(solution)/shard_map/all_gather | solution.py:95
  111.3 1.3 collective-permute-start.7
  112.6 4.9 %collective-permute-start.6 = (f32[4,64,32]{2,1,0:T(8,128)S(1)}, f32[4,64,32]{2,1,0:T(8,128)S(1)}, u32[]{:S(2)}, u32[]{:S(2)}) collective-permute-start(f32[4,64,32]{2,1,0:T(8,128)S(1)} %fusion.9), channel_id=1, source_target_pairs={{0,192},{4,196},{8,200},{12,204},{16,208},{20,212},{24,216},{28,22... | collective-permute-start | bytes 98312 | tf_op jit(solution)/shard_map/ppermute | solution.py:14
  117.5 4.6 %collective-permute-start.5 = (f32[4,64,32]{2,1,0:T(8,128)S(1)}, f32[4,64,32]{2,1,0:T(8,128)S(1)}, u32[]{:S(2)}, u32[]{:S(2)}) collective-permute-start(f32[4,64,32]{2,1,0:T(8,128)S(1)} %fusion.10), channel_id=1, source_target_pairs={{4,0},{8,4},{12,8},{16,12},{20,16},{24,20},{28,24},{32,28},{36,32}... | collective-permute-start | bytes 98312 | tf_op jit(solution)/shard_map/ppermute | solution.py:14
  122.1 2.1 collective-permute-start.4
  126.1 1.3 concatenate.29
  127.4 2.3 %fusion.3 = f32[64,256]{1,0:T(8,128)S(1)} fusion(f32[64,256]{1,0:T(8,128)S(1)} %copy-done.5, f32[4,64,384]{2,1,0:T(8,128)S(1)} %concatenate.29, f32[4,384,256]{2,1,0:T(8,128)} %bitcast.105), kind=kOutput, calls=%fused_computation.6 | convolution fusion | flops 302006272 | bytes 2097152 | tf_op jit(solution)/shard_map/dot_general | solution.py:60
  130.0 11.3 %all-gather.3 = f32[256,384]{1,0:T(8,128)S(1)} all-gather(f32[64,384]{1,0:T(8,128)S(1)} %pad_maximum_fusion.1), channel_id=5, replica_groups=mesh['y'=8,'z'=12,'core'=2,'col'=4] {'col'}, dimensions={0}, use_global_device_ids=true | all-gather | bytes 491520 | tf_op jit(solution)/shard_map/all_gather | solution.py:66
  142.1 1.6 fusion.30
  143.7 1.6 copy.75
  145.3 3.9 %collective-permute-start.10 = (f32[4,64,32]{2,1,0:T(8,128)}, f32[4,64,32]{2,1,0:T(8,128)}, u32[]{:S(2)}, u32[]{:S(2)}) collective-permute-start(f32[4,64,32]{2,1,0:T(8,128)} %bitcast.111), channel_id=1, source_target_pairs={{0,192},{4,196},{8,200},{12,204},{16,208},{20,212},{24,216},{28,22... | collective-permute-start | bytes 98312 | tf_op jit(solution)/shard_map/ppermute | solution.py:14
  149.2 1.6 copy.76
  152.8 7.2 %collective-permute-start.8 = (f32[4,64,32]{2,1,0:T(8,128)}, f32[4,64,32]{2,1,0:T(8,128)}, u32[]{:S(2)}, u32[]{:S(2)}) collective-permute-start(f32[4,64,32]{2,1,0:T(8,128)} %bitcast.113), channel_id=1, source_target_pairs={{0,4},{4,8},{8,12},{12,16},{16,20},{20,24},{24,28},{28,32},{32,36}... | collective-permute-start | bytes 98312 | tf_op jit(solution)/shard_map/ppermute | solution.py:14
  160.8 3.8 %collective-permute-start.9 = (f32[4,64,32]{2,1,0:T(8,128)}, f32[4,64,32]{2,1,0:T(8,128)S(1)}, u32[]{:S(2)}, u32[]{:S(2)}) collective-permute-start(f32[4,64,32]{2,1,0:T(8,128)} %bitcast.114), channel_id=1, source_target_pairs={{4,0},{8,4},{12,8},{16,12},{20,16},{24,20},{28,24},{32,28},{36,32}... | collective-permute-start | bytes 98312 | tf_op jit(solution)/shard_map/ppermute | solution.py:14
  165.4 1.9 collective-permute-done.9
  167.3 1.3 concatenate.31
  169.8 8.5 %all-to-all-start.1 = ((f32[12,1,1024]{2,1,0:T(1,128)}), f32[12,1,1024]{2,1,0:T(1,128)S(1)}, u32[]{:S(2)}, u32[]{:S(2)}) async-start(f32[12,1,1024]{2,1,0:T(1,128)} %reshape.101), calls=%async_computation.1 | async-start | bytes 98304 | tf_op jit(solution)/shard_map/all_to_all | solution.py:75
  178.4 9.7 %all-to-all-done.1 = f32[12,1,1024]{2,1,0:T(1,128)S(1)} async-done(((f32[12,1,1024]{2,1,0:T(1,128)}), f32[12,1,1024]{2,1,0:T(1,128)S(1)}, u32[]{:S(2)}, u32[]{:S(2)}) %all-to-all-start.1) | async-done | bytes 49184 | tf_op jit(solution)/shard_map/all_to_all | solution.py:75
  188.9 23.5 %all-gather.4 = f32[192,16,64]{2,1,0:T(8,128)S(1)} all-gather(f32[12,16,64]{2,1,0:T(8,128)S(1)} %reshape.102), channel_id=6, replica_groups=mesh['y'=8,'z'=12,'core'=2,'col'=4] {'y','core'}, dimensions={0}, use_global_device_ids=true | all-gather | bytes 835584 | tf_op jit(solution)/shard_map/all_gather | solution.py:76
  212.7 2.6 %fusion.33 = f32[64,64]{1,0:T(8,128)S(1)} fusion(f32[3072,64]{1,0:T(8,128)S(1)} %bitcast.102, f32[64,3072]{1,0:T(8,128)S(1)} %copy-done.1), kind=kOutput, calls=%fused_computation.58 | convolution fusion | flops 150994944 | bytes 1589248 | tf_op jit(solution)/shard_map/dot_general | solution.py:79
  215.3 9.4 %all-gather.5 = f32[256,64]{1,0:T(8,128)S(1)} all-gather(f32[64,64]{1,0:T(8,128)S(1)} %fusion.33), channel_id=7, replica_groups=mesh['y'=8,'z'=12,'core'=2,'col'=4] {'col'}, dimensions={0}, use_global_device_ids=true | all-gather | bytes 81920 | tf_op jit(solution)/shard_map/all_gather | solution.py:123
  225.0 1.5 fusion.2
  (100 shorter events, 27.2 us)
Async XLA Ops:
  0.6 61.0 %copy-start = (f32[1,1536,256]{2,1,0:T(8,128)S(1)}, f32[1,1536,256]{2,1,0:T(8,128)}, u32[]{:S(2)}) copy-start(f32[1,1536,256]{2,1,0:T(8,128)} %param.9) | copy-start | bytes 4718596
  16.0 22.5 %copy-start.4 = (f32[1,1536,64]{1,2,0:T(8,128)S(1)}, f32[1,1536,64]{1,2,0:T(8,128)}, u32[]{:S(2)}) copy-start(f32[1,1536,64]{1,2,0:T(8,128)} %param.10) | copy-start | bytes 1179652
  16.9 21.8 %collective-permute-start = (f32[4,64,32]{2,1,0:T(8,128)}, f32[4,64,32]{2,1,0:T(8,128)S(1)}, u32[]{:S(2)}, u32[]{:S(2)}) collective-permute-start(f32[4,64,32]{2,1,0:T(8,128)} %bitcast.4), channel_id=1, source_target_pairs={{0,4},{4,8},{8,12},{12,16},{16,20},{20,24},{24,28},{28,32},{32,36}... | collective-permute-start | bytes 98312 | tf_op jit(solution)/shard_map/ppermute | solution.py:14
  25.1 13.6 %collective-permute-start.1 = (f32[4,64,32]{2,1,0:T(8,128)}, f32[4,64,32]{2,1,0:T(8,128)S(1)}, u32[]{:S(2)}, u32[]{:S(2)}) collective-permute-start(f32[4,64,32]{2,1,0:T(8,128)} %bitcast.5), channel_id=1, source_target_pairs={{4,0},{8,4},{12,8},{16,12},{20,16},{24,20},{28,24},{32,28},{36,32}... | collective-permute-start | bytes 98312 | tf_op jit(solution)/shard_map/ppermute | solution.py:14
  33.8 4.9 %collective-permute-start.2 = (f32[4,64,32]{2,1,0:T(8,128)}, f32[4,64,32]{2,1,0:T(8,128)S(1)}, u32[]{:S(2)}, u32[]{:S(2)}) collective-permute-start(f32[4,64,32]{2,1,0:T(8,128)} %bitcast.6), channel_id=1, source_target_pairs={{0,192},{4,196},{8,200},{12,204},{16,208},{20,212},{24,216},{28,22... | collective-permute-start | bytes 98312 | tf_op jit(solution)/shard_map/ppermute | solution.py:14
  35.9 6.9 %collective-permute-start.3 = (f32[4,64,32]{2,1,0:T(8,128)}, f32[4,64,32]{2,1,0:T(8,128)}, u32[]{:S(2)}, u32[]{:S(2)}) collective-permute-start(f32[4,64,32]{2,1,0:T(8,128)} %bitcast.7), channel_id=1, source_target_pairs={{192,0},{196,4},{200,8},{204,12},{208,16},{212,20},{216,24},{220,2... | collective-permute-start | bytes 98312 | tf_op jit(solution)/shard_map/ppermute | solution.py:14
  38.7 70.8 %copy-start.2 = (f32[4,384,64]{1,2,0:T(8,128)}, f32[4,384,64]{1,2,0:T(8,128)S(1)}, u32[]{:S(2)}) copy-start(f32[4,384,64]{1,2,0:T(8,128)S(1)} %copy.48) | copy-start | bytes 1179652
  38.7 0.7 copy-start.7
  39.4 0.6 copy-start.8
  45.3 26.0 %all-to-all-start = ((f32[12,1,1024]{2,1,0:T(1,128)}), f32[12,1,1024]{2,1,0:T(1,128)S(1)}, u32[]{:S(2)}, u32[]{:S(2)}) async-start(f32[12,1,1024]{2,1,0:T(1,128)} %reshape.99), calls=%async_computation | async-start | bytes 98304 | tf_op jit(solution)/shard_map/all_to_all | solution.py:75
  95.1 1.1 copy-start.1
  96.2 13.6 %copy-start.3 = (f32[4,256,4,32]{1,3,0,2:T(8,128)S(1)}, f32[4,256,4,32]{1,3,0,2:T(8,128)}, u32[]{:S(2)}) copy-start(f32[4,256,4,32]{1,3,0,2:T(8,128)} %fusion.4) | copy-start | bytes 1572868
  109.9 17.5 %copy-start.5 = (f32[64,256]{1,0:T(8,128)S(1)}, f32[64,256]{1,0:T(8,128)}, u32[]{:S(2)}) copy-start(f32[64,256]{1,0:T(8,128)} %param.7) | copy-start | bytes 196612
  111.3 12.9 %collective-permute-start.7 = (f32[4,64,32]{2,1,0:T(8,128)S(1)}, f32[4,64,32]{2,1,0:T(8,128)S(1)}, u32[]{:S(2)}, u32[]{:S(2)}) collective-permute-start(f32[4,64,32]{2,1,0:T(8,128)S(1)} %fusion.8), channel_id=1, source_target_pairs={{192,0},{196,4},{200,8},{204,12},{208,16},{212,20},{216,24},{220,2... | collective-permute-start | bytes 98312 | tf_op jit(solution)/shard_map/ppermute | solution.py:14
  112.6 11.6 %collective-permute-start.6 = (f32[4,64,32]{2,1,0:T(8,128)S(1)}, f32[4,64,32]{2,1,0:T(8,128)S(1)}, u32[]{:S(2)}, u32[]{:S(2)}) collective-permute-start(f32[4,64,32]{2,1,0:T(8,128)S(1)} %fusion.9), channel_id=1, source_target_pairs={{0,192},{4,196},{8,200},{12,204},{16,208},{20,212},{24,216},{28,22... | collective-permute-start | bytes 98312 | tf_op jit(solution)/shard_map/ppermute | solution.py:14
  117.5 7.4 %collective-permute-start.5 = (f32[4,64,32]{2,1,0:T(8,128)S(1)}, f32[4,64,32]{2,1,0:T(8,128)S(1)}, u32[]{:S(2)}, u32[]{:S(2)}) collective-permute-start(f32[4,64,32]{2,1,0:T(8,128)S(1)} %fusion.10), channel_id=1, source_target_pairs={{4,0},{8,4},{12,8},{16,12},{20,16},{24,20},{28,24},{32,28},{36,32}... | collective-permute-start | bytes 98312 | tf_op jit(solution)/shard_map/ppermute | solution.py:14
  122.1 4.0 %collective-permute-start.4 = (f32[4,64,32]{2,1,0:T(8,128)S(1)}, f32[4,64,32]{2,1,0:T(8,128)}, u32[]{:S(2)}, u32[]{:S(2)}) collective-permute-start(f32[4,64,32]{2,1,0:T(8,128)S(1)} %fusion.11), channel_id=1, source_target_pairs={{0,4},{4,8},{8,12},{12,16},{16,20},{20,24},{24,28},{28,32},{32,36}... | collective-permute-start | bytes 98312 | tf_op jit(solution)/shard_map/ppermute | solution.py:14
  124.2 0.7 copy-start.9
  124.2 0.7 copy-start.10
  124.9 0.6 copy-start.11
  129.7 11.5 %copy-start.6 = (f32[64,256]{1,0:T(8,128)}, f32[64,256]{1,0:T(8,128)S(1)}, u32[]{:S(2)}) copy-start(f32[64,256]{1,0:T(8,128)S(1)} %fusion.3) | copy-start | bytes 196612
  145.3 20.1 %collective-permute-start.10 = (f32[4,64,32]{2,1,0:T(8,128)}, f32[4,64,32]{2,1,0:T(8,128)}, u32[]{:S(2)}, u32[]{:S(2)}) collective-permute-start(f32[4,64,32]{2,1,0:T(8,128)} %bitcast.111), channel_id=1, source_target_pairs={{0,192},{4,196},{8,200},{12,204},{16,208},{20,212},{24,216},{28,22... | collective-permute-start | bytes 98312 | tf_op jit(solution)/shard_map/ppermute | solution.py:14
  150.8 14.6 %collective-permute-start.11 = (f32[4,64,32]{2,1,0:T(8,128)}, f32[4,64,32]{2,1,0:T(8,128)}, u32[]{:S(2)}, u32[]{:S(2)}) collective-permute-start(f32[4,64,32]{2,1,0:T(8,128)} %bitcast.112), channel_id=1, source_target_pairs={{192,0},{196,4},{200,8},{204,12},{208,16},{212,20},{216,24},{220,2... | collective-permute-start | bytes 98312 | tf_op jit(solution)/shard_map/ppermute | solution.py:14
  152.8 12.6 %collective-permute-start.8 = (f32[4,64,32]{2,1,0:T(8,128)}, f32[4,64,32]{2,1,0:T(8,128)}, u32[]{:S(2)}, u32[]{:S(2)}) collective-permute-start(f32[4,64,32]{2,1,0:T(8,128)} %bitcast.113), channel_id=1, source_target_pairs={{0,4},{4,8},{8,12},{12,16},{16,20},{20,24},{24,28},{28,32},{32,36}... | collective-permute-start | bytes 98312 | tf_op jit(solution)/shard_map/ppermute | solution.py:14
  160.8 6.5 %collective-permute-start.9 = (f32[4,64,32]{2,1,0:T(8,128)}, f32[4,64,32]{2,1,0:T(8,128)S(1)}, u32[]{:S(2)}, u32[]{:S(2)}) collective-permute-start(f32[4,64,32]{2,1,0:T(8,128)} %bitcast.114), channel_id=1, source_target_pairs={{4,0},{8,4},{12,8},{16,12},{20,16},{24,20},{28,24},{32,28},{36,32}... | collective-permute-start | bytes 98312 | tf_op jit(solution)/shard_map/ppermute | solution.py:14
  169.8 18.2 %all-to-all-start.1 = ((f32[12,1,1024]{2,1,0:T(1,128)}), f32[12,1,1024]{2,1,0:T(1,128)S(1)}, u32[]{:S(2)}, u32[]{:S(2)}) async-start(f32[12,1,1024]{2,1,0:T(1,128)} %reshape.101), calls=%async_computation.1 | async-start | bytes 98304 | tf_op jit(solution)/shard_map/all_to_all | solution.py:75
  212.7 12.1 %slice-start = ((f32[4,384,64]{1,2,0:T(8,128)}), f32[4,256,64]{1,2,0:T(8,128)S(1)}, s32[]{:S(2)}) async-start(f32[4,384,64]{1,2,0:T(8,128)} %copy-done.2), calls=%async_computation.2 | async-start | bytes 524288 | tf_op jit(solution)/shard_map/slice | solution.py:40

commit v5 on v4

--- a/solution.py
+++ b/solution.py
@@ -34,7 +34,6 @@
     mode_count = basis_rows.shape[1]
     block_len = basis_rows.shape[0] // n_col
     blocks_of = lambda m: m.reshape(n_col, block_len, m.shape[-1])
-    operator_rows = blocks_of(operator[0])
     inverse_rows = blocks_of(local_inverse[0])
     basis_blocks = blocks_of(basis_rows)
     own_basis_all = basis_blocks[:, :own_width]
@@ -66,7 +65,7 @@
         g = lax.all_gather(payload[None], "col", axis=0, tiled=True)
         own_all = g[:, :rhs_width, :own_width]
         packs = g[:, :rhs_width, own_width:].reshape(n_col, rhs_width, n_nb, halo_slots)
-        return ext_of(own_all, halos(packs)), g[:, rhs_width:]
+        return ext_of(own_all, halos(packs)), g[:, rhs_width:], own_all
 
     def coarse_partial(ext):
         coeff = apply(ext, basis_blocks)
@@ -85,7 +84,11 @@
             jnp.zeros((own_width + n_nb * halo_slots - n_nb * halo_slots - n_nb,), jnp.float32),
         ]
     )[None]
-    ext_b, idx = gathered_ext(right_sides, index_row)
+    operator_rel = [operator[0]] + [
+        lax.ppermute(operator[0], "col", [(i, (i + k) % n_col) for i in range(n_col)])
+        for k in range(1, n_col)
+    ]
+    ext_b, idx, own_b_all = gathered_ext(right_sides, index_row)
     send_all = idx[:, 0, : n_nb * halo_slots].astype(jnp.int32).reshape(n_col, n_nb, halo_slots)
     counts_all = idx[:, 0, n_nb * halo_slots : n_nb * halo_slots + n_nb].astype(jnp.int32)
     live_all = (slots[None, None, :] < counts_all[:, :, None]).astype(jnp.float32)
@@ -113,11 +116,23 @@
         for n in range(n_nb)
     ]
     ext_f = ext_of(first_all, got_first)
-    applied = apply(ext_f, operator_rows)
-    residual = right_sides - applied
+    applied_rel = jnp.stack([apply(ext_f, blocks_of(m)) for m in operator_rel])
+    residual = right_sides - applied_rel[0]
+    back = (column_index - jnp.arange(n_col, dtype=jnp.int32)) % n_col
+    residual_all = own_b_all - jnp.take(applied_rel, back, axis=0)
     first_pass = lax.dynamic_index_in_dim(first_all, column_index, 0, keepdims=False)
 
-    ext_r, _ = gathered_ext(residual)
+    got_res = [
+        passed_along(
+            lax.dot_general(
+                residual_all, select_all[:, :, n], (((2,), (1,)), ((0,), (0,))), precision=HIGH
+            ),
+            offsets[n],
+            subs,
+        )
+        for n in range(n_nb)
+    ]
+    ext_r = ext_of(residual_all, got_res)
     local_2 = apply(ext_r, inverse_rows)
     partial_2 = coarse_partial(ext_r)
     g2 = lax.all_gather(partial_2.T[None], "col", axis=0, tiled=True)

time: 229 us -> 242 us (1.057)
  matrix products: 14.2 us -> 23 us
  starting transfers between devices: 71.9 us -> 80.1 us
  local copies, waits for them, and re-layouts: 22.6 us -> 16.9 us
  blocking collectives: 88 us -> 91 us
    all_gather x2 -> x1, blocking collectives: 22.2 us -> 10.9 us  [gathered_ext(): g = lax.all_gather(payload[None], 'col', axis=0, tiled=True)]
    all_gather x1, blocking collectives: 10.6 us -> 19.4 us  [body(): lax.all_gather(jnp.concatenate([local_1, partial_1.T], axis=1)[None], 'co...]
    ppermute x0 -> x3, starting transfers between devices: none -> 7.78 us  [body(): lax.ppermute(operator[0], 'col', [(i, (i + k) % n_col) for i in range(n_c...]
    dot_general x5 -> x8, matrix products: 5.7 us -> 13.3 us  [apply(): lax.dot_general(ext, blocks, (((0, 2), (0, 1)), ((), ())), precision=HIGH)]
    all_gather x2, blocking collectives: 45.9 us -> 51.5 us  [coarse_partial(): g = lax.all_gather(g[None], ('y', 'core'), axis=0, tiled=True)]
    ppermute x12, starting transfers between devices: 47 us -> 51.8 us  [passed_along(): return lax.ppermute(block, SUB, route)]
    unnamed x37 -> x29, local copies, waits for them, and re-layouts: 12.4 us -> 7.95 us
    all_to_all x2, starting transfers between devices: 24.8 us -> 20.6 us  [coarse_partial(): g = lax.all_to_all(spread, 'z', 0, 0, tiled=True)]
  transfers between devices with their start and end apart: 14 -> 17, of which waited for: 6 -> 6; matrix products, arithmetic and copies ran while one was open for 4% -> 9% of each run, Pallas kernels for 0% -> 0%
where the time goes in v5:
time: 242 us; the launch traced here: 240 us
  blocking collectives  91 us (38%)
  starting transfers between devices  80.1 us (33%)
  waiting for transfers between devices  23.6 us (10%)
  matrix products  23 us (10%)
  local copies, waits for them, and re-layouts  16.9 us (7%)
  other arithmetic  4.58 us (2%)
    ppermute x12, starting transfers between devices, passed_along(): return lax.ppermute(block, SUB, route)  51.8 us
    all_gather x2, blocking collectives, coarse_partial(): g = lax.all_gather(g[None], ('y', 'core'), axis=0, tiled=True)  51.5 us
    all_to_all x2, starting transfers between devices, coarse_partial(): g = lax.all_to_all(spread, 'z', 0, 0, tiled=True)  20.6 us
    all_gather x1, blocking collectives, body(): lax.all_gather(jnp.concatenate([local_1, partial_1.T], axis=1)[None], 'co...  19.4 us
    all_to_all x2, waiting for transfers between devices, coarse_partial(): g = lax.all_to_all(spread, 'z', 0, 0, tiled=True)  18.4 us
    dot_general x8, matrix products, apply(): lax.dot_general(ext, blocks, (((0, 2), (0, 1)), ((), ())), precision=HIGH)  13.3 us
    all_gather x1, blocking collectives, gathered_ext(): g = lax.all_gather(payload[None], 'col', axis=0, tiled=True)  10.9 us
    all_gather x1, blocking collectives, body(): g2 = lax.all_gather(partial_2.T[None], 'col', axis=0, tiled=True)  9.11 us
  transfers between devices with their start and end apart: 17, of which 6 were waited for; matrix products, arithmetic and copies ran while one was open for 9% of the time, Pallas kernels for 0%

profile of v5, /device:TPU:1, one launch (start us, length us, event | category | flops | bytes accessed | tf_op | source)
XLA Modules:
  0.0 240.3 jit_solution(1535756032649898278)
XLA Ops:
  5.1 10.9 %all-gather.5 = f32[4,65,384]{2,1,0:T(8,128)S(1)} all-gather(f32[1,65,384]{2,1,0:T(8,128)S(1)} %maximum_bitcast_fusion), channel_id=2, replica_groups=mesh['y'=8,'z'=12,'core'=2,'col'=4] {'col'}, dimensions={0}, use_global_device_ids=true | all-gather | bytes 499200 | tf_op jit(solution)/shard_map/all_gather | solution.py:65
  16.9 7.4 %collective-permute-start = (f32[4,64,32]{2,1,0:T(8,128)}, f32[4,64,32]{2,1,0:T(8,128)}, u32[]{:S(2)}, u32[]{:S(2)}) collective-permute-start(f32[4,64,32]{2,1,0:T(8,128)} %bitcast.4), channel_id=1, source_target_pairs={{0,4},{4,8},{8,12},{12,16},{16,20},{20,24},{24,28},{28,32},{32,36}... | collective-permute-start | bytes 98312 | tf_op jit(solution)/shard_map/ppermute | solution.py:14
  25.1 8.6 %collective-permute-start.1 = (f32[4,64,32]{2,1,0:T(8,128)}, f32[4,64,32]{2,1,0:T(8,128)}, u32[]{:S(2)}, u32[]{:S(2)}) collective-permute-start(f32[4,64,32]{2,1,0:T(8,128)} %bitcast.5), channel_id=1, source_target_pairs={{4,0},{8,4},{12,8},{16,12},{20,16},{24,20},{28,24},{32,28},{36,32}... | collective-permute-start | bytes 98312 | tf_op jit(solution)/shard_map/ppermute | solution.py:14
  34.5 1.9 collective-permute-start.2
  38.5 1.9 collective-permute-start.10
  41.9 3.1 %collective-permute-start.9 = (f32[1536,256]{1,0:T(8,128)}, f32[1536,256]{1,0:T(8,128)}, u32[]{:S(2)}, u32[]{:S(2)}) collective-permute-start(f32[1536,256]{1,0:T(8,128)} %bitcast.127), channel_id=1, source_target_pairs={{0,2},{1,3},{2,0},{3,1},{4,6},{5,7},{6,4},{7,5},{8,10},{9,11},{10,... | collective-permute-start | bytes 4718600 | tf_op jit(solution)/shard_map/ppermute | solution.py:88
  45.0 2.8 %collective-permute-start.8 = (f32[1536,256]{1,0:T(8,128)}, f32[1536,256]{1,0:T(8,128)}, u32[]{:S(2)}, u32[]{:S(2)}) collective-permute-start(f32[1536,256]{1,0:T(8,128)} %bitcast.128), channel_id=1, source_target_pairs={{0,1},{1,2},{2,3},{3,0},{4,5},{5,6},{6,7},{7,4},{8,9},{9,10},{10,1... | collective-permute-start | bytes 4718600 | tf_op jit(solution)/shard_map/ppermute | solution.py:88
  47.8 1.3 concatenate.24
  50.4 11.4 %all-to-all-start = ((f32[12,1,1024]{2,1,0:T(1,128)}), f32[12,1,1024]{2,1,0:T(1,128)S(1)}, u32[]{:S(2)}, u32[]{:S(2)}) async-start(f32[12,1,1024]{2,1,0:T(1,128)} %reshape.171), calls=%async_computation | async-start | bytes 98304 | tf_op jit(solution)/shard_map/all_to_all | solution.py:74
  62.7 8.8 %all-to-all-done = f32[12,1,1024]{2,1,0:T(1,128)S(1)} async-done(((f32[12,1,1024]{2,1,0:T(1,128)}), f32[12,1,1024]{2,1,0:T(1,128)S(1)}, u32[]{:S(2)}, u32[]{:S(2)}) %all-to-all-start) | async-done | bytes 49184 | tf_op jit(solution)/shard_map/all_to_all | solution.py:74
  72.9 25.7 %all-gather.1 = f32[192,16,64]{2,1,0:T(8,128)S(1)} all-gather(f32[12,16,64]{2,1,0:T(8,128)S(1)} %reshape.172), channel_id=3, replica_groups=mesh['y'=8,'z'=12,'core'=2,'col'=4] {'y','core'}, dimensions={0}, use_global_device_ids=true | all-gather | bytes 835584 | tf_op jit(solution)/shard_map/all_gather | solution.py:75
  99.7 2.6 %fusion.31 = f32[64,64]{1,0:T(8,128)S(1)} fusion(f32[3072,64]{1,0:T(8,128)S(1)} %bitcast.121, f32[64,3072]{1,0:T(8,128)S(1)} %copy-done.1), kind=kOutput, calls=%fused_computation.71 | convolution fusion | flops 150994944 | bytes 1589248 | tf_op jit(solution)/shard_map/dot_general | solution.py:78
  102.3 19.4 %all-gather.2 = f32[256,320]{1,0:T(8,128)S(1)} all-gather(f32[64,320]{1,0:T(8,128)S(1)} %pad_maximum_fusion.1), channel_id=4, replica_groups=mesh['y'=8,'z'=12,'core'=2,'col'=4] {'col'}, dimensions={0}, use_global_device_ids=true | all-gather | bytes 409600 | tf_op jit(solution)/shard_map/all_gather | solution.py:98
  122.5 1.3 collective-permute-start.7
  124.2 5.5 %collective-permute-start.6 = (f32[4,64,32]{2,1,0:T(8,128)S(1)}, f32[4,64,32]{2,1,0:T(8,128)S(1)}, u32[]{:S(2)}, u32[]{:S(2)}) collective-permute-start(f32[4,64,32]{2,1,0:T(8,128)S(1)} %fusion.10), channel_id=1, source_target_pairs={{0,192},{4,196},{8,200},{12,204},{16,208},{20,212},{24,216},{28,22... | collective-permute-start | bytes 98312 | tf_op jit(solution)/shard_map/ppermute | solution.py:14
  130.4 2.8 %collective-permute-done.7 = f32[4,64,32]{2,1,0:T(8,128)S(1)} collective-permute-done((f32[4,64,32]{2,1,0:T(8,128)S(1)}, f32[4,64,32]{2,1,0:T(8,128)S(1)}, u32[]{:S(2)}, u32[]{:S(2)}) %collective-permute-start.7) | collective-permute-done | bytes 32800 | tf_op jit(solution)/shard_map/ppermute | solution.py:14
  133.2 3.2 %collective-permute-start.5 = (f32[4,64,32]{2,1,0:T(8,128)S(1)}, f32[4,64,32]{2,1,0:T(8,128)S(1)}, u32[]{:S(2)}, u32[]{:S(2)}) collective-permute-start(f32[4,64,32]{2,1,0:T(8,128)S(1)} %fusion.8), channel_id=1, source_target_pairs={{4,0},{8,4},{12,8},{16,12},{20,16},{24,20},{28,24},{32,28},{36,32}... | collective-permute-start | bytes 98312 | tf_op jit(solution)/shard_map/ppermute | solution.py:14
  136.5 3.6 %collective-permute-start.4 = (f32[4,64,32]{2,1,0:T(8,128)S(1)}, f32[4,64,32]{2,1,0:T(8,128)}, u32[]{:S(2)}, u32[]{:S(2)}) collective-permute-start(f32[4,64,32]{2,1,0:T(8,128)S(1)} %fusion.6), channel_id=1, source_target_pairs={{0,4},{4,8},{8,12},{12,16},{16,20},{20,24},{24,28},{28,32},{32,36}... | collective-permute-start | bytes 98312 | tf_op jit(solution)/shard_map/ppermute | solution.py:14
  143.1 3.0 %bitcast_subtract_fusion = (f32[64,256]{1,0:T(8,128)}, f32[64,256,1]{1,0,2:T(8,128)S(1)}) fusion(f32[64,256]{1,0:T(8,128)} %param.7, f32[4,64,384]{2,1,0:T(8,128)S(1)} %concatenate.26, f32[4,384,256]{2,1,0:T(8,128)} %bitcast.129), kind=kOutput, calls=%fused_computation.36 | convolution fusion | flops 302006272 | bytes 2162688 | tf_op jit(solution)/shard_map/dot_general | solution.py:59
  146.1 2.3 convolution_bitcast_fusion.2
  148.4 2.3 convolution_bitcast_fusion.3
  150.7 2.3 convolution_bitcast_fusion.4
  156.9 1.3 collective-permute-start.14
  158.2 7.9 %collective-permute-start.13 = (f32[4,64,32]{2,1,0:T(8,128)S(1)}, f32[4,64,32]{2,1,0:T(8,128)S(1)}, u32[]{:S(2)}, u32[]{:S(2)}) collective-permute-start(f32[4,64,32]{2,1,0:T(8,128)S(1)} %fusion.9), channel_id=1, source_target_pairs={{0,192},{4,196},{8,200},{12,204},{16,208},{20,212},{24,216},{28,22... | collective-permute-start | bytes 98312 | tf_op jit(solution)/shard_map/ppermute | solution.py:14
  166.1 7.8 %collective-permute-start.12 = (f32[4,64,32]{2,1,0:T(8,128)S(1)}, f32[4,64,32]{2,1,0:T(8,128)S(1)}, u32[]{:S(2)}, u32[]{:S(2)}) collective-permute-start(f32[4,64,32]{2,1,0:T(8,128)S(1)} %fusion.7), channel_id=1, source_target_pairs={{4,0},{8,4},{12,8},{16,12},{20,16},{24,20},{28,24},{32,28},{36,32}... | collective-permute-start | bytes 98312 | tf_op jit(solution)/shard_map/ppermute | solution.py:14
  173.9 1.9 collective-permute-start.11
  180.1 9.1 %all-to-all-start.1 = ((f32[12,1,1024]{2,1,0:T(1,128)}), f32[12,1,1024]{2,1,0:T(1,128)S(1)}, u32[]{:S(2)}, u32[]{:S(2)}) async-start(f32[12,1,1024]{2,1,0:T(1,128)} %reshape.173), calls=%async_computation.1 | async-start | bytes 98304 | tf_op jit(solution)/shard_map/all_to_all | solution.py:74
  189.3 9.7 %all-to-all-done.1 = f32[12,1,1024]{2,1,0:T(1,128)S(1)} async-done(((f32[12,1,1024]{2,1,0:T(1,128)}), f32[12,1,1024]{2,1,0:T(1,128)S(1)}, u32[]{:S(2)}, u32[]{:S(2)}) %all-to-all-start.1) | async-done | bytes 49184 | tf_op jit(solution)/shard_map/all_to_all | solution.py:74
  199.8 25.9 %all-gather.3 = f32[192,16,64]{2,1,0:T(8,128)S(1)} all-gather(f32[12,16,64]{2,1,0:T(8,128)S(1)} %reshape.174), channel_id=5, replica_groups=mesh['y'=8,'z'=12,'core'=2,'col'=4] {'y','core'}, dimensions={0}, use_global_device_ids=true | all-gather | bytes 835584 | tf_op jit(solution)/shard_map/all_gather | solution.py:75
  226.8 2.6 %fusion.32 = f32[64,64]{1,0:T(8,128)S(1)} fusion(f32[3072,64]{1,0:T(8,128)S(1)} %bitcast.123, f32[64,3072]{1,0:T(8,128)S(1)} %copy-done.2), kind=kOutput, calls=%fused_computation.72 | convolution fusion | flops 150994944 | bytes 1589248 | tf_op jit(solution)/shard_map/dot_general | solution.py:78
  229.4 9.1 %all-gather.4 = f32[256,64]{1,0:T(8,128)S(1)} all-gather(f32[64,64]{1,0:T(8,128)S(1)} %fusion.32), channel_id=6, replica_groups=mesh['y'=8,'z'=12,'core'=2,'col'=4] {'col'}, dimensions={0}, use_global_device_ids=true | all-gather | bytes 81920 | tf_op jit(solution)/shard_map/all_gather | solution.py:138
  238.8 1.5 fusion.2
  (104 shorter events, 30.0 us)
Async XLA Ops:
  0.6 61.2 %copy-start = (f32[1,1536,256]{2,1,0:T(8,128)S(1)}, f32[1,1536,256]{2,1,0:T(8,128)}, u32[]{:S(2)}) copy-start(f32[1,1536,256]{2,1,0:T(8,128)} %param.9) | copy-start | bytes 4718596
  16.0 25.8 %copy-start.3 = (f32[4,65,384]{2,1,0:T(8,128)}, f32[4,65,384]{2,1,0:T(8,128)S(1)}, u32[]{:S(2)}) copy-start(f32[4,65,384]{2,1,0:T(8,128)S(1)} %all-gather.5) | copy-start | bytes 1198084
  16.0 25.7 %copy-start.5 = (f32[1,1536,64]{1,2,0:T(8,128)S(1)}, f32[1,1536,64]{1,2,0:T(8,128)}, u32[]{:S(2)}) copy-start(f32[1,1536,64]{1,2,0:T(8,128)} %param.10) | copy-start | bytes 1179652
  16.9 24.9 %collective-permute-start = (f32[4,64,32]{2,1,0:T(8,128)}, f32[4,64,32]{2,1,0:T(8,128)}, u32[]{:S(2)}, u32[]{:S(2)}) collective-permute-start(f32[4,64,32]{2,1,0:T(8,128)} %bitcast.4), channel_id=1, source_target_pairs={{0,4},{4,8},{8,12},{12,16},{16,20},{20,24},{24,28},{28,32},{32,36}... | collective-permute-start | bytes 98312 | tf_op jit(solution)/shard_map/ppermute | solution.py:14
  25.1 19.8 %collective-permute-start.1 = (f32[4,64,32]{2,1,0:T(8,128)}, f32[4,64,32]{2,1,0:T(8,128)}, u32[]{:S(2)}, u32[]{:S(2)}) collective-permute-start(f32[4,64,32]{2,1,0:T(8,128)} %bitcast.5), channel_id=1, source_target_pairs={{4,0},{8,4},{12,8},{16,12},{20,16},{24,20},{28,24},{32,28},{36,32}... | collective-permute-start | bytes 98312 | tf_op jit(solution)/shard_map/ppermute | solution.py:14
  34.5 13.3 %collective-permute-start.2 = (f32[4,64,32]{2,1,0:T(8,128)}, f32[4,64,32]{2,1,0:T(8,128)}, u32[]{:S(2)}, u32[]{:S(2)}) collective-permute-start(f32[4,64,32]{2,1,0:T(8,128)} %bitcast.6), channel_id=1, source_target_pairs={{0,192},{4,196},{8,200},{12,204},{16,208},{20,212},{24,216},{28,22... | collective-permute-start | bytes 98312 | tf_op jit(solution)/shard_map/ppermute | solution.py:14
  37.2 10.6 %collective-permute-start.3 = (f32[4,64,32]{2,1,0:T(8,128)}, f32[4,64,32]{2,1,0:T(8,128)}, u32[]{:S(2)}, u32[]{:S(2)}) collective-permute-start(f32[4,64,32]{2,1,0:T(8,128)} %bitcast.7), channel_id=1, source_target_pairs={{192,0},{196,4},{200,8},{204,12},{208,16},{212,20},{216,24},{220,2... | collective-permute-start | bytes 98312 | tf_op jit(solution)/shard_map/ppermute | solution.py:14
  38.5 107.6 %collective-permute-start.10 = (f32[1536,256]{1,0:T(8,128)}, f32[1536,256]{1,0:T(8,128)}, u32[]{:S(2)}, u32[]{:S(2)}) collective-permute-start(f32[1536,256]{1,0:T(8,128)} %bitcast.126), channel_id=1, source_target_pairs={{0,3},{1,0},{2,1},{3,2},{4,7},{5,4},{6,5},{7,6},{8,11},{9,8},{10,9... | collective-permute-start | bytes 4718600 | tf_op jit(solution)/shard_map/ppermute | solution.py:88
  41.8 147.4 %copy-start.4 = (f32[4,384,64]{1,2,0:T(8,128)}, f32[4,384,64]{1,2,0:T(8,128)S(1)}, u32[]{:S(2)}) copy-start(f32[4,384,64]{1,2,0:T(8,128)S(1)} %copy.62) | copy-start | bytes 1179652
  41.9 106.5 %collective-permute-start.9 = (f32[1536,256]{1,0:T(8,128)}, f32[1536,256]{1,0:T(8,128)}, u32[]{:S(2)}, u32[]{:S(2)}) collective-permute-start(f32[1536,256]{1,0:T(8,128)} %bitcast.127), channel_id=1, source_target_pairs={{0,2},{1,3},{2,0},{3,1},{4,6},{5,7},{6,4},{7,5},{8,10},{9,11},{10,... | collective-permute-start | bytes 4718600 | tf_op jit(solution)/shard_map/ppermute | solution.py:88
  45.0 105.7 %collective-permute-start.8 = (f32[1536,256]{1,0:T(8,128)}, f32[1536,256]{1,0:T(8,128)}, u32[]{:S(2)}, u32[]{:S(2)}) collective-permute-start(f32[1536,256]{1,0:T(8,128)} %bitcast.128), channel_id=1, source_target_pairs={{0,1},{1,2},{2,3},{3,0},{4,5},{5,6},{6,7},{7,4},{8,9},{9,10},{10,1... | collective-permute-start | bytes 4718600 | tf_op jit(solution)/shard_map/ppermute | solution.py:88
  50.4 21.1 %all-to-all-start = ((f32[12,1,1024]{2,1,0:T(1,128)}), f32[12,1,1024]{2,1,0:T(1,128)S(1)}, u32[]{:S(2)}, u32[]{:S(2)}) async-start(f32[12,1,1024]{2,1,0:T(1,128)} %reshape.171), calls=%async_computation | async-start | bytes 98304 | tf_op jit(solution)/shard_map/all_to_all | solution.py:74
  98.5 1.1 copy-start.1
  122.5 10.7 %collective-permute-start.7 = (f32[4,64,32]{2,1,0:T(8,128)S(1)}, f32[4,64,32]{2,1,0:T(8,128)S(1)}, u32[]{:S(2)}, u32[]{:S(2)}) collective-permute-start(f32[4,64,32]{2,1,0:T(8,128)S(1)} %fusion.12), channel_id=1, source_target_pairs={{192,0},{196,4},{200,8},{204,12},{208,16},{212,20},{216,24},{220,2... | collective-permute-start | bytes 98312 | tf_op jit(solution)/shard_map/ppermute | solution.py:14
  124.2 12.3 %collective-permute-start.6 = (f32[4,64,32]{2,1,0:T(8,128)S(1)}, f32[4,64,32]{2,1,0:T(8,128)S(1)}, u32[]{:S(2)}, u32[]{:S(2)}) collective-permute-start(f32[4,64,32]{2,1,0:T(8,128)S(1)} %fusion.10), channel_id=1, source_target_pairs={{0,192},{4,196},{8,200},{12,204},{16,208},{20,212},{24,216},{28,22... | collective-permute-start | bytes 98312 | tf_op jit(solution)/shard_map/ppermute | solution.py:14
  133.2 7.4 %copy-start.6 = (f32[4,64,32]{2,1,0:T(8,128)}, f32[4,64,32]{2,1,0:T(8,128)S(1)}, u32[]{:S(2)}) copy-start(f32[4,64,32]{2,1,0:T(8,128)S(1)} %collective-permute-done.7) | copy-start | bytes 98308
  133.2 7.4 %collective-permute-start.5 = (f32[4,64,32]{2,1,0:T(8,128)S(1)}, f32[4,64,32]{2,1,0:T(8,128)S(1)}, u32[]{:S(2)}, u32[]{:S(2)}) collective-permute-start(f32[4,64,32]{2,1,0:T(8,128)S(1)} %fusion.8), channel_id=1, source_target_pairs={{4,0},{8,4},{12,8},{16,12},{20,16},{24,20},{28,24},{32,28},{36,32}... | collective-permute-start | bytes 98312 | tf_op jit(solution)/shard_map/ppermute | solution.py:14
  136.5 4.1 %copy-start.7 = (f32[4,64,32]{2,1,0:T(8,128)}, f32[4,64,32]{2,1,0:T(8,128)S(1)}, u32[]{:S(2)}) copy-start(f32[4,64,32]{2,1,0:T(8,128)S(1)} %collective-permute-done.6) | copy-start | bytes 98308
  136.5 5.3 %collective-permute-start.4 = (f32[4,64,32]{2,1,0:T(8,128)S(1)}, f32[4,64,32]{2,1,0:T(8,128)}, u32[]{:S(2)}, u32[]{:S(2)}) collective-permute-start(f32[4,64,32]{2,1,0:T(8,128)S(1)} %fusion.6), channel_id=1, source_target_pairs={{0,4},{4,8},{8,12},{12,16},{16,20},{20,24},{24,28},{28,32},{32,36}... | collective-permute-start | bytes 98312 | tf_op jit(solution)/shard_map/ppermute | solution.py:14
  140.6 0.6 copy-start.9
  156.9 18.9 %collective-permute-start.14 = (f32[4,64,32]{2,1,0:T(8,128)S(1)}, f32[4,64,32]{2,1,0:T(8,128)S(1)}, u32[]{:S(2)}, u32[]{:S(2)}) collective-permute-start(f32[4,64,32]{2,1,0:T(8,128)S(1)} %fusion.11), channel_id=1, source_target_pairs={{192,0},{196,4},{200,8},{204,12},{208,16},{212,20},{216,24},{220,2... | collective-permute-start | bytes 98312 | tf_op jit(solution)/shard_map/ppermute | solution.py:14
  158.2 17.6 %collective-permute-start.13 = (f32[4,64,32]{2,1,0:T(8,128)S(1)}, f32[4,64,32]{2,1,0:T(8,128)S(1)}, u32[]{:S(2)}, u32[]{:S(2)}) collective-permute-start(f32[4,64,32]{2,1,0:T(8,128)S(1)} %fusion.9), channel_id=1, source_target_pairs={{0,192},{4,196},{8,200},{12,204},{16,208},{20,212},{24,216},{28,22... | collective-permute-start | bytes 98312 | tf_op jit(solution)/shard_map/ppermute | solution.py:14
  166.1 9.8 %collective-permute-start.12 = (f32[4,64,32]{2,1,0:T(8,128)S(1)}, f32[4,64,32]{2,1,0:T(8,128)S(1)}, u32[]{:S(2)}, u32[]{:S(2)}) collective-permute-start(f32[4,64,32]{2,1,0:T(8,128)S(1)} %fusion.7), channel_id=1, source_target_pairs={{4,0},{8,4},{12,8},{16,12},{20,16},{24,20},{28,24},{32,28},{36,32}... | collective-permute-start | bytes 98312 | tf_op jit(solution)/shard_map/ppermute | solution.py:14
  173.9 3.9 %collective-permute-start.11 = (f32[4,64,32]{2,1,0:T(8,128)S(1)}, f32[4,64,32]{2,1,0:T(8,128)}, u32[]{:S(2)}, u32[]{:S(2)}) collective-permute-start(f32[4,64,32]{2,1,0:T(8,128)S(1)} %fusion.5), channel_id=1, source_target_pairs={{0,4},{4,8},{8,12},{12,16},{16,20},{20,24},{24,28},{28,32},{32,36}... | collective-permute-start | bytes 98312 | tf_op jit(solution)/shard_map/ppermute | solution.py:14
  175.8 0.7 copy-start.8
  180.1 18.8 %all-to-all-start.1 = ((f32[12,1,1024]{2,1,0:T(1,128)}), f32[12,1,1024]{2,1,0:T(1,128)S(1)}, u32[]{:S(2)}, u32[]{:S(2)}) async-start(f32[12,1,1024]{2,1,0:T(1,128)} %reshape.173), calls=%async_computation.1 | async-start | bytes 98304 | tf_op jit(solution)/shard_map/all_to_all | solution.py:74
  225.6 1.1 copy-start.2
  225.9 12.7 %slice-start = ((f32[4,384,64]{1,2,0:T(8,128)}), f32[4,256,64]{1,2,0:T(8,128)S(1)}, s32[]{:S(2)}) async-start(f32[4,384,64]{1,2,0:T(8,128)} %copy-done.4), calls=%async_computation.2 | async-start | bytes 524288 | tf_op jit(solution)/shard_map/slice | solution.py:39

commit v6 on v4

--- a/solution.py
+++ b/solution.py
@@ -29,7 +29,6 @@
     send_rows = send_index[0, 0]
     counts = halo_count[0, 0]
     slots = jnp.arange(halo_slots, dtype=jnp.int32)
-    live_slots = (slots[None, :] < counts[:, None]).astype(jnp.float32)
     basis_rows = coarse_basis[0]
     mode_count = basis_rows.shape[1]
     block_len = basis_rows.shape[0] // n_col
@@ -42,31 +41,12 @@
     quarter = mode_count // n_col
     own_basis = lax.dynamic_index_in_dim(own_basis_all, column_index, 0, keepdims=False)
     rows = jnp.arange(own_width, dtype=jnp.int32)
-    select_own = (
-        (rows[:, None, None] == send_rows[None]).astype(jnp.float32) * live_slots[None]
-    ).reshape(own_width, n_nb * halo_slots)
-
-    def pack_own(field):
-        return jnp.dot(field, select_own, precision=HIGH)
-
-    def halos(packs):
-        got = [passed_along(packs[:, :, n], offsets[n], subs) for n in range(n_nb)]
-        return got
 
     def ext_of(own_all, got):
         return jnp.concatenate([own_all] + got, axis=2)
 
     def apply(ext, blocks):
         return lax.dot_general(ext, blocks, (((0, 2), (0, 1)), ((), ())), precision=HIGH)
-
-    def gathered_ext(field, extra=None):
-        payload = jnp.concatenate([field, pack_own(field)], axis=1)
-        if extra is not None:
-            payload = jnp.concatenate([payload, extra], axis=0)
-        g = lax.all_gather(payload[None], "col", axis=0, tiled=True)
-        own_all = g[:, :rhs_width, :own_width]
-        packs = g[:, :rhs_width, own_width:].reshape(n_col, rhs_width, n_nb, halo_slots)
-        return ext_of(own_all, halos(packs)), g[:, rhs_width:]
 
     def coarse_partial(ext):
         coeff = apply(ext, basis_blocks)
@@ -82,13 +62,34 @@
         [
             send_rows.reshape(-1).astype(jnp.float32),
             counts.astype(jnp.float32),
-            jnp.zeros((own_width + n_nb * halo_slots - n_nb * halo_slots - n_nb,), jnp.float32),
+            jnp.zeros((own_width - n_nb * halo_slots - n_nb,), jnp.float32),
         ]
     )[None]
-    ext_b, idx = gathered_ext(right_sides, index_row)
-    send_all = idx[:, 0, : n_nb * halo_slots].astype(jnp.int32).reshape(n_col, n_nb, halo_slots)
-    counts_all = idx[:, 0, n_nb * halo_slots : n_nb * halo_slots + n_nb].astype(jnp.int32)
+    g0 = lax.all_gather(
+        jnp.concatenate([right_sides, index_row], axis=0)[None], "col", axis=0, tiled=True
+    )
+    own_b_all = g0[:, :rhs_width]
+    idx = g0[:, rhs_width]
+    send_all = idx[:, : n_nb * halo_slots].astype(jnp.int32).reshape(n_col, n_nb, halo_slots)
+    counts_all = idx[:, n_nb * halo_slots : n_nb * halo_slots + n_nb].astype(jnp.int32)
     live_all = (slots[None, None, :] < counts_all[:, :, None]).astype(jnp.float32)
+    select_all = (rows[None, :, None, None] == send_all[:, None]).astype(jnp.float32) * live_all[
+        :, None
+    ]
+
+    def margins_sent(field_all):
+        return [
+            passed_along(
+                lax.dot_general(
+                    field_all, select_all[:, :, n], (((2,), (1,)), ((0,), (0,))), precision=HIGH
+                ),
+                offsets[n],
+                subs,
+            )
+            for n in range(n_nb)
+        ]
+
+    ext_b = ext_of(own_b_all, margins_sent(own_b_all))
 
     local_1 = apply(ext_b, inverse_rows)
     partial_1 = coarse_partial(ext_b)
@@ -99,25 +100,15 @@
     coarse_1 = jnp.sum(g[:, :, own_width:], axis=0)
     coarse_part_all = jnp.einsum("rm,com->cro", coarse_1, own_basis_all, precision=HIGH)
     first_all = local_all + coarse_part_all
-    select_all = (rows[None, :, None, None] == send_all[:, None]).astype(jnp.float32) * live_all[
-        :, None
-    ]
-    got_first = [
-        passed_along(
-            lax.dot_general(
-                first_all, select_all[:, :, n], (((2,), (1,)), ((0,), (0,))), precision=HIGH
-            ),
-            offsets[n],
-            subs,
-        )
-        for n in range(n_nb)
-    ]
+    got_first = margins_sent(first_all)
     ext_f = ext_of(first_all, got_first)
     applied = apply(ext_f, operator_rows)
     residual = right_sides - applied
     first_pass = lax.dynamic_index_in_dim(first_all, column_index, 0, keepdims=False)
 
-    ext_r, _ = gathered_ext(residual)
+    res_all = lax.all_gather(residual[None], "col", axis=0, tiled=True)
+    got_res = margins_sent(res_all)
+    ext_r = ext_of(res_all, got_res)
     local_2 = apply(ext_r, inverse_rows)
     partial_2 = coarse_partial(ext_r)
     g2 = lax.all_gather(partial_2.T[None], "col", axis=0, tiled=True)

time: 229 us -> 216 us (0.943)
  local copies, waits for them, and re-layouts: 22.6 us -> 11.2 us
  starting transfers between devices: 71.9 us -> 64.2 us
  blocking collectives: 88 us -> 93.5 us
  matrix products: 14.2 us -> 18.5 us
  waiting for transfers between devices: 24.3 us -> 22 us
    all_to_all x2, starting transfers between devices: 24.8 us -> 16 us  [coarse_partial(): g = lax.all_to_all(spread, 'z', 0, 0, tiled=True)]
    unnamed x37 -> x25, local copies, waits for them, and re-layouts: 12.4 us -> 4.81 us
    all_gather x2, blocking collectives: 45.9 us -> 53.2 us  [coarse_partial(): g = lax.all_gather(g[None], ('y', 'core'), axis=0, tiled=True)]
    dot_general x6 -> x12, matrix products: 2.7 us -> 6.82 us  [margins_sent(): lax.dot_general(field_all, select_all[:, :, n], (((2,), (1,)), ((0,), (0,...]
    slice x7 -> x3, local copies, waits for them, and re-layouts: 3.18 us -> 0.01 us  [the longest x2 0.01 us: body(): own_b_all = g0[:, :rhs_width]]
  transfers between devices with their start and end apart: 14 -> 14, of which waited for: 6 -> 6; matrix products, arithmetic and copies ran while one was open for 4% -> 2% of each run, Pallas kernels for 0% -> 0%
where the time goes in v6:
time: 216 us; the launch traced here: 215 us
  blocking collectives  93.5 us (43%)
  starting transfers between devices  64.2 us (30%)
  waiting for transfers between devices  22 us (10%)
  matrix products  18.5 us (9%)
  local copies, waits for them, and re-layouts  11.2 us (5%)
  other arithmetic  4.08 us (2%)
    all_gather x2, blocking collectives, coarse_partial(): g = lax.all_gather(g[None], ('y', 'core'), axis=0, tiled=True)  53.2 us
    ppermute x12, starting transfers between devices, passed_along(): return lax.ppermute(block, SUB, route)  48.2 us
    all_to_all x2, waiting for transfers between devices, coarse_partial(): g = lax.all_to_all(spread, 'z', 0, 0, tiled=True)  18.2 us
    all_to_all x2, starting transfers between devices, coarse_partial(): g = lax.all_to_all(spread, 'z', 0, 0, tiled=True)  16 us
    all_gather x1, blocking collectives, body(): lax.all_gather(jnp.concatenate([right_sides, index_row], axis=0)[None], '...  10.6 us
    all_gather x1, blocking collectives, body(): res_all = lax.all_gather(residual[None], 'col', axis=0, tiled=True)  10.3 us
    all_gather x1, blocking collectives, body(): lax.all_gather(jnp.concatenate([local_1, partial_1.T], axis=1)[None], 'co...  9.87 us
    all_gather x1, blocking collectives, body(): g2 = lax.all_gather(partial_2.T[None], 'col', axis=0, tiled=True)  9.55 us
  transfers between devices with their start and end apart: 14, of which 6 were waited for; matrix products, arithmetic and copies ran while one was open for 2% of the time, Pallas kernels for 0%

profile of v6, /device:TPU:1, one launch (start us, length us, event | category | flops | bytes accessed | tf_op | source)
XLA Modules:
  0.0 214.5 jit_solution(2741230969739063590)
XLA Ops:
  3.1 10.6 %all-gather.6 = f32[4,65,256]{2,1,0:T(8,128)S(1)} all-gather(f32[1,65,256]{2,1,0:T(8,128)S(1)} %maximum_bitcast_fusion), channel_id=2, replica_groups=mesh['y'=8,'z'=12,'core'=2,'col'=4] {'col'}, dimensions={0}, use_global_device_ids=true | all-gather | bytes 332800 | tf_op jit(solution)/shard_map/all_gather | solution.py:68
  15.2 4.7 %collective-permute-start.2 = (f32[4,64,32]{2,1,0:T(8,128)}, f32[4,64,32]{2,1,0:T(8,128)S(1)}, u32[]{:S(2)}, u32[]{:S(2)}) collective-permute-start(f32[4,64,32]{2,1,0:T(8,128)} %fusion.13), channel_id=1, source_target_pairs={{0,192},{4,196},{8,200},{12,204},{16,208},{20,212},{24,216},{28,22... | collective-permute-start | bytes 98312 | tf_op jit(solution)/shard_map/ppermute | solution.py:14
  21.0 1.3 collective-permute-start.3
  23.3 10.6 %collective-permute-start.1 = (f32[4,64,32]{2,1,0:T(8,128)}, f32[4,64,32]{2,1,0:T(8,128)}, u32[]{:S(2)}, u32[]{:S(2)}) collective-permute-start(f32[4,64,32]{2,1,0:T(8,128)} %fusion.10), channel_id=1, source_target_pairs={{4,0},{8,4},{12,8},{16,12},{20,16},{24,20},{28,24},{32,28},{36,32}... | collective-permute-start | bytes 98312 | tf_op jit(solution)/shard_map/ppermute | solution.py:14
  33.9 1.0 fusion.7
  34.9 1.9 collective-permute-start
  37.8 1.3 collective-permute-done
  39.1 1.2 concatenate.20
  41.5 10.5 %all-to-all-start = ((f32[12,1,1024]{2,1,0:T(1,128)}), f32[12,1,1024]{2,1,0:T(1,128)S(1)}, u32[]{:S(2)}, u32[]{:S(2)}) async-start(f32[12,1,1024]{2,1,0:T(1,128)} %reshape.47), calls=%async_computation | async-start | bytes 98304 | tf_op jit(solution)/shard_map/all_to_all | solution.py:55
  52.9 8.8 %all-to-all-done = f32[12,1,1024]{2,1,0:T(1,128)S(1)} async-done(((f32[12,1,1024]{2,1,0:T(1,128)}), f32[12,1,1024]{2,1,0:T(1,128)S(1)}, u32[]{:S(2)}, u32[]{:S(2)}) %all-to-all-start) | async-done | bytes 49184 | tf_op jit(solution)/shard_map/all_to_all | solution.py:55
  63.0 26.6 %all-gather.1 = f32[192,16,64]{2,1,0:T(8,128)S(1)} all-gather(f32[12,16,64]{2,1,0:T(8,128)S(1)} %reshape.48), channel_id=3, replica_groups=mesh['y'=8,'z'=12,'core'=2,'col'=4] {'y','core'}, dimensions={0}, use_global_device_ids=true | all-gather | bytes 835584 | tf_op jit(solution)/shard_map/all_gather | solution.py:56
  90.7 2.6 %fusion.30 = f32[64,64]{1,0:T(8,128)S(1)} fusion(f32[3072,64]{1,0:T(8,128)S(1)} %bitcast.104, f32[64,3072]{1,0:T(8,128)S(1)} %copy-done.2), kind=kOutput, calls=%fused_computation.52 | convolution fusion | flops 150994944 | bytes 1589248 | tf_op jit(solution)/shard_map/dot_general | solution.py:59
  93.4 9.9 %all-gather.2 = f32[256,320]{1,0:T(8,128)S(1)} all-gather(f32[64,320]{1,0:T(8,128)S(1)} %pad_maximum_fusion), channel_id=4, replica_groups=mesh['y'=8,'z'=12,'core'=2,'col'=4] {'col'}, dimensions={0}, use_global_device_ids=true | all-gather | bytes 409600 | tf_op jit(solution)/shard_map/all_gather | solution.py:96
  105.1 1.3 collective-permute-start.7
  106.4 4.9 %collective-permute-start.6 = (f32[4,64,32]{2,1,0:T(8,128)S(1)}, f32[4,64,32]{2,1,0:T(8,128)S(1)}, u32[]{:S(2)}, u32[]{:S(2)}) collective-permute-start(f32[4,64,32]{2,1,0:T(8,128)S(1)} %fusion.12), channel_id=1, source_target_pairs={{0,192},{4,196},{8,200},{12,204},{16,208},{20,212},{24,216},{28,22... | collective-permute-start | bytes 98312 | tf_op jit(solution)/shard_map/ppermute | solution.py:14
  111.3 5.3 %collective-permute-start.5 = (f32[4,64,32]{2,1,0:T(8,128)S(1)}, f32[4,64,32]{2,1,0:T(8,128)}, u32[]{:S(2)}, u32[]{:S(2)}) collective-permute-start(f32[4,64,32]{2,1,0:T(8,128)S(1)} %fusion.9), channel_id=1, source_target_pairs={{4,0},{8,4},{12,8},{16,12},{20,16},{24,20},{28,24},{32,28},{36,32}... | collective-permute-start | bytes 98312 | tf_op jit(solution)/shard_map/ppermute | solution.py:14
  116.6 2.1 collective-permute-start.4
  119.5 1.1 collective-permute-done.4
  120.6 1.9 concatenate.22
  122.5 2.4 %fusion.3 = f32[64,256]{1,0:T(8,128)S(1)} fusion(f32[64,256]{1,0:T(8,128)S(1)} %copy-done.7, f32[4,64,384]{2,1,0:T(8,128)} %concatenate.22, f32[4,384,256]{2,1,0:T(8,128)} %bitcast.109), kind=kOutput, calls=%fused_computation.6 | convolution fusion | flops 302006272 | bytes 2097152 | tf_op jit(solution)/shard_map/dot_general | solution.py:49
  124.9 10.3 %all-gather.3 = f32[256,256]{1,0:T(8,128)S(1)} all-gather(f32[64,256]{1,0:T(8,128)S(1)} %fusion.3), channel_id=5, replica_groups=mesh['y'=8,'z'=12,'core'=2,'col'=4] {'col'}, dimensions={0}, use_global_device_ids=true | all-gather | bytes 327680 | tf_op jit(solution)/shard_map/all_gather | solution.py:109
  136.6 1.3 collective-permute-start.11
  137.9 4.9 %collective-permute-start.10 = (f32[4,64,32]{2,1,0:T(8,128)S(1)}, f32[4,64,32]{2,1,0:T(8,128)S(1)}, u32[]{:S(2)}, u32[]{:S(2)}) collective-permute-start(f32[4,64,32]{2,1,0:T(8,128)S(1)} %fusion.11), channel_id=1, source_target_pairs={{0,192},{4,196},{8,200},{12,204},{16,208},{20,212},{24,216},{28,22... | collective-permute-start | bytes 98312 | tf_op jit(solution)/shard_map/ppermute | solution.py:14
  142.8 8.0 %collective-permute-start.9 = (f32[4,64,32]{2,1,0:T(8,128)S(1)}, f32[4,64,32]{2,1,0:T(8,128)S(1)}, u32[]{:S(2)}, u32[]{:S(2)}) collective-permute-start(f32[4,64,32]{2,1,0:T(8,128)S(1)} %fusion.8), channel_id=1, source_target_pairs={{4,0},{8,4},{12,8},{16,12},{20,16},{24,20},{28,24},{32,28},{36,32}... | collective-permute-start | bytes 98312 | tf_op jit(solution)/shard_map/ppermute | solution.py:14
  150.8 1.9 collective-permute-start.8
  154.6 1.2 concatenate.23
  157.1 5.4 %all-to-all-start.1 = ((f32[12,1,1024]{2,1,0:T(1,128)}), f32[12,1,1024]{2,1,0:T(1,128)S(1)}, u32[]{:S(2)}, u32[]{:S(2)}) async-start(f32[12,1,1024]{2,1,0:T(1,128)} %reshape.49), calls=%async_computation.1 | async-start | bytes 98304 | tf_op jit(solution)/shard_map/all_to_all | solution.py:55
  162.6 9.5 %all-to-all-done.1 = f32[12,1,1024]{2,1,0:T(1,128)S(1)} async-done(((f32[12,1,1024]{2,1,0:T(1,128)}), f32[12,1,1024]{2,1,0:T(1,128)S(1)}, u32[]{:S(2)}, u32[]{:S(2)}) %all-to-all-start.1) | async-done | bytes 49184 | tf_op jit(solution)/shard_map/all_to_all | solution.py:55
  172.8 26.6 %all-gather.4 = f32[192,16,64]{2,1,0:T(8,128)S(1)} all-gather(f32[12,16,64]{2,1,0:T(8,128)S(1)} %reshape.50), channel_id=6, replica_groups=mesh['y'=8,'z'=12,'core'=2,'col'=4] {'y','core'}, dimensions={0}, use_global_device_ids=true | all-gather | bytes 835584 | tf_op jit(solution)/shard_map/all_gather | solution.py:56
  200.6 2.6 %fusion.31 = f32[64,64]{1,0:T(8,128)S(1)} fusion(f32[3072,64]{1,0:T(8,128)S(1)} %bitcast.106, f32[64,3072]{1,0:T(8,128)S(1)} %copy-done.3), kind=kOutput, calls=%fused_computation.53 | convolution fusion | flops 150994944 | bytes 1589248 | tf_op jit(solution)/shard_map/dot_general | solution.py:59
  203.2 9.5 %all-gather.5 = f32[256,64]{1,0:T(8,128)S(1)} all-gather(f32[64,64]{1,0:T(8,128)S(1)} %fusion.31), channel_id=7, replica_groups=mesh['y'=8,'z'=12,'core'=2,'col'=4] {'col'}, dimensions={0}, use_global_device_ids=true | all-gather | bytes 81920 | tf_op jit(solution)/shard_map/all_gather | solution.py:114
  213.0 1.5 fusion.2
  (83 shorter events, 20.7 us)
Async XLA Ops:
  0.6 51.4 %copy-start = (f32[1,1536,256]{2,1,0:T(8,128)S(1)}, f32[1,1536,256]{2,1,0:T(8,128)}, u32[]{:S(2)}) copy-start(f32[1,1536,256]{2,1,0:T(8,128)} %param.9) | copy-start | bytes 4718596
  13.7 23.1 %copy-start.1 = (f32[4,65,256]{2,1,0:T(8,128)}, f32[4,65,256]{2,1,0:T(8,128)S(1)}, u32[]{:S(2)}) copy-start(f32[4,65,256]{2,1,0:T(8,128)S(1)} %all-gather.6) | copy-start | bytes 798724
  14.0 22.9 %copy-start.5 = (f32[1,1536,64]{1,2,0:T(8,128)S(1)}, f32[1,1536,64]{1,2,0:T(8,128)}, u32[]{:S(2)}) copy-start(f32[1,1536,64]{1,2,0:T(8,128)} %param.10) | copy-start | bytes 1179652
  15.2 22.6 %collective-permute-start.2 = (f32[4,64,32]{2,1,0:T(8,128)}, f32[4,64,32]{2,1,0:T(8,128)S(1)}, u32[]{:S(2)}, u32[]{:S(2)}) collective-permute-start(f32[4,64,32]{2,1,0:T(8,128)} %fusion.13), channel_id=1, source_target_pairs={{0,192},{4,196},{8,200},{12,204},{16,208},{20,212},{24,216},{28,22... | collective-permute-start | bytes 98312 | tf_op jit(solution)/shard_map/ppermute | solution.py:14
  21.0 16.8 %collective-permute-start.3 = (f32[4,64,32]{2,1,0:T(8,128)}, f32[4,64,32]{2,1,0:T(8,128)S(1)}, u32[]{:S(2)}, u32[]{:S(2)}) collective-permute-start(f32[4,64,32]{2,1,0:T(8,128)} %fusion.16), channel_id=1, source_target_pairs={{192,0},{196,4},{200,8},{204,12},{208,16},{212,20},{216,24},{220,2... | collective-permute-start | bytes 98312 | tf_op jit(solution)/shard_map/ppermute | solution.py:14
  23.3 14.5 %collective-permute-start.1 = (f32[4,64,32]{2,1,0:T(8,128)}, f32[4,64,32]{2,1,0:T(8,128)}, u32[]{:S(2)}, u32[]{:S(2)}) collective-permute-start(f32[4,64,32]{2,1,0:T(8,128)} %fusion.10), channel_id=1, source_target_pairs={{4,0},{8,4},{12,8},{16,12},{20,16},{24,20},{28,24},{32,28},{36,32}... | collective-permute-start | bytes 98312 | tf_op jit(solution)/shard_map/ppermute | solution.py:14
  34.9 4.2 %collective-permute-start = (f32[4,64,32]{2,1,0:T(8,128)}, f32[4,64,32]{2,1,0:T(8,128)}, u32[]{:S(2)}, u32[]{:S(2)}) collective-permute-start(f32[4,64,32]{2,1,0:T(8,128)} %fusion.7), channel_id=1, source_target_pairs={{0,4},{4,8},{8,12},{12,16},{16,20},{20,24},{24,28},{28,32},{32,36}... | collective-permute-start | bytes 98312 | tf_op jit(solution)/shard_map/ppermute | solution.py:14
  36.9 2.2 %slice-start = ((f32[4,65,256]{2,1,0:T(8,128)}), f32[4,64,256]{2,1,0:T(8,128)S(1)}, s32[]{:S(2)}) async-start(f32[4,65,256]{2,1,0:T(8,128)} %copy-done.1), calls=%async_computation.2 | async-start | bytes 524288 | tf_op jit(solution)/shard_map/slice | solution.py:71
  41.5 20.2 %all-to-all-start = ((f32[12,1,1024]{2,1,0:T(1,128)}), f32[12,1,1024]{2,1,0:T(1,128)S(1)}, u32[]{:S(2)}, u32[]{:S(2)}) async-start(f32[12,1,1024]{2,1,0:T(1,128)} %reshape.47), calls=%async_computation | async-start | bytes 98304 | tf_op jit(solution)/shard_map/all_to_all | solution.py:55
  89.6 1.1 copy-start.2
  90.7 12.6 %copy-start.4 = (f32[4,384,64]{1,2,0:T(8,128)S(1)}, f32[4,384,64]{1,2,0:T(8,128)}, u32[]{:S(2)}) copy-start(f32[4,384,64]{1,2,0:T(8,128)} %copy.57) | copy-start | bytes 1179652
  103.6 18.8 %copy-start.7 = (f32[64,256]{1,0:T(8,128)S(1)}, f32[64,256]{1,0:T(8,128)}, u32[]{:S(2)}) copy-start(f32[64,256]{1,0:T(8,128)} %param.7) | copy-start | bytes 196612
  105.1 13.6 %collective-permute-start.7 = (f32[4,64,32]{2,1,0:T(8,128)S(1)}, f32[4,64,32]{2,1,0:T(8,128)S(1)}, u32[]{:S(2)}, u32[]{:S(2)}) collective-permute-start(f32[4,64,32]{2,1,0:T(8,128)S(1)} %fusion.15), channel_id=1, source_target_pairs={{192,0},{196,4},{200,8},{204,12},{208,16},{212,20},{216,24},{220,2... | collective-permute-start | bytes 98312 | tf_op jit(solution)/shard_map/ppermute | solution.py:14
  106.4 12.3 %collective-permute-start.6 = (f32[4,64,32]{2,1,0:T(8,128)S(1)}, f32[4,64,32]{2,1,0:T(8,128)S(1)}, u32[]{:S(2)}, u32[]{:S(2)}) collective-permute-start(f32[4,64,32]{2,1,0:T(8,128)S(1)} %fusion.12), channel_id=1, source_target_pairs={{0,192},{4,196},{8,200},{12,204},{16,208},{20,212},{24,216},{28,22... | collective-permute-start | bytes 98312 | tf_op jit(solution)/shard_map/ppermute | solution.py:14
  111.3 8.2 %collective-permute-start.5 = (f32[4,64,32]{2,1,0:T(8,128)S(1)}, f32[4,64,32]{2,1,0:T(8,128)}, u32[]{:S(2)}, u32[]{:S(2)}) collective-permute-start(f32[4,64,32]{2,1,0:T(8,128)S(1)} %fusion.9), channel_id=1, source_target_pairs={{4,0},{8,4},{12,8},{16,12},{20,16},{24,20},{28,24},{32,28},{36,32}... | collective-permute-start | bytes 98312 | tf_op jit(solution)/shard_map/ppermute | solution.py:14
  116.6 4.0 %collective-permute-start.4 = (f32[4,64,32]{2,1,0:T(8,128)S(1)}, f32[4,64,32]{2,1,0:T(8,128)}, u32[]{:S(2)}, u32[]{:S(2)}) collective-permute-start(f32[4,64,32]{2,1,0:T(8,128)S(1)} %fusion.6), channel_id=1, source_target_pairs={{0,4},{4,8},{8,12},{12,16},{16,20},{20,24},{24,28},{28,32},{32,36}... | collective-permute-start | bytes 98312 | tf_op jit(solution)/shard_map/ppermute | solution.py:14
  124.9 30.9 %copy-start.6 = (f32[64,256]{1,0:T(8,128)}, f32[64,256]{1,0:T(8,128)S(1)}, u32[]{:S(2)}) copy-start(f32[64,256]{1,0:T(8,128)S(1)} %fusion.3) | copy-start | bytes 196612
  136.6 16.1 %collective-permute-start.11 = (f32[4,64,32]{2,1,0:T(8,128)S(1)}, f32[4,64,32]{2,1,0:T(8,128)S(1)}, u32[]{:S(2)}, u32[]{:S(2)}) collective-permute-start(f32[4,64,32]{2,1,0:T(8,128)S(1)} %fusion.14), channel_id=1, source_target_pairs={{192,0},{196,4},{200,8},{204,12},{208,16},{212,20},{216,24},{220,2... | collective-permute-start | bytes 98312 | tf_op jit(solution)/shard_map/ppermute | solution.py:14
  137.9 14.8 %collective-permute-start.10 = (f32[4,64,32]{2,1,0:T(8,128)S(1)}, f32[4,64,32]{2,1,0:T(8,128)S(1)}, u32[]{:S(2)}, u32[]{:S(2)}) collective-permute-start(f32[4,64,32]{2,1,0:T(8,128)S(1)} %fusion.11), channel_id=1, source_target_pairs={{0,192},{4,196},{8,200},{12,204},{16,208},{20,212},{24,216},{28,22... | collective-permute-start | bytes 98312 | tf_op jit(solution)/shard_map/ppermute | solution.py:14
  142.8 9.9 %collective-permute-start.9 = (f32[4,64,32]{2,1,0:T(8,128)S(1)}, f32[4,64,32]{2,1,0:T(8,128)S(1)}, u32[]{:S(2)}, u32[]{:S(2)}) collective-permute-start(f32[4,64,32]{2,1,0:T(8,128)S(1)} %fusion.8), channel_id=1, source_target_pairs={{4,0},{8,4},{12,8},{16,12},{20,16},{24,20},{28,24},{32,28},{36,32}... | collective-permute-start | bytes 98312 | tf_op jit(solution)/shard_map/ppermute | solution.py:14
  150.8 3.9 %collective-permute-start.8 = (f32[4,64,32]{2,1,0:T(8,128)S(1)}, f32[4,64,32]{2,1,0:T(8,128)}, u32[]{:S(2)}, u32[]{:S(2)}) collective-permute-start(f32[4,64,32]{2,1,0:T(8,128)S(1)} %fusion.5), channel_id=1, source_target_pairs={{0,4},{4,8},{8,12},{12,16},{16,20},{20,24},{24,28},{28,32},{32,36}... | collective-permute-start | bytes 98312 | tf_op jit(solution)/shard_map/ppermute | solution.py:14
  152.7 0.7 copy-start.8
  153.4 0.6 copy-start.9
  157.1 14.9 %all-to-all-start.1 = ((f32[12,1,1024]{2,1,0:T(1,128)}), f32[12,1,1024]{2,1,0:T(1,128)S(1)}, u32[]{:S(2)}, u32[]{:S(2)}) async-start(f32[12,1,1024]{2,1,0:T(1,128)} %reshape.49), calls=%async_computation.1 | async-start | bytes 98304 | tf_op jit(solution)/shard_map/all_to_all | solution.py:55
  199.4 1.1 copy-start.3
  199.6 13.1 %slice-start.1 = ((f32[4,384,64]{1,2,0:T(8,128)}), f32[4,256,64]{1,2,0:T(8,128)S(1)}, s32[]{:S(2)}) async-start(f32[4,384,64]{1,2,0:T(8,128)} %copy.57), calls=%async_computation.3 | async-start | bytes 524288 | tf_op jit(solution)/shard_map/slice | solution.py:39

commit v7 on v6

--- a/solution.py
+++ b/solution.py
@@ -43,10 +43,18 @@
     rows = jnp.arange(own_width, dtype=jnp.int32)
 
     def ext_of(own_all, got):
-        return jnp.concatenate([own_all] + got, axis=2)
+        return (own_all, got)
+
+    def contract(part, rows_of):
+        return lax.dot_general(part, rows_of, (((0, 2), (0, 1)), ((), ())), precision=HIGH)
 
     def apply(ext, blocks):
-        return lax.dot_general(ext, blocks, (((0, 2), (0, 1)), ((), ())), precision=HIGH)
+        own_all, got = ext
+        total = contract(own_all, blocks[:, :own_width])
+        for n in range(n_nb):
+            low = own_width + n * halo_slots
+            total = total + contract(got[n], blocks[:, low : low + halo_slots])
+        return total
 
     def coarse_partial(ext):
         coeff = apply(ext, basis_blocks)

time: 216 us -> 229 us (1.060)
  matrix products: 18.5 us -> 29.3 us
  blocking collectives: 93.5 us -> 90 us
  local copies, waits for them, and re-layouts: 11.2 us -> 13.6 us
    dot_general x5 -> x25, matrix products: 5.83 us -> 15.9 us  [contract(): lax.dot_general(part, rows_of, (((0, 2), (0, 1)), ((), ())), precision=HIGH)]
    ppermute x12, waiting for transfers between devices: 3.79 us -> 9.73 us  [passed_along(): return lax.ppermute(block, SUB, route)]
    all_to_all x2, waiting for transfers between devices: 18.2 us -> 13.4 us  [coarse_partial(): g = lax.all_to_all(spread, 'z', 0, 0, tiled=True)]
    concatenate x3 -> x0, local copies, waits for them, and re-layouts: 4.27 us -> none  [ext_of(): return jnp.concatenate([own_all] + got, axis=2)]
    slice x4 -> x2, local copies, waits for them, and re-layouts: 0.01 us -> 3.16 us  [the longest x1 2.2 us: apply(): total = total + contract(got[n], blocks[:, low:low + halo_slots])]
    all_gather x2, blocking collectives: 53.2 us -> 50.1 us  [coarse_partial(): g = lax.all_gather(g[None], ('y', 'core'), axis=0, tiled=True)]
    unnamed x25 -> x32, local copies, waits for them, and re-layouts: 4.81 us -> 7.27 us
  transfers between devices with their start and end apart: 14 -> 14, of which waited for: 6 -> 4; matrix products, arithmetic and copies ran while one was open for 2% -> 11% of each run, Pallas kernels for 0% -> 0%
where the time goes in v7:
time: 229 us; the launch traced here: 225 us
  blocking collectives  90 us (39%)
  starting transfers between devices  63.3 us (28%)
  matrix products  29.3 us (13%)
  waiting for transfers between devices  23.1 us (10%)
  local copies, waits for them, and re-layouts  13.6 us (6%)
  other arithmetic  4.9 us (2%)
    all_gather x2, blocking collectives, coarse_partial(): g = lax.all_gather(g[None], ('y', 'core'), axis=0, tiled=True)  50.1 us
    ppermute x12, starting transfers between devices, passed_along(): return lax.ppermute(block, SUB, route)  47.7 us
    dot_general x25, matrix products, contract(): lax.dot_general(part, rows_of, (((0, 2), (0, 1)), ((), ())), precision=HIGH)  15.9 us
    all_to_all x2, starting transfers between devices, coarse_partial(): g = lax.all_to_all(spread, 'z', 0, 0, tiled=True)  15.6 us
    all_to_all x2, waiting for transfers between devices, coarse_partial(): g = lax.all_to_all(spread, 'z', 0, 0, tiled=True)  13.4 us
    all_gather x1, blocking collectives, body(): lax.all_gather(jnp.concatenate([right_sides, index_row], axis=0)[None], '...  10.6 us
    all_gather x1, blocking collectives, body(): lax.all_gather(jnp.concatenate([local_1, partial_1.T], axis=1)[None], 'co...  10.5 us
    ppermute x12, waiting for transfers between devices, passed_along(): return lax.ppermute(block, SUB, route)  9.73 us
  transfers between devices with their start and end apart: 14, of which 4 were waited for; matrix products, arithmetic and copies ran while one was open for 11% of the time, Pallas kernels for 0%

profile of v7, /device:TPU:1, one launch (start us, length us, event | category | flops | bytes accessed | tf_op | source)
XLA Modules:
  0.0 225.5 jit_solution(17022645914461146353)
XLA Ops:
  3.1 10.6 %all-gather.6 = f32[4,65,256]{2,1,0:T(8,128)S(1)} all-gather(f32[1,65,256]{2,1,0:T(8,128)S(1)} %maximum_bitcast_fusion), channel_id=2, replica_groups=mesh['y'=8,'z'=12,'core'=2,'col'=4] {'col'}, dimensions={0}, use_global_device_ids=true | all-gather | bytes 332800 | tf_op jit(solution)/shard_map/all_gather | solution.py:76
  15.1 7.4 %collective-permute-start = (f32[4,64,32]{1,2,0:T(8,128)}, f32[4,64,32]{1,2,0:T(8,128)S(1)}, u32[]{:S(2)}, u32[]{:S(2)}) collective-permute-start(f32[4,64,32]{1,2,0:T(8,128)} %fusion.27), channel_id=1, source_target_pairs={{0,4},{4,8},{8,12},{12,16},{16,20},{20,24},{24,28},{28,32},{32,36}... | collective-permute-start | bytes 98312 | tf_op jit(solution)/shard_map/ppermute | solution.py:14
  23.6 8.1 %collective-permute-start.1 = (f32[4,64,32]{1,2,0:T(8,128)}, f32[4,64,32]{1,2,0:T(8,128)}, u32[]{:S(2)}, u32[]{:S(2)}) collective-permute-start(f32[4,64,32]{1,2,0:T(8,128)} %fusion.25), channel_id=1, source_target_pairs={{4,0},{8,4},{12,8},{16,12},{20,16},{24,20},{28,24},{32,28},{36,32}... | collective-permute-start | bytes 98312 | tf_op jit(solution)/shard_map/ppermute | solution.py:14
  32.6 1.9 collective-permute-start.2
  35.5 1.3 collective-permute-start.3
  36.8 1.9 reshape_squeeze.11
  39.7 2.2 fusion.61
  41.9 1.3 convolution_bitcast_fusion.15
  52.7 10.9 %all-to-all-start = ((f32[12,1,1024]{2,1,0:T(1,128)}), f32[12,1,1024]{2,1,0:T(1,128)S(1)}, u32[]{:S(2)}, u32[]{:S(2)}) async-start(f32[12,1,1024]{2,1,0:T(1,128)} %reshape.67), calls=%async_computation | async-start | bytes 98304 | tf_op jit(solution)/shard_map/all_to_all | solution.py:63
  65.8 1.1 fusion.9
  67.0 1.8 fusion.10
  68.7 4.5 %all-to-all-done = f32[12,1,1024]{2,1,0:T(1,128)S(1)} async-done(((f32[12,1,1024]{2,1,0:T(1,128)}), f32[12,1,1024]{2,1,0:T(1,128)S(1)}, u32[]{:S(2)}, u32[]{:S(2)}) %all-to-all-start) | async-done | bytes 49184 | tf_op jit(solution)/shard_map/all_to_all | solution.py:63
  73.9 1.4 reduce
  76.2 25.2 %all-gather.1 = f32[192,16,64]{2,1,0:T(8,128)S(1)} all-gather(f32[12,16,64]{2,1,0:T(8,128)S(1)} %reshape.68), channel_id=3, replica_groups=mesh['y'=8,'z'=12,'core'=2,'col'=4] {'y','core'}, dimensions={0}, use_global_device_ids=true | all-gather | bytes 835584 | tf_op jit(solution)/shard_map/all_gather | solution.py:64
  101.7 2.6 %fusion.62 = f32[64,64]{1,0:T(8,128)S(1)} fusion(f32[3072,64]{1,0:T(8,128)S(1)} %bitcast.200, f32[64,3072]{1,0:T(8,128)S(1)} %copy-done), kind=kOutput, calls=%fused_computation.110 | convolution fusion | flops 150994944 | bytes 1589248 | tf_op jit(solution)/shard_map/dot_general | solution.py:67
  104.3 10.5 %all-gather.2 = f32[256,320]{1,0:T(8,128)S(1)} all-gather(f32[64,320]{1,0:T(8,128)S(1)} %pad_maximum_fusion), channel_id=4, replica_groups=mesh['y'=8,'z'=12,'core'=2,'col'=4] {'col'}, dimensions={0}, use_global_device_ids=true | all-gather | bytes 409600 | tf_op jit(solution)/shard_map/all_gather | solution.py:104
  116.7 4.4 %collective-permute-start.4 = (f32[4,64,32]{1,2,0:T(8,128)S(1)}, f32[4,64,32]{1,2,0:T(8,128)S(1)}, u32[]{:S(2)}, u32[]{:S(2)}) collective-permute-start(f32[4,64,32]{1,2,0:T(8,128)S(1)} %fusion.43), channel_id=1, source_target_pairs={{0,4},{4,8},{8,12},{12,16},{16,20},{20,24},{24,28},{28,32},{32,36}... | collective-permute-start | bytes 98312 | tf_op jit(solution)/shard_map/ppermute | solution.py:14
  121.7 1.9 collective-permute-start.5
  123.6 2.3 %collective-permute-start.6 = (f32[4,64,32]{1,2,0:T(8,128)S(1)}, f32[4,64,32]{1,2,0:T(8,128)S(1)}, u32[]{:S(2)}, u32[]{:S(2)}) collective-permute-start(f32[4,64,32]{1,2,0:T(8,128)S(1)} %fusion.47), channel_id=1, source_target_pairs={{0,192},{4,196},{8,200},{12,204},{16,208},{20,212},{24,216},{28,22... | collective-permute-start | bytes 98312 | tf_op jit(solution)/shard_map/ppermute | solution.py:14
  126.0 1.3 collective-permute-start.7
  127.8 6.0 %collective-permute-done.7 = f32[4,64,32]{1,2,0:T(8,128)S(1)} collective-permute-done((f32[4,64,32]{1,2,0:T(8,128)S(1)}, f32[4,64,32]{1,2,0:T(8,128)S(1)}, u32[]{:S(2)}, u32[]{:S(2)}) %collective-permute-start.7) | collective-permute-done | bytes 32800 | tf_op jit(solution)/shard_map/ppermute | solution.py:14
  134.4 9.6 %all-gather.3 = f32[256,256]{1,0:T(8,128)S(1)} all-gather(f32[64,256]{1,0:T(8,128)S(1)} %fusion.12), channel_id=5, replica_groups=mesh['y'=8,'z'=12,'core'=2,'col'=4] {'col'}, dimensions={0}, use_global_device_ids=true | all-gather | bytes 327680 | tf_op jit(solution)/shard_map/all_gather | solution.py:117
  146.1 7.6 %collective-permute-start.8 = (f32[4,64,32]{1,2,0:T(8,128)S(1)}, f32[4,64,32]{1,2,0:T(8,128)S(1)}, u32[]{:S(2)}, u32[]{:S(2)}) collective-permute-start(f32[4,64,32]{1,2,0:T(8,128)S(1)} %fusion.42), channel_id=1, source_target_pairs={{0,4},{4,8},{8,12},{12,16},{16,20},{20,24},{24,28},{28,32},{32,36}... | collective-permute-start | bytes 98312 | tf_op jit(solution)/shard_map/ppermute | solution.py:14
  154.1 3.9 %collective-permute-start.9 = (f32[4,64,32]{1,2,0:T(8,128)S(1)}, f32[4,64,32]{1,2,0:T(8,128)S(1)}, u32[]{:S(2)}, u32[]{:S(2)}) collective-permute-start(f32[4,64,32]{1,2,0:T(8,128)S(1)} %fusion.44), channel_id=1, source_target_pairs={{4,0},{8,4},{12,8},{16,12},{20,16},{24,20},{28,24},{32,28},{36,32}... | collective-permute-start | bytes 98312 | tf_op jit(solution)/shard_map/ppermute | solution.py:14
  157.9 6.4 %collective-permute-start.10 = (f32[4,64,32]{1,2,0:T(8,128)S(1)}, f32[4,64,32]{1,2,0:T(8,128)S(1)}, u32[]{:S(2)}, u32[]{:S(2)}) collective-permute-start(f32[4,64,32]{1,2,0:T(8,128)S(1)} %fusion.46), channel_id=1, source_target_pairs={{0,192},{4,196},{8,200},{12,204},{16,208},{20,212},{24,216},{28,22... | collective-permute-start | bytes 98312 | tf_op jit(solution)/shard_map/ppermute | solution.py:14
  164.3 1.3 collective-permute-start.11
  166.5 3.7 %collective-permute-done.11 = f32[4,64,32]{1,2,0:T(8,128)S(1)} collective-permute-done((f32[4,64,32]{1,2,0:T(8,128)S(1)}, f32[4,64,32]{1,2,0:T(8,128)S(1)}, u32[]{:S(2)}, u32[]{:S(2)}) %collective-permute-start.11) | collective-permute-done | bytes 32800 | tf_op jit(solution)/shard_map/ppermute | solution.py:14
  171.3 4.7 %all-to-all-start.1 = ((f32[12,1,1024]{2,1,0:T(1,128)}), f32[12,1,1024]{2,1,0:T(1,128)S(1)}, u32[]{:S(2)}, u32[]{:S(2)}) async-start(f32[12,1,1024]{2,1,0:T(1,128)} %reshape.69), calls=%async_computation.1 | async-start | bytes 98304 | tf_op jit(solution)/shard_map/all_to_all | solution.py:63
  176.9 8.8 %all-to-all-done.1 = f32[12,1,1024]{2,1,0:T(1,128)S(1)} async-done(((f32[12,1,1024]{2,1,0:T(1,128)}), f32[12,1,1024]{2,1,0:T(1,128)S(1)}, u32[]{:S(2)}, u32[]{:S(2)}) %all-to-all-start.1) | async-done | bytes 49184 | tf_op jit(solution)/shard_map/all_to_all | solution.py:63
  186.6 24.8 %all-gather.4 = f32[192,16,64]{2,1,0:T(8,128)S(1)} all-gather(f32[12,16,64]{2,1,0:T(8,128)S(1)} %reshape.70), channel_id=6, replica_groups=mesh['y'=8,'z'=12,'core'=2,'col'=4] {'y','core'}, dimensions={0}, use_global_device_ids=true | all-gather | bytes 835584 | tf_op jit(solution)/shard_map/all_gather | solution.py:64
  211.6 2.6 %fusion.63 = f32[64,64]{1,0:T(8,128)S(1)} fusion(f32[3072,64]{1,0:T(8,128)S(1)} %bitcast.202, f32[64,3072]{1,0:T(8,128)S(1)} %copy-done), kind=kOutput, calls=%fused_computation.111 | convolution fusion | flops 150994944 | bytes 1589248 | tf_op jit(solution)/shard_map/dot_general | solution.py:67
  214.3 9.2 %all-gather.5 = f32[256,64]{1,0:T(8,128)S(1)} all-gather(f32[64,64]{1,0:T(8,128)S(1)} %fusion.63), channel_id=7, replica_groups=mesh['y'=8,'z'=12,'core'=2,'col'=4] {'col'}, dimensions={0}, use_global_device_ids=true | all-gather | bytes 81920 | tf_op jit(solution)/shard_map/all_gather | solution.py:122
  (104 shorter events, 32.9 us)
Async XLA Ops:
  0.6 101.0 %copy-start = (f32[64,3072]{1,0:T(8,128)S(1)}, f32[64,3072]{1,0:T(8,128)}, u32[]{:S(2)}) copy-start(f32[64,3072]{1,0:T(8,128)} %param.11) | copy-start | bytes 2359300
  15.1 33.1 %collective-permute-start = (f32[4,64,32]{1,2,0:T(8,128)}, f32[4,64,32]{1,2,0:T(8,128)S(1)}, u32[]{:S(2)}, u32[]{:S(2)}) collective-permute-start(f32[4,64,32]{1,2,0:T(8,128)} %fusion.27), channel_id=1, source_target_pairs={{0,4},{4,8},{8,12},{12,16},{16,20},{20,24},{24,28},{28,32},{32,36}... | collective-permute-start | bytes 98312 | tf_op jit(solution)/shard_map/ppermute | solution.py:14
  23.6 18.3 %copy-start.1 = (f32[1,1536,256]{2,1,0:T(8,128)S(1)}, f32[1,1536,256]{2,1,0:T(8,128)}, u32[]{:S(2)}) copy-start(f32[1,1536,256]{2,1,0:T(8,128)} %param.9) | copy-start | bytes 4718596
  23.6 25.0 %collective-permute-start.1 = (f32[4,64,32]{1,2,0:T(8,128)}, f32[4,64,32]{1,2,0:T(8,128)}, u32[]{:S(2)}, u32[]{:S(2)}) collective-permute-start(f32[4,64,32]{1,2,0:T(8,128)} %fusion.25), channel_id=1, source_target_pairs={{4,0},{8,4},{12,8},{16,12},{20,16},{24,20},{28,24},{32,28},{36,32}... | collective-permute-start | bytes 98312 | tf_op jit(solution)/shard_map/ppermute | solution.py:14
  32.6 17.1 %collective-permute-start.2 = (f32[4,64,32]{1,2,0:T(8,128)}, f32[4,64,32]{1,2,0:T(8,128)}, u32[]{:S(2)}, u32[]{:S(2)}) collective-permute-start(f32[4,64,32]{1,2,0:T(8,128)} %fusion.23), channel_id=1, source_target_pairs={{0,192},{4,196},{8,200},{12,204},{16,208},{20,212},{24,216},{28,22... | collective-permute-start | bytes 98312 | tf_op jit(solution)/shard_map/ppermute | solution.py:14
  35.5 15.3 %collective-permute-start.3 = (f32[4,64,32]{1,2,0:T(8,128)}, f32[4,64,32]{1,2,0:T(8,128)}, u32[]{:S(2)}, u32[]{:S(2)}) collective-permute-start(f32[4,64,32]{1,2,0:T(8,128)} %fusion.21), channel_id=1, source_target_pairs={{192,0},{196,4},{200,8},{204,12},{208,16},{212,20},{216,24},{220,2... | collective-permute-start | bytes 98312 | tf_op jit(solution)/shard_map/ppermute | solution.py:14
  45.2 31.0 %copy-start.5 = (f32[4,32,64]{2,1,0:T(8,128)}, f32[4,32,64]{2,1,0:T(8,128)S(1)}, u32[]{:S(2)}) copy-start(f32[4,32,64]{2,1,0:T(8,128)S(1)} %copy.46) | copy-start | bytes 98308
  46.2 55.2 %copy-start.3 = (f32[4,32,64]{2,1,0:T(8,128)}, f32[4,32,64]{2,1,0:T(8,128)S(1)}, u32[]{:S(2)}) copy-start(f32[4,32,64]{2,1,0:T(8,128)S(1)} %copy.47) | copy-start | bytes 98308
  48.3 3.7 %copy-start.8 = (f32[4,64,32]{1,2,0:T(8,128)}, f32[4,64,32]{1,2,0:T(8,128)S(1)}, u32[]{:S(2)}) copy-start(f32[4,64,32]{1,2,0:T(8,128)S(1)} %collective-permute-done) | copy-start | bytes 98308
  52.7 20.6 %all-to-all-start = ((f32[12,1,1024]{2,1,0:T(1,128)}), f32[12,1,1024]{2,1,0:T(1,128)S(1)}, u32[]{:S(2)}, u32[]{:S(2)}) async-start(f32[12,1,1024]{2,1,0:T(1,128)} %reshape.67), calls=%async_computation | async-start | bytes 98304 | tf_op jit(solution)/shard_map/all_to_all | solution.py:63
  101.6 2.7 %copy-start.7 = (f32[64,256]{1,0:T(8,128)S(1)}, f32[64,256]{1,0:T(8,128)}, u32[]{:S(2)}) copy-start(f32[64,256]{1,0:T(8,128)} %fusion.10) | copy-start | bytes 196612
  104.3 16.7 %copy-start.2 = (f32[1,1536,256]{2,1,0:T(8,128)S(1)}, f32[1,1536,256]{2,1,0:T(8,128)}, u32[]{:S(2)}) copy-start(f32[1,1536,256]{2,1,0:T(8,128)} %param.8) | copy-start | bytes 4718596
  116.0 18.1 %copy-start.10 = (f32[64,256]{1,0:T(8,128)S(1)}, f32[64,256]{1,0:T(8,128)}, u32[]{:S(2)}) copy-start(f32[64,256]{1,0:T(8,128)} %param.7) | copy-start | bytes 196612
  116.7 10.6 %collective-permute-start.4 = (f32[4,64,32]{1,2,0:T(8,128)S(1)}, f32[4,64,32]{1,2,0:T(8,128)S(1)}, u32[]{:S(2)}, u32[]{:S(2)}) collective-permute-start(f32[4,64,32]{1,2,0:T(8,128)S(1)} %fusion.43), channel_id=1, source_target_pairs={{0,4},{4,8},{8,12},{12,16},{16,20},{20,24},{24,28},{28,32},{32,36}... | collective-permute-start | bytes 98312 | tf_op jit(solution)/shard_map/ppermute | solution.py:14
  121.7 12.4 %collective-permute-start.5 = (f32[4,64,32]{1,2,0:T(8,128)S(1)}, f32[4,64,32]{1,2,0:T(8,128)S(1)}, u32[]{:S(2)}, u32[]{:S(2)}) collective-permute-start(f32[4,64,32]{1,2,0:T(8,128)S(1)} %fusion.45), channel_id=1, source_target_pairs={{4,0},{8,4},{12,8},{16,12},{20,16},{24,20},{28,24},{32,28},{36,32}... | collective-permute-start | bytes 98312 | tf_op jit(solution)/shard_map/ppermute | solution.py:14
  123.6 3.9 %collective-permute-start.6 = (f32[4,64,32]{1,2,0:T(8,128)S(1)}, f32[4,64,32]{1,2,0:T(8,128)S(1)}, u32[]{:S(2)}, u32[]{:S(2)}) collective-permute-start(f32[4,64,32]{1,2,0:T(8,128)S(1)} %fusion.47), channel_id=1, source_target_pairs={{0,192},{4,196},{8,200},{12,204},{16,208},{20,212},{24,216},{28,22... | collective-permute-start | bytes 98312 | tf_op jit(solution)/shard_map/ppermute | solution.py:14
  126.0 7.9 %collective-permute-start.7 = (f32[4,64,32]{1,2,0:T(8,128)S(1)}, f32[4,64,32]{1,2,0:T(8,128)S(1)}, u32[]{:S(2)}, u32[]{:S(2)}) collective-permute-start(f32[4,64,32]{1,2,0:T(8,128)S(1)} %fusion.49), channel_id=1, source_target_pairs={{192,0},{196,4},{200,8},{204,12},{208,16},{212,20},{216,24},{220,2... | collective-permute-start | bytes 98312 | tf_op jit(solution)/shard_map/ppermute | solution.py:14
  134.4 10.0 %copy-start.9 = (f32[64,256]{1,0:T(8,128)}, f32[64,256]{1,0:T(8,128)S(1)}, u32[]{:S(2)}) copy-start(f32[64,256]{1,0:T(8,128)S(1)} %fusion.12) | copy-start | bytes 196612
  144.4 21.2 %copy-start.6 = (f32[4,32,64]{2,1,0:T(8,128)S(1)}, f32[4,32,64]{2,1,0:T(8,128)}, u32[]{:S(2)}) copy-start(f32[4,32,64]{2,1,0:T(8,128)} %copy-done.5) | copy-start | bytes 98308
  144.8 21.2 %copy-start.4 = (f32[4,32,64]{2,1,0:T(8,128)S(1)}, f32[4,32,64]{2,1,0:T(8,128)}, u32[]{:S(2)}) copy-start(f32[4,32,64]{2,1,0:T(8,128)} %copy-done.3) | copy-start | bytes 98308
  146.1 19.5 %collective-permute-start.8 = (f32[4,64,32]{1,2,0:T(8,128)S(1)}, f32[4,64,32]{1,2,0:T(8,128)S(1)}, u32[]{:S(2)}, u32[]{:S(2)}) collective-permute-start(f32[4,64,32]{1,2,0:T(8,128)S(1)} %fusion.42), channel_id=1, source_target_pairs={{0,4},{4,8},{8,12},{12,16},{16,20},{20,24},{24,28},{28,32},{32,36}... | collective-permute-start | bytes 98312 | tf_op jit(solution)/shard_map/ppermute | solution.py:14
  154.1 11.9 %collective-permute-start.9 = (f32[4,64,32]{1,2,0:T(8,128)S(1)}, f32[4,64,32]{1,2,0:T(8,128)S(1)}, u32[]{:S(2)}, u32[]{:S(2)}) collective-permute-start(f32[4,64,32]{1,2,0:T(8,128)S(1)} %fusion.44), channel_id=1, source_target_pairs={{4,0},{8,4},{12,8},{16,12},{20,16},{24,20},{28,24},{32,28},{36,32}... | collective-permute-start | bytes 98312 | tf_op jit(solution)/shard_map/ppermute | solution.py:14
  157.9 8.3 %collective-permute-start.10 = (f32[4,64,32]{1,2,0:T(8,128)S(1)}, f32[4,64,32]{1,2,0:T(8,128)S(1)}, u32[]{:S(2)}, u32[]{:S(2)}) collective-permute-start(f32[4,64,32]{1,2,0:T(8,128)S(1)} %fusion.46), channel_id=1, source_target_pairs={{0,192},{4,196},{8,200},{12,204},{16,208},{20,212},{24,216},{28,22... | collective-permute-start | bytes 98312 | tf_op jit(solution)/shard_map/ppermute | solution.py:14
  164.3 5.9 %collective-permute-start.11 = (f32[4,64,32]{1,2,0:T(8,128)S(1)}, f32[4,64,32]{1,2,0:T(8,128)S(1)}, u32[]{:S(2)}, u32[]{:S(2)}) collective-permute-start(f32[4,64,32]{1,2,0:T(8,128)S(1)} %fusion.48), channel_id=1, source_target_pairs={{192,0},{196,4},{200,8},{204,12},{208,16},{212,20},{216,24},{220,2... | collective-permute-start | bytes 98312 | tf_op jit(solution)/shard_map/ppermute | solution.py:14
  171.3 14.4 %all-to-all-start.1 = ((f32[12,1,1024]{2,1,0:T(1,128)}), f32[12,1,1024]{2,1,0:T(1,128)S(1)}, u32[]{:S(2)}, u32[]{:S(2)}) async-start(f32[12,1,1024]{2,1,0:T(1,128)} %reshape.69), calls=%async_computation.1 | async-start | bytes 98304 | tf_op jit(solution)/shard_map/all_to_all | solution.py:63

commit v8 on v6

--- a/solution.py
+++ b/solution.py
@@ -42,6 +42,10 @@
     own_basis = lax.dynamic_index_in_dim(own_basis_all, column_index, 0, keepdims=False)
     rows = jnp.arange(own_width, dtype=jnp.int32)
 
+    def col_gather(part):
+        spread = jnp.broadcast_to(part, (n_col,) + part.shape[1:])
+        return lax.all_to_all(spread, "col", 0, 0, tiled=True)
+
     def ext_of(own_all, got):
         return jnp.concatenate([own_all] + got, axis=2)
 
@@ -65,9 +69,7 @@
             jnp.zeros((own_width - n_nb * halo_slots - n_nb,), jnp.float32),
         ]
     )[None]
-    g0 = lax.all_gather(
-        jnp.concatenate([right_sides, index_row], axis=0)[None], "col", axis=0, tiled=True
-    )
+    g0 = col_gather(jnp.concatenate([right_sides, index_row], axis=0)[None])
     own_b_all = g0[:, :rhs_width]
     idx = g0[:, rhs_width]
     send_all = idx[:, : n_nb * halo_slots].astype(jnp.int32).reshape(n_col, n_nb, halo_slots)
@@ -93,9 +95,7 @@
 
     local_1 = apply(ext_b, inverse_rows)
     partial_1 = coarse_partial(ext_b)
-    g = lax.all_gather(
-        jnp.concatenate([local_1, partial_1.T], axis=1)[None], "col", axis=0, tiled=True
-    )
+    g = col_gather(jnp.concatenate([local_1, partial_1.T], axis=1)[None])
     local_all = g[:, :, :own_width]
     coarse_1 = jnp.sum(g[:, :, own_width:], axis=0)
     coarse_part_all = jnp.einsum("rm,com->cro", coarse_1, own_basis_all, precision=HIGH)
@@ -106,12 +106,12 @@
     residual = right_sides - applied
     first_pass = lax.dynamic_index_in_dim(first_all, column_index, 0, keepdims=False)
 
-    res_all = lax.all_gather(residual[None], "col", axis=0, tiled=True)
+    res_all = col_gather(residual[None])
     got_res = margins_sent(res_all)
     ext_r = ext_of(res_all, got_res)
     local_2 = apply(ext_r, inverse_rows)
     partial_2 = coarse_partial(ext_r)
-    g2 = lax.all_gather(partial_2.T[None], "col", axis=0, tiled=True)
+    g2 = col_gather(partial_2.T[None])
     coarse_2 = jnp.sum(g2, axis=0)
     coarse_part_2 = lax.dot_general(
         coarse_2, own_basis, (((1,), (1,)), ((), ())), precision=HIGH

time: 216 us -> 210 us (0.972)
  blocking collectives: 93.5 us -> 87.2 us
  waiting for transfers between devices: 22 us -> 25.6 us
  starting transfers between devices: 64.2 us -> 61.2 us
    all_gather x4 -> x0, blocking collectives: 40.3 us -> none  [the longest x1 10.6 us: body(): lax.all_gather(jnp.concatenate([right_sides, index_row], axis=0)[None], '...]
    all_to_all x0 -> x3, blocking collectives: none -> 34.2 us  [the longest x2 19.2 us: col_gather(): return lax.all_to_all(spread, 'col', 0, 0, tiled=True)]
    all_to_all x0 -> x2, waiting for transfers between devices: none -> 12.4 us  [col_gather(): return lax.all_to_all(spread, 'col', 0, 0, tiled=True)]
    all_to_all x2 -> x1, waiting for transfers between devices: 18.2 us -> 8.77 us  [coarse_partial(): g = lax.all_to_all(spread, 'z', 0, 0, tiled=True)]
    all_to_all x0 -> x2, starting transfers between devices: none -> 6.74 us  [col_gather(): return lax.all_to_all(spread, 'col', 0, 0, tiled=True)]
    ppermute x12, starting transfers between devices: 48.2 us -> 42.4 us  [passed_along(): return lax.ppermute(block, SUB, route)]
    all_to_all x2 -> x1, starting transfers between devices: 16 us -> 12.1 us  [coarse_partial(): g = lax.all_to_all(spread, 'z', 0, 0, tiled=True)]
  transfers between devices with their start and end apart: 14 -> 15, of which waited for: 6 -> 7; matrix products, arithmetic and copies ran while one was open for 2% -> 2% of each run, Pallas kernels for 0% -> 0%
where the time goes in v8:
time: 210 us; the launch traced here: 209 us
  blocking collectives  87.2 us (42%)
  starting transfers between devices  61.2 us (29%)
  waiting for transfers between devices  25.6 us (12%)
  matrix products  18.4 us (9%)
  local copies, waits for them, and re-layouts  11 us (5%)
  other arithmetic  4.96 us (2%)
    all_gather x2, blocking collectives, coarse_partial(): g = lax.all_gather(g[None], ('y', 'core'), axis=0, tiled=True)  53 us
    ppermute x12, starting transfers between devices, passed_along(): return lax.ppermute(block, SUB, route)  42.4 us
    all_to_all x2, blocking collectives, col_gather(): return lax.all_to_all(spread, 'col', 0, 0, tiled=True)  19.2 us
    all_to_all x1, blocking collectives, coarse_partial(): g = lax.all_to_all(spread, 'z', 0, 0, tiled=True)  15 us
    all_to_all x2, waiting for transfers between devices, col_gather(): return lax.all_to_all(spread, 'col', 0, 0, tiled=True)  12.4 us
    all_to_all x1, starting transfers between devices, coarse_partial(): g = lax.all_to_all(spread, 'z', 0, 0, tiled=True)  12.1 us
    all_to_all x1, waiting for transfers between devices, coarse_partial(): g = lax.all_to_all(spread, 'z', 0, 0, tiled=True)  8.77 us
    dot_general x12, matrix products, margins_sent(): lax.dot_general(field_all, select_all[:, :, n], (((2,), (1,)), ((0,), (0,...  6.83 us
  transfers between devices with their start and end apart: 15, of which 7 were waited for; matrix products, arithmetic and copies ran while one was open for 2% of the time, Pallas kernels for 0%

profile of v8, /device:TPU:1, one launch (start us, length us, event | category | flops | bytes accessed | tf_op | source)
XLA Modules:
  0.0 209.4 jit_solution(12128994684576718495)
XLA Ops:
  3.2 10.5 %all_to_all.30 = f32[4,65,256]{2,1,0:T(8,128)S(1)} all-to-all(f32[4,65,256]{2,1,0:T(8,128)S(1)} %broadcast_in_dim.22), channel_id=1, replica_groups=mesh['y'=8,'z'=12,'core'=2,'col'=4] {'col'}, dimensions={0} | all-to-all | bytes 532480 | tf_op jit(solution)/shard_map/all_to_all | solution.py:47
  15.1 4.4 %collective-permute-start.2 = (f32[4,64,32]{2,1,0:T(8,128)}, f32[4,64,32]{2,1,0:T(8,128)S(1)}, u32[]{:S(2)}, u32[]{:S(2)}) collective-permute-start(f32[4,64,32]{2,1,0:T(8,128)} %fusion.13), channel_id=1, source_target_pairs={{0,192},{4,196},{8,200},{12,204},{16,208},{20,212},{24,216},{28,22... | collective-permute-start | bytes 98312 | tf_op jit(solution)/shard_map/ppermute | solution.py:14
  20.5 1.3 collective-permute-start.3
  22.8 8.2 %collective-permute-start.1 = (f32[4,64,32]{2,1,0:T(8,128)}, f32[4,64,32]{2,1,0:T(8,128)}, u32[]{:S(2)}, u32[]{:S(2)}) collective-permute-start(f32[4,64,32]{2,1,0:T(8,128)} %fusion.10), channel_id=1, source_target_pairs={{4,0},{8,4},{12,8},{16,12},{20,16},{24,20},{28,24},{32,28},{36,32}... | collective-permute-start | bytes 98312 | tf_op jit(solution)/shard_map/ppermute | solution.py:14
  32.0 1.9 collective-permute-start
  34.1 2.0 collective-permute-done
  36.2 1.2 concatenate.20
  38.6 12.1 %all-to-all-start.1 = ((f32[12,1,1024]{2,1,0:T(1,128)}), f32[12,1,1024]{2,1,0:T(1,128)S(1)}, u32[]{:S(2)}, u32[]{:S(2)}) async-start(f32[12,1,1024]{2,1,0:T(1,128)} %reshape.44), calls=%async_computation.1 | async-start | bytes 98304 | tf_op jit(solution)/shard_map/all_to_all | solution.py:59
  51.6 8.8 %all-to-all-done.1 = f32[12,1,1024]{2,1,0:T(1,128)S(1)} async-done(((f32[12,1,1024]{2,1,0:T(1,128)}), f32[12,1,1024]{2,1,0:T(1,128)S(1)}, u32[]{:S(2)}, u32[]{:S(2)}) %all-to-all-start.1) | async-done | bytes 49184 | tf_op jit(solution)/shard_map/all_to_all | solution.py:59
  61.7 27.4 %all-gather = f32[192,16,64]{2,1,0:T(8,128)S(1)} all-gather(f32[12,16,64]{2,1,0:T(8,128)S(1)} %reshape.45), channel_id=2, replica_groups=mesh['y'=8,'z'=12,'core'=2,'col'=4] {'y','core'}, dimensions={0}, use_global_device_ids=true | all-gather | bytes 835584 | tf_op jit(solution)/shard_map/all_gather | solution.py:60
  90.2 2.6 %fusion.30 = f32[64,64]{1,0:T(8,128)S(1)} fusion(f32[3072,64]{1,0:T(8,128)S(1)} %bitcast.94, f32[64,3072]{1,0:T(8,128)S(1)} %copy-done.1), kind=kOutput, calls=%fused_computation.52 | convolution fusion | flops 150994944 | bytes 1589248 | tf_op jit(solution)/shard_map/dot_general | solution.py:63
  93.6 3.5 %all-to-all-start.2 = ((f32[4,64,320]{2,1,0:T(8,128)}), f32[4,64,320]{2,1,0:T(8,128)S(1)}, u32[]{:S(2)}, u32[]{:S(2)}) async-start(f32[4,64,320]{2,1,0:T(8,128)} %broadcast_in_dim.25), calls=%async_computation.2 | async-start | bytes 786432 | tf_op jit(solution)/shard_map/all_to_all | solution.py:47
  97.1 7.9 %all-to-all-done.2 = f32[4,64,320]{2,1,0:T(8,128)S(1)} async-done(((f32[4,64,320]{2,1,0:T(8,128)}), f32[4,64,320]{2,1,0:T(8,128)S(1)}, u32[]{:S(2)}, u32[]{:S(2)}) %all-to-all-start.2) | async-done | bytes 327712 | tf_op jit(solution)/shard_map/all_to_all | solution.py:47
  106.9 1.3 collective-permute-start.7
  108.2 4.9 %collective-permute-start.6 = (f32[4,64,32]{2,1,0:T(8,128)S(1)}, f32[4,64,32]{2,1,0:T(8,128)S(1)}, u32[]{:S(2)}, u32[]{:S(2)}) collective-permute-start(f32[4,64,32]{2,1,0:T(8,128)S(1)} %fusion.12), channel_id=1, source_target_pairs={{0,192},{4,196},{8,200},{12,204},{16,208},{20,212},{24,216},{28,22... | collective-permute-start | bytes 98312 | tf_op jit(solution)/shard_map/ppermute | solution.py:14
  113.1 3.5 %collective-permute-start.5 = (f32[4,64,32]{2,1,0:T(8,128)S(1)}, f32[4,64,32]{2,1,0:T(8,128)S(1)}, u32[]{:S(2)}, u32[]{:S(2)}) collective-permute-start(f32[4,64,32]{2,1,0:T(8,128)S(1)} %fusion.9), channel_id=1, source_target_pairs={{4,0},{8,4},{12,8},{16,12},{20,16},{24,20},{28,24},{32,28},{36,32}... | collective-permute-start | bytes 98312 | tf_op jit(solution)/shard_map/ppermute | solution.py:14
  116.6 2.1 collective-permute-start.4
  120.6 1.3 concatenate.22
  121.9 2.3 %fusion.3 = f32[64,256]{1,0:T(8,128)S(1)} fusion(f32[64,256]{1,0:T(8,128)} %param.7, f32[4,64,384]{2,1,0:T(8,128)S(1)} %concatenate.22, f32[4,384,256]{2,1,0:T(8,128)} %bitcast.97), kind=kOutput, calls=%fused_computation.6 | convolution fusion | flops 302006272 | bytes 2097152 | tf_op jit(solution)/shard_map/dot_general | solution.py:53
  124.3 8.7 %all_to_all.31 = f32[4,64,256]{2,1,0:T(8,128)S(1)} all-to-all(f32[4,64,256]{2,1,0:T(8,128)S(1)} %broadcast_in_dim.26), channel_id=1, replica_groups=mesh['y'=8,'z'=12,'core'=2,'col'=4] {'col'}, dimensions={0} | all-to-all | bytes 524288 | tf_op jit(solution)/shard_map/all_to_all | solution.py:47
  133.3 1.3 collective-permute-start.11
  135.0 5.5 %collective-permute-start.10 = (f32[4,64,32]{2,1,0:T(8,128)S(1)}, f32[4,64,32]{2,1,0:T(8,128)}, u32[]{:S(2)}, u32[]{:S(2)}) collective-permute-start(f32[4,64,32]{2,1,0:T(8,128)S(1)} %fusion.11), channel_id=1, source_target_pairs={{0,192},{4,196},{8,200},{12,204},{16,208},{20,212},{24,216},{28,22... | collective-permute-start | bytes 98312 | tf_op jit(solution)/shard_map/ppermute | solution.py:14
  140.9 6.1 %collective-permute-start.9 = (f32[4,64,32]{2,1,0:T(8,128)S(1)}, f32[4,64,32]{2,1,0:T(8,128)S(1)}, u32[]{:S(2)}, u32[]{:S(2)}) collective-permute-start(f32[4,64,32]{2,1,0:T(8,128)S(1)} %fusion.8), channel_id=1, source_target_pairs={{4,0},{8,4},{12,8},{16,12},{20,16},{24,20},{28,24},{32,28},{36,32}... | collective-permute-start | bytes 98312 | tf_op jit(solution)/shard_map/ppermute | solution.py:14
  147.4 1.9 collective-permute-start.8
  150.0 1.2 collective-permute-done.8
  151.2 1.2 concatenate.23
  153.1 15.0 %all_to_all.32 = f32[12,1,1024]{2,1,0:T(1,128)S(1)} all-to-all(f32[12,1,1024]{2,1,0:T(1,128)S(1)} %reshape.46), channel_id=1, replica_groups=mesh['y'=8,'z'=12,'core'=2,'col'=4] {'z'}, dimensions={0} | all-to-all | bytes 98304 | tf_op jit(solution)/shard_map/all_to_all | solution.py:59
  168.9 25.6 %all-gather.1 = f32[192,16,64]{2,1,0:T(8,128)S(1)} all-gather(f32[12,16,64]{2,1,0:T(8,128)S(1)} %reshape.47), channel_id=3, replica_groups=mesh['y'=8,'z'=12,'core'=2,'col'=4] {'y','core'}, dimensions={0}, use_global_device_ids=true | all-gather | bytes 835584 | tf_op jit(solution)/shard_map/all_gather | solution.py:60
  195.6 2.6 %fusion.31 = f32[64,64]{1,0:T(8,128)S(1)} fusion(f32[3072,64]{1,0:T(8,128)S(1)} %bitcast.96, f32[64,3072]{1,0:T(8,128)S(1)} %copy-done.2), kind=kOutput, calls=%fused_computation.53 | convolution fusion | flops 150994944 | bytes 1589248 | tf_op jit(solution)/shard_map/dot_general | solution.py:63
  199.0 3.3 %all-to-all-start.5 = ((f32[4,1,4096]{2,1,0:T(1,128)}), f32[4,1,4096]{2,1,0:T(1,128)S(1)}, u32[]{:S(2)}, u32[]{:S(2)}) async-start(f32[4,1,4096]{2,1,0:T(1,128)} %reshape.48), calls=%async_computation.5 | async-start | bytes 131072 | tf_op jit(solution)/shard_map/all_to_all | solution.py:47
  202.3 4.4 %all-to-all-done.5 = f32[4,1,4096]{2,1,0:T(1,128)S(1)} async-done(((f32[4,1,4096]{2,1,0:T(1,128)}), f32[4,1,4096]{2,1,0:T(1,128)S(1)}, u32[]{:S(2)}, u32[]{:S(2)}) %all-to-all-start.5) | async-done | bytes 65568 | tf_op jit(solution)/shard_map/all_to_all | solution.py:47
  207.9 1.5 fusion.2
  (87 shorter events, 22.7 us)
Async XLA Ops:
  0.6 50.0 %copy-start = (f32[1,1536,256]{2,1,0:T(8,128)S(1)}, f32[1,1536,256]{2,1,0:T(8,128)}, u32[]{:S(2)}) copy-start(f32[1,1536,256]{2,1,0:T(8,128)} %param.9) | copy-start | bytes 4718596
  3.1 30.8 %copy-start.3 = (f32[1,1536,64]{1,2,0:T(8,128)S(1)}, f32[1,1536,64]{1,2,0:T(8,128)}, u32[]{:S(2)}) copy-start(f32[1,1536,64]{1,2,0:T(8,128)} %param.10) | copy-start | bytes 1179652
  15.1 19.0 %collective-permute-start.2 = (f32[4,64,32]{2,1,0:T(8,128)}, f32[4,64,32]{2,1,0:T(8,128)S(1)}, u32[]{:S(2)}, u32[]{:S(2)}) collective-permute-start(f32[4,64,32]{2,1,0:T(8,128)} %fusion.13), channel_id=1, source_target_pairs={{0,192},{4,196},{8,200},{12,204},{16,208},{20,212},{24,216},{28,22... | collective-permute-start | bytes 98312 | tf_op jit(solution)/shard_map/ppermute | solution.py:14
  20.5 13.6 %collective-permute-start.3 = (f32[4,64,32]{2,1,0:T(8,128)}, f32[4,64,32]{2,1,0:T(8,128)S(1)}, u32[]{:S(2)}, u32[]{:S(2)}) collective-permute-start(f32[4,64,32]{2,1,0:T(8,128)} %fusion.16), channel_id=1, source_target_pairs={{192,0},{196,4},{200,8},{204,12},{208,16},{212,20},{216,24},{220,2... | collective-permute-start | bytes 98312 | tf_op jit(solution)/shard_map/ppermute | solution.py:14
  22.8 11.3 %collective-permute-start.1 = (f32[4,64,32]{2,1,0:T(8,128)}, f32[4,64,32]{2,1,0:T(8,128)}, u32[]{:S(2)}, u32[]{:S(2)}) collective-permute-start(f32[4,64,32]{2,1,0:T(8,128)} %fusion.10), channel_id=1, source_target_pairs={{4,0},{8,4},{12,8},{16,12},{20,16},{24,20},{28,24},{32,28},{36,32}... | collective-permute-start | bytes 98312 | tf_op jit(solution)/shard_map/ppermute | solution.py:14
  32.0 4.2 %collective-permute-start = (f32[4,64,32]{2,1,0:T(8,128)}, f32[4,64,32]{2,1,0:T(8,128)}, u32[]{:S(2)}, u32[]{:S(2)}) collective-permute-start(f32[4,64,32]{2,1,0:T(8,128)} %fusion.7), channel_id=1, source_target_pairs={{0,4},{4,8},{8,12},{12,16},{16,20},{20,24},{24,28},{28,32},{32,36}... | collective-permute-start | bytes 98312 | tf_op jit(solution)/shard_map/ppermute | solution.py:14
  38.6 21.8 %all-to-all-start.1 = ((f32[12,1,1024]{2,1,0:T(1,128)}), f32[12,1,1024]{2,1,0:T(1,128)S(1)}, u32[]{:S(2)}, u32[]{:S(2)}) async-start(f32[12,1,1024]{2,1,0:T(1,128)} %reshape.44), calls=%async_computation.1 | async-start | bytes 98304 | tf_op jit(solution)/shard_map/all_to_all | solution.py:59
  89.1 1.1 copy-start.1
  93.6 11.4 %all-to-all-start.2 = ((f32[4,64,320]{2,1,0:T(8,128)}), f32[4,64,320]{2,1,0:T(8,128)S(1)}, u32[]{:S(2)}, u32[]{:S(2)}) async-start(f32[4,64,320]{2,1,0:T(8,128)} %broadcast_in_dim.25), calls=%async_computation.2 | async-start | bytes 786432 | tf_op jit(solution)/shard_map/all_to_all | solution.py:47
  106.9 11.8 %collective-permute-start.7 = (f32[4,64,32]{2,1,0:T(8,128)S(1)}, f32[4,64,32]{2,1,0:T(8,128)S(1)}, u32[]{:S(2)}, u32[]{:S(2)}) collective-permute-start(f32[4,64,32]{2,1,0:T(8,128)S(1)} %fusion.15), channel_id=1, source_target_pairs={{192,0},{196,4},{200,8},{204,12},{208,16},{212,20},{216,24},{220,2... | collective-permute-start | bytes 98312 | tf_op jit(solution)/shard_map/ppermute | solution.py:14
  108.2 10.5 %collective-permute-start.6 = (f32[4,64,32]{2,1,0:T(8,128)S(1)}, f32[4,64,32]{2,1,0:T(8,128)S(1)}, u32[]{:S(2)}, u32[]{:S(2)}) collective-permute-start(f32[4,64,32]{2,1,0:T(8,128)S(1)} %fusion.12), channel_id=1, source_target_pairs={{0,192},{4,196},{8,200},{12,204},{16,208},{20,212},{24,216},{28,22... | collective-permute-start | bytes 98312 | tf_op jit(solution)/shard_map/ppermute | solution.py:14
  113.1 6.3 %collective-permute-start.5 = (f32[4,64,32]{2,1,0:T(8,128)S(1)}, f32[4,64,32]{2,1,0:T(8,128)S(1)}, u32[]{:S(2)}, u32[]{:S(2)}) collective-permute-start(f32[4,64,32]{2,1,0:T(8,128)S(1)} %fusion.9), channel_id=1, source_target_pairs={{4,0},{8,4},{12,8},{16,12},{20,16},{24,20},{28,24},{32,28},{36,32}... | collective-permute-start | bytes 98312 | tf_op jit(solution)/shard_map/ppermute | solution.py:14
  116.6 4.0 %collective-permute-start.4 = (f32[4,64,32]{2,1,0:T(8,128)S(1)}, f32[4,64,32]{2,1,0:T(8,128)}, u32[]{:S(2)}, u32[]{:S(2)}) collective-permute-start(f32[4,64,32]{2,1,0:T(8,128)S(1)} %fusion.6), channel_id=1, source_target_pairs={{0,4},{4,8},{8,12},{12,16},{16,20},{20,24},{24,28},{28,32},{32,36}... | collective-permute-start | bytes 98312 | tf_op jit(solution)/shard_map/ppermute | solution.py:14
  118.7 0.7 copy-start.5
  118.7 0.7 copy-start.6
  119.4 0.6 copy-start.8
  124.2 25.1 %copy-start.4 = (f32[64,256]{1,0:T(8,128)}, f32[64,256]{1,0:T(8,128)S(1)}, u32[]{:S(2)}) copy-start(f32[64,256]{1,0:T(8,128)S(1)} %fusion.3) | copy-start | bytes 196612
  133.3 16.0 %collective-permute-start.11 = (f32[4,64,32]{2,1,0:T(8,128)S(1)}, f32[4,64,32]{2,1,0:T(8,128)S(1)}, u32[]{:S(2)}, u32[]{:S(2)}) collective-permute-start(f32[4,64,32]{2,1,0:T(8,128)S(1)} %fusion.14), channel_id=1, source_target_pairs={{192,0},{196,4},{200,8},{204,12},{208,16},{212,20},{216,24},{220,2... | collective-permute-start | bytes 98312 | tf_op jit(solution)/shard_map/ppermute | solution.py:14
  135.0 14.3 %collective-permute-start.10 = (f32[4,64,32]{2,1,0:T(8,128)S(1)}, f32[4,64,32]{2,1,0:T(8,128)}, u32[]{:S(2)}, u32[]{:S(2)}) collective-permute-start(f32[4,64,32]{2,1,0:T(8,128)S(1)} %fusion.11), channel_id=1, source_target_pairs={{0,192},{4,196},{8,200},{12,204},{16,208},{20,212},{24,216},{28,22... | collective-permute-start | bytes 98312 | tf_op jit(solution)/shard_map/ppermute | solution.py:14
  140.9 8.4 %collective-permute-start.9 = (f32[4,64,32]{2,1,0:T(8,128)S(1)}, f32[4,64,32]{2,1,0:T(8,128)S(1)}, u32[]{:S(2)}, u32[]{:S(2)}) collective-permute-start(f32[4,64,32]{2,1,0:T(8,128)S(1)} %fusion.8), channel_id=1, source_target_pairs={{4,0},{8,4},{12,8},{16,12},{20,16},{24,20},{28,24},{32,28},{36,32}... | collective-permute-start | bytes 98312 | tf_op jit(solution)/shard_map/ppermute | solution.py:14
  147.4 3.9 %collective-permute-start.8 = (f32[4,64,32]{2,1,0:T(8,128)S(1)}, f32[4,64,32]{2,1,0:T(8,128)S(1)}, u32[]{:S(2)}, u32[]{:S(2)}) collective-permute-start(f32[4,64,32]{2,1,0:T(8,128)S(1)} %fusion.5), channel_id=1, source_target_pairs={{0,4},{4,8},{8,12},{12,16},{16,20},{20,24},{24,28},{28,32},{32,36}... | collective-permute-start | bytes 98312 | tf_op jit(solution)/shard_map/ppermute | solution.py:14
  149.4 0.7 copy-start.7
  194.5 1.1 copy-start.2
  199.0 7.7 %all-to-all-start.5 = ((f32[4,1,4096]{2,1,0:T(1,128)}), f32[4,1,4096]{2,1,0:T(1,128)S(1)}, u32[]{:S(2)}, u32[]{:S(2)}) async-start(f32[4,1,4096]{2,1,0:T(1,128)} %reshape.48), calls=%async_computation.5 | async-start | bytes 131072 | tf_op jit(solution)/shard_map/all_to_all | solution.py:47

commit v9 on v8

--- a/solution.py
+++ b/solution.py
@@ -62,18 +62,12 @@
         kept_rows = g.reshape(subs * quarter, rhs_width)
         return jnp.dot(coarse_inverse, kept_rows, precision=HIGH)
 
-    index_row = jnp.concatenate(
-        [
-            send_rows.reshape(-1).astype(jnp.float32),
-            counts.astype(jnp.float32),
-            jnp.zeros((own_width - n_nb * halo_slots - n_nb,), jnp.float32),
-        ]
-    )[None]
-    g0 = col_gather(jnp.concatenate([right_sides, index_row], axis=0)[None])
-    own_b_all = g0[:, :rhs_width]
-    idx = g0[:, rhs_width]
-    send_all = idx[:, : n_nb * halo_slots].astype(jnp.int32).reshape(n_col, n_nb, halo_slots)
-    counts_all = idx[:, n_nb * halo_slots : n_nb * halo_slots + n_nb].astype(jnp.int32)
+    index_all = lax.all_gather(
+        jnp.concatenate([send_rows.reshape(-1), counts])[None], "col", axis=0, tiled=True
+    )
+    own_b_all = col_gather(right_sides[None])
+    send_all = index_all[:, : n_nb * halo_slots].reshape(n_col, n_nb, halo_slots)
+    counts_all = index_all[:, n_nb * halo_slots : n_nb * halo_slots + n_nb]
     live_all = (slots[None, None, :] < counts_all[:, :, None]).astype(jnp.float32)
     select_all = (rows[None, :, None, None] == send_all[:, None]).astype(jnp.float32) * live_all[
         :, None

time: 210 us -> 216 us (1.029)
  blocking collectives: 87.2 us -> 79.5 us
  starting transfers between devices: 61.2 us -> 68.7 us
  local copies, waits for them, and re-layouts: 11 us -> 15.2 us
  waiting for transfers between devices: 25.6 us -> 27.9 us
    all_to_all x2 -> x1, blocking collectives: 19.2 us -> 8.73 us  [col_gather(): return lax.all_to_all(spread, 'col', 0, 0, tiled=True)]
    unnamed x0 -> x1, blocking collectives: none -> 7.08 us
    all_to_all x2 -> x3, starting transfers between devices: 6.74 us -> 11.7 us  [col_gather(): return lax.all_to_all(spread, 'col', 0, 0, tiled=True)]
    all_gather x2, blocking collectives: 53 us -> 48.9 us  [coarse_partial(): g = lax.all_gather(g[None], ('y', 'core'), axis=0, tiled=True)]
    ppermute x12, waiting for transfers between devices: 4.49 us -> 6.75 us  [passed_along(): return lax.ppermute(block, SUB, route)]
    unnamed x25 -> x28, local copies, waits for them, and re-layouts: 5.09 us -> 6.98 us
    all_to_all x2 -> x3, waiting for transfers between devices: 12.4 us -> 12.4 us  [col_gather(): return lax.all_to_all(spread, 'col', 0, 0, tiled=True)]
  transfers between devices with their start and end apart: 15 -> 16, of which waited for: 7 -> 8; matrix products, arithmetic and copies ran while one was open for 2% -> 4% of each run, Pallas kernels for 0% -> 0%
where the time goes in v9:
time: 216 us; the launch traced here: 215 us
  blocking collectives  79.5 us (37%)
  starting transfers between devices  68.7 us (32%)
  waiting for transfers between devices  27.9 us (13%)
  matrix products  18.4 us (9%)
  local copies, waits for them, and re-layouts  15.2 us (7%)
  other arithmetic  3.34 us (2%)
    all_gather x2, blocking collectives, coarse_partial(): g = lax.all_gather(g[None], ('y', 'core'), axis=0, tiled=True)  48.9 us
    ppermute x12, starting transfers between devices, passed_along(): return lax.ppermute(block, SUB, route)  44.3 us
    all_to_all x1, blocking collectives, coarse_partial(): g = lax.all_to_all(spread, 'z', 0, 0, tiled=True)  14.8 us
    all_to_all x1, starting transfers between devices, coarse_partial(): g = lax.all_to_all(spread, 'z', 0, 0, tiled=True)  12.7 us
    all_to_all x3, waiting for transfers between devices, col_gather(): return lax.all_to_all(spread, 'col', 0, 0, tiled=True)  12.4 us
    all_to_all x3, starting transfers between devices, col_gather(): return lax.all_to_all(spread, 'col', 0, 0, tiled=True)  11.7 us
    all_to_all x1, waiting for transfers between devices, coarse_partial(): g = lax.all_to_all(spread, 'z', 0, 0, tiled=True)  8.77 us
    all_to_all x1, blocking collectives, col_gather(): return lax.all_to_all(spread, 'col', 0, 0, tiled=True)  8.73 us
  transfers between devices with their start and end apart: 16, of which 8 were waited for; matrix products, arithmetic and copies ran while one was open for 4% of the time, Pallas kernels for 0%

profile of v9, /device:TPU:1, one launch (start us, length us, event | category | flops | bytes accessed | tf_op | source)
XLA Modules:
  0.0 214.9 jit_solution(7875849399628825462)
XLA Ops:
  0.6 1.7 broadcast_in_dim.18
  2.3 5.0 %all-to-all-start = ((f32[4,64,256]{2,1,0:T(8,128)}), f32[4,64,256]{2,1,0:T(8,128)S(1)}, u32[]{:S(2)}, u32[]{:S(2)}) async-start(f32[4,64,256]{2,1,0:T(8,128)} %broadcast_in_dim.18), calls=%async_computation | async-start | bytes 524288 | tf_op jit(solution)/shard_map/all_to_all | solution.py:47
  10.8 7.1 %all-reduce = s32[528]{0:T(1024)S(1)} all-reduce(s32[528]{0:T(1024)S(1)} %add_dynamic-update-slice_fusion), channel_id=2, replica_groups=mesh['y'=8,'z'=12,'core'=2,'col'=4] {'col'}, use_global_device_ids=true, to_apply=%add | all-reduce | flops 528 | bytes 4224
  19.4 13.2 %collective-permute-start.1 = (f32[4,64,32]{2,1,0:T(8,128)}, f32[4,64,32]{2,1,0:T(8,128)S(1)}, u32[]{:S(2)}, u32[]{:S(2)}) collective-permute-start(f32[4,64,32]{2,1,0:T(8,128)} %convolution_bitcast_fusion.3), channel_id=1, source_target_pairs={{4,0},{8,4},{12,8},{16,12},{20,16},{24,20},{28,24},{32,28},{36,32}... | collective-permute-start | bytes 98312 | tf_op jit(solution)/shard_map/ppermute | solution.py:14
  33.7 1.3 collective-permute-start.2
  36.0 1.3 collective-permute-start.3
  38.3 1.9 collective-permute-start
  40.4 2.4 %collective-permute-done.3 = f32[4,64,32]{2,1,0:T(8,128)S(1)} collective-permute-done((f32[4,64,32]{2,1,0:T(8,128)}, f32[4,64,32]{2,1,0:T(8,128)S(1)}, u32[]{:S(2)}, u32[]{:S(2)}) %collective-permute-start.3) | collective-permute-done | bytes 32800 | tf_op jit(solution)/shard_map/ppermute | solution.py:14
  42.8 2.5 %collective-permute-done = f32[4,64,32]{2,1,0:T(8,128)} collective-permute-done((f32[4,64,32]{2,1,0:T(8,128)}, f32[4,64,32]{2,1,0:T(8,128)}, u32[]{:S(2)}, u32[]{:S(2)}) %collective-permute-start) | collective-permute-done | bytes 32800 | tf_op jit(solution)/shard_map/ppermute | solution.py:14
  47.6 12.7 %all-to-all-start.1 = ((f32[12,1,1024]{2,1,0:T(1,128)}), f32[12,1,1024]{2,1,0:T(1,128)S(1)}, u32[]{:S(2)}, u32[]{:S(2)}) async-start(f32[12,1,1024]{2,1,0:T(1,128)} %reshape.48), calls=%async_computation.1 | async-start | bytes 98304 | tf_op jit(solution)/shard_map/all_to_all | solution.py:59
  61.3 8.8 %all-to-all-done.1 = f32[12,1,1024]{2,1,0:T(1,128)S(1)} async-done(((f32[12,1,1024]{2,1,0:T(1,128)}), f32[12,1,1024]{2,1,0:T(1,128)S(1)}, u32[]{:S(2)}, u32[]{:S(2)}) %all-to-all-start.1) | async-done | bytes 49184 | tf_op jit(solution)/shard_map/all_to_all | solution.py:59
  71.4 22.6 %all-gather.1 = f32[192,16,64]{2,1,0:T(8,128)S(1)} all-gather(f32[12,16,64]{2,1,0:T(8,128)S(1)} %reshape.49), channel_id=3, replica_groups=mesh['y'=8,'z'=12,'core'=2,'col'=4] {'y','core'}, dimensions={0}, use_global_device_ids=true | all-gather | bytes 835584 | tf_op jit(solution)/shard_map/all_gather | solution.py:60
  95.1 2.6 %fusion.22 = f32[64,64]{1,0:T(8,128)S(1)} fusion(f32[3072,64]{1,0:T(8,128)S(1)} %bitcast.102, f32[64,3072]{1,0:T(8,128)S(1)} %copy-done.1), kind=kOutput, calls=%fused_computation.43 | convolution fusion | flops 150994944 | bytes 1589248 | tf_op jit(solution)/shard_map/dot_general | solution.py:63
  98.6 3.5 %all-to-all-start.2 = ((f32[4,64,320]{2,1,0:T(8,128)}), f32[4,64,320]{2,1,0:T(8,128)S(1)}, u32[]{:S(2)}, u32[]{:S(2)}) async-start(f32[4,64,320]{2,1,0:T(8,128)} %broadcast_in_dim.22), calls=%async_computation.2 | async-start | bytes 786432 | tf_op jit(solution)/shard_map/all_to_all | solution.py:47
  102.1 7.9 %all-to-all-done.2 = f32[4,64,320]{2,1,0:T(8,128)S(1)} async-done(((f32[4,64,320]{2,1,0:T(8,128)}), f32[4,64,320]{2,1,0:T(8,128)S(1)}, u32[]{:S(2)}, u32[]{:S(2)}) %all-to-all-start.2) | async-done | bytes 327712 | tf_op jit(solution)/shard_map/all_to_all | solution.py:47
  111.8 1.3 collective-permute-start.7
  113.1 4.9 %collective-permute-start.6 = (f32[4,64,32]{2,1,0:T(8,128)S(1)}, f32[4,64,32]{2,1,0:T(8,128)S(1)}, u32[]{:S(2)}, u32[]{:S(2)}) collective-permute-start(f32[4,64,32]{2,1,0:T(8,128)S(1)} %fusion.10), channel_id=1, source_target_pairs={{0,192},{4,196},{8,200},{12,204},{16,208},{20,212},{24,216},{28,22... | collective-permute-start | bytes 98312 | tf_op jit(solution)/shard_map/ppermute | solution.py:14
  118.0 3.5 %collective-permute-start.5 = (f32[4,64,32]{2,1,0:T(8,128)S(1)}, f32[4,64,32]{2,1,0:T(8,128)S(1)}, u32[]{:S(2)}, u32[]{:S(2)}) collective-permute-start(f32[4,64,32]{2,1,0:T(8,128)S(1)} %fusion.8), channel_id=1, source_target_pairs={{4,0},{8,4},{12,8},{16,12},{20,16},{24,20},{28,24},{32,28},{36,32}... | collective-permute-start | bytes 98312 | tf_op jit(solution)/shard_map/ppermute | solution.py:14
  121.5 2.1 collective-permute-start.4
  125.5 1.3 concatenate.18
  126.8 2.3 %fusion.3 = f32[64,256]{1,0:T(8,128)S(1)} fusion(f32[64,256]{1,0:T(8,128)} %param.7, f32[4,64,384]{2,1,0:T(8,128)S(1)} %concatenate.18, f32[4,384,256]{2,1,0:T(8,128)} %bitcast.105), kind=kOutput, calls=%fused_computation.10 | convolution fusion | flops 302006272 | bytes 2097152 | tf_op jit(solution)/shard_map/dot_general | solution.py:53
  129.2 8.7 %all_to_all.30 = f32[4,64,256]{2,1,0:T(8,128)S(1)} all-to-all(f32[4,64,256]{2,1,0:T(8,128)S(1)} %broadcast_in_dim.23), channel_id=1, replica_groups=mesh['y'=8,'z'=12,'core'=2,'col'=4] {'col'}, dimensions={0} | all-to-all | bytes 524288 | tf_op jit(solution)/shard_map/all_to_all | solution.py:47
  138.3 1.3 collective-permute-start.11
  139.9 4.9 %collective-permute-start.10 = (f32[4,64,32]{2,1,0:T(8,128)S(1)}, f32[4,64,32]{2,1,0:T(8,128)S(1)}, u32[]{:S(2)}, u32[]{:S(2)}) collective-permute-start(f32[4,64,32]{2,1,0:T(8,128)S(1)} %fusion.9), channel_id=1, source_target_pairs={{0,192},{4,196},{8,200},{12,204},{16,208},{20,212},{24,216},{28,22... | collective-permute-start | bytes 98312 | tf_op jit(solution)/shard_map/ppermute | solution.py:14
  145.2 6.8 %collective-permute-start.9 = (f32[4,64,32]{2,1,0:T(8,128)S(1)}, f32[4,64,32]{2,1,0:T(8,128)S(1)}, u32[]{:S(2)}, u32[]{:S(2)}) collective-permute-start(f32[4,64,32]{2,1,0:T(8,128)S(1)} %fusion.7), channel_id=1, source_target_pairs={{4,0},{8,4},{12,8},{16,12},{20,16},{24,20},{28,24},{32,28},{36,32}... | collective-permute-start | bytes 98312 | tf_op jit(solution)/shard_map/ppermute | solution.py:14
  152.3 1.9 collective-permute-start.8
  158.0 14.8 %all_to_all.31 = f32[12,1,1024]{2,1,0:T(1,128)S(1)} all-to-all(f32[12,1,1024]{2,1,0:T(1,128)S(1)} %reshape.50), channel_id=1, replica_groups=mesh['y'=8,'z'=12,'core'=2,'col'=4] {'z'}, dimensions={0} | all-to-all | bytes 98304 | tf_op jit(solution)/shard_map/all_to_all | solution.py:59
  173.6 26.3 %all-gather.2 = f32[192,16,64]{2,1,0:T(8,128)S(1)} all-gather(f32[12,16,64]{2,1,0:T(8,128)S(1)} %reshape.51), channel_id=4, replica_groups=mesh['y'=8,'z'=12,'core'=2,'col'=4] {'y','core'}, dimensions={0}, use_global_device_ids=true | all-gather | bytes 835584 | tf_op jit(solution)/shard_map/all_gather | solution.py:60
  201.0 2.6 %fusion.23 = f32[64,64]{1,0:T(8,128)S(1)} fusion(f32[3072,64]{1,0:T(8,128)S(1)} %bitcast.104, f32[64,3072]{1,0:T(8,128)S(1)} %copy-done.2), kind=kOutput, calls=%fused_computation.44 | convolution fusion | flops 150994944 | bytes 1589248 | tf_op jit(solution)/shard_map/dot_general | solution.py:63
  204.4 3.3 %all-to-all-start.5 = ((f32[4,1,4096]{2,1,0:T(1,128)}), f32[4,1,4096]{2,1,0:T(1,128)S(1)}, u32[]{:S(2)}, u32[]{:S(2)}) async-start(f32[4,1,4096]{2,1,0:T(1,128)} %reshape.52), calls=%async_computation.5 | async-start | bytes 131072 | tf_op jit(solution)/shard_map/all_to_all | solution.py:47
  207.8 4.4 %all-to-all-done.5 = f32[4,1,4096]{2,1,0:T(1,128)S(1)} async-done(((f32[4,1,4096]{2,1,0:T(1,128)}), f32[4,1,4096]{2,1,0:T(1,128)S(1)}, u32[]{:S(2)}, u32[]{:S(2)}) %all-to-all-start.5) | async-done | bytes 65568 | tf_op jit(solution)/shard_map/all_to_all | solution.py:47
  213.3 1.5 fusion.2
  (87 shorter events, 26.7 us)
Async XLA Ops:
  0.6 59.7 %copy-start = (f32[1,1536,256]{2,1,0:T(8,128)S(1)}, f32[1,1536,256]{2,1,0:T(8,128)}, u32[]{:S(2)}) copy-start(f32[1,1536,256]{2,1,0:T(8,128)} %param.9) | copy-start | bytes 4718596
  2.3 37.9 %copy-start.3 = (f32[1,1536,64]{1,2,0:T(8,128)S(1)}, f32[1,1536,64]{1,2,0:T(8,128)}, u32[]{:S(2)}) copy-start(f32[1,1536,64]{1,2,0:T(8,128)} %param.10) | copy-start | bytes 1179652
  2.3 16.1 %all-to-all-start = ((f32[4,64,256]{2,1,0:T(8,128)}), f32[4,64,256]{2,1,0:T(8,128)S(1)}, u32[]{:S(2)}, u32[]{:S(2)}) async-start(f32[4,64,256]{2,1,0:T(8,128)} %broadcast_in_dim.18), calls=%async_computation | async-start | bytes 524288 | tf_op jit(solution)/shard_map/all_to_all | solution.py:47
  19.4 20.9 %collective-permute-start.1 = (f32[4,64,32]{2,1,0:T(8,128)}, f32[4,64,32]{2,1,0:T(8,128)S(1)}, u32[]{:S(2)}, u32[]{:S(2)}) collective-permute-start(f32[4,64,32]{2,1,0:T(8,128)} %convolution_bitcast_fusion.3), channel_id=1, source_target_pairs={{4,0},{8,4},{12,8},{16,12},{20,16},{24,20},{28,24},{32,28},{36,32}... | collective-permute-start | bytes 98312 | tf_op jit(solution)/shard_map/ppermute | solution.py:14
  33.7 6.7 %collective-permute-start.2 = (f32[4,64,32]{2,1,0:T(8,128)}, f32[4,64,32]{2,1,0:T(8,128)S(1)}, u32[]{:S(2)}, u32[]{:S(2)}) collective-permute-start(f32[4,64,32]{2,1,0:T(8,128)} %convolution_bitcast_fusion.2), channel_id=1, source_target_pairs={{0,192},{4,196},{8,200},{12,204},{16,208},{20,212},{24,216},{28,22... | collective-permute-start | bytes 98312 | tf_op jit(solution)/shard_map/ppermute | solution.py:14
  36.0 6.8 %collective-permute-start.3 = (f32[4,64,32]{2,1,0:T(8,128)}, f32[4,64,32]{2,1,0:T(8,128)S(1)}, u32[]{:S(2)}, u32[]{:S(2)}) collective-permute-start(f32[4,64,32]{2,1,0:T(8,128)} %convolution_bitcast_fusion.1), channel_id=1, source_target_pairs={{192,0},{196,4},{200,8},{204,12},{208,16},{212,20},{216,24},{220,2... | collective-permute-start | bytes 98312 | tf_op jit(solution)/shard_map/ppermute | solution.py:14
  38.3 7.0 %collective-permute-start = (f32[4,64,32]{2,1,0:T(8,128)}, f32[4,64,32]{2,1,0:T(8,128)}, u32[]{:S(2)}, u32[]{:S(2)}) collective-permute-start(f32[4,64,32]{2,1,0:T(8,128)} %convolution_bitcast_fusion.4), channel_id=1, source_target_pairs={{0,4},{4,8},{8,12},{12,16},{16,20},{20,24},{24,28},{28,32},{32,36}... | collective-permute-start | bytes 98312 | tf_op jit(solution)/shard_map/ppermute | solution.py:14
  47.6 22.4 %all-to-all-start.1 = ((f32[12,1,1024]{2,1,0:T(1,128)}), f32[12,1,1024]{2,1,0:T(1,128)S(1)}, u32[]{:S(2)}, u32[]{:S(2)}) async-start(f32[12,1,1024]{2,1,0:T(1,128)} %reshape.48), calls=%async_computation.1 | async-start | bytes 98304 | tf_op jit(solution)/shard_map/all_to_all | solution.py:59
  94.0 1.1 copy-start.1
  98.6 11.4 %all-to-all-start.2 = ((f32[4,64,320]{2,1,0:T(8,128)}), f32[4,64,320]{2,1,0:T(8,128)S(1)}, u32[]{:S(2)}, u32[]{:S(2)}) async-start(f32[4,64,320]{2,1,0:T(8,128)} %broadcast_in_dim.22), calls=%async_computation.2 | async-start | bytes 786432 | tf_op jit(solution)/shard_map/all_to_all | solution.py:47
  111.8 11.8 %collective-permute-start.7 = (f32[4,64,32]{2,1,0:T(8,128)S(1)}, f32[4,64,32]{2,1,0:T(8,128)S(1)}, u32[]{:S(2)}, u32[]{:S(2)}) collective-permute-start(f32[4,64,32]{2,1,0:T(8,128)S(1)} %fusion.12), channel_id=1, source_target_pairs={{192,0},{196,4},{200,8},{204,12},{208,16},{212,20},{216,24},{220,2... | collective-permute-start | bytes 98312 | tf_op jit(solution)/shard_map/ppermute | solution.py:14
  113.1 10.5 %collective-permute-start.6 = (f32[4,64,32]{2,1,0:T(8,128)S(1)}, f32[4,64,32]{2,1,0:T(8,128)S(1)}, u32[]{:S(2)}, u32[]{:S(2)}) collective-permute-start(f32[4,64,32]{2,1,0:T(8,128)S(1)} %fusion.10), channel_id=1, source_target_pairs={{0,192},{4,196},{8,200},{12,204},{16,208},{20,212},{24,216},{28,22... | collective-permute-start | bytes 98312 | tf_op jit(solution)/shard_map/ppermute | solution.py:14
  118.0 6.3 %collective-permute-start.5 = (f32[4,64,32]{2,1,0:T(8,128)S(1)}, f32[4,64,32]{2,1,0:T(8,128)S(1)}, u32[]{:S(2)}, u32[]{:S(2)}) collective-permute-start(f32[4,64,32]{2,1,0:T(8,128)S(1)} %fusion.8), channel_id=1, source_target_pairs={{4,0},{8,4},{12,8},{16,12},{20,16},{24,20},{28,24},{32,28},{36,32}... | collective-permute-start | bytes 98312 | tf_op jit(solution)/shard_map/ppermute | solution.py:14
  121.5 4.0 %collective-permute-start.4 = (f32[4,64,32]{2,1,0:T(8,128)S(1)}, f32[4,64,32]{2,1,0:T(8,128)}, u32[]{:S(2)}, u32[]{:S(2)}) collective-permute-start(f32[4,64,32]{2,1,0:T(8,128)S(1)} %fusion.6), channel_id=1, source_target_pairs={{0,4},{4,8},{8,12},{12,16},{16,20},{20,24},{24,28},{28,32},{32,36}... | collective-permute-start | bytes 98312 | tf_op jit(solution)/shard_map/ppermute | solution.py:14
  123.6 0.7 copy-start.6
  123.6 0.7 copy-start.7
  124.3 0.6 copy-start.9
  129.1 25.1 %copy-start.4 = (f32[64,256]{1,0:T(8,128)}, f32[64,256]{1,0:T(8,128)S(1)}, u32[]{:S(2)}) copy-start(f32[64,256]{1,0:T(8,128)S(1)} %fusion.3) | copy-start | bytes 196612
  138.3 16.0 %collective-permute-start.11 = (f32[4,64,32]{2,1,0:T(8,128)S(1)}, f32[4,64,32]{2,1,0:T(8,128)S(1)}, u32[]{:S(2)}, u32[]{:S(2)}) collective-permute-start(f32[4,64,32]{2,1,0:T(8,128)S(1)} %fusion.11), channel_id=1, source_target_pairs={{192,0},{196,4},{200,8},{204,12},{208,16},{212,20},{216,24},{220,2... | collective-permute-start | bytes 98312 | tf_op jit(solution)/shard_map/ppermute | solution.py:14
  139.9 14.3 %collective-permute-start.10 = (f32[4,64,32]{2,1,0:T(8,128)S(1)}, f32[4,64,32]{2,1,0:T(8,128)S(1)}, u32[]{:S(2)}, u32[]{:S(2)}) collective-permute-start(f32[4,64,32]{2,1,0:T(8,128)S(1)} %fusion.9), channel_id=1, source_target_pairs={{0,192},{4,196},{8,200},{12,204},{16,208},{20,212},{24,216},{28,22... | collective-permute-start | bytes 98312 | tf_op jit(solution)/shard_map/ppermute | solution.py:14
  145.2 9.1 %collective-permute-start.9 = (f32[4,64,32]{2,1,0:T(8,128)S(1)}, f32[4,64,32]{2,1,0:T(8,128)S(1)}, u32[]{:S(2)}, u32[]{:S(2)}) collective-permute-start(f32[4,64,32]{2,1,0:T(8,128)S(1)} %fusion.7), channel_id=1, source_target_pairs={{4,0},{8,4},{12,8},{16,12},{20,16},{24,20},{28,24},{32,28},{36,32}... | collective-permute-start | bytes 98312 | tf_op jit(solution)/shard_map/ppermute | solution.py:14
  152.3 3.9 %collective-permute-start.8 = (f32[4,64,32]{2,1,0:T(8,128)S(1)}, f32[4,64,32]{2,1,0:T(8,128)S(1)}, u32[]{:S(2)}, u32[]{:S(2)}) collective-permute-start(f32[4,64,32]{2,1,0:T(8,128)S(1)} %fusion.5), channel_id=1, source_target_pairs={{0,4},{4,8},{8,12},{12,16},{16,20},{20,24},{24,28},{28,32},{32,36}... | collective-permute-start | bytes 98312 | tf_op jit(solution)/shard_map/ppermute | solution.py:14
  154.2 0.6 copy-start.5
  154.9 0.6 copy-start.8
  199.9 1.1 copy-start.2
  204.4 7.7 %all-to-all-start.5 = ((f32[4,1,4096]{2,1,0:T(1,128)}), f32[4,1,4096]{2,1,0:T(1,128)S(1)}, u32[]{:S(2)}, u32[]{:S(2)}) async-start(f32[4,1,4096]{2,1,0:T(1,128)} %reshape.52), calls=%async_computation.5 | async-start | bytes 131072 | tf_op jit(solution)/shard_map/all_to_all | solution.py:47
